TPU v7x, 512 devices: a whole 4x8x8 slice. The times are simulated.
512 devices in a mesh: chan: 128 (over z, y, core), win: 4 (over x).
Axes of the slice: x: 4, y: 8, z: 8, core: 2. Of those that a mesh axis runs over, the one named last changes fastest.
Arguments:
- traces: bfloat16 [4, 8192, 2048], P('win', 'chan'), may hold values from -6 to 6
- round_masks: int32 [2], replicated, may hold values from 1 to 127, as said below
- row_owner: int32 [49152, 1], P('chan'), may hold values from 0 to 127; in each aligned block of 384 rows (0 to 383, 384 to 767, ...) at most 6 rows name the same one
- row_slot: int32 [49152], P('chan'), may hold values from 0 to 3
Outputs:
- binned: float32 [512, 1024], P('chan', 'win')
Inputs may be any that keep to these rules, and one draw needn't show every extreme that they name: `round_masks`: all different; group g is matched in round r with group g XOR round_masks[r]. One of the rounds has the mask 128 - 1. `row_owner`: among the 384 pairs of one channel group no owner is named more than 6 times, a bound that some block reaches.
All inputs are finite; a program needn't handle non-finite values.
Results may differ from a plain program's by a relative error of at most 0.0039.
Values may be sent and summed in bfloat16 or wider, within the bound.
No kernel may reach another device: no remote copies, remote signals or barrier semaphores. Data moves between devices by JAX's collectives and lax.ppermute only.
A program may use at most 64 MiB of HBM per device.

v0:
```python
import jax
import jax.numpy as jnp
from jax import lax
from jax.sharding import PartitionSpec as P

LAG = 512
SRC = 2
ROUNDS = 2
BINCAP = 4


block_width = 128


def partner(x, axis, bit):
    return lax.ppermute(x, axis, [(i, i ^ 1 << bit) for i in range(lax.axis_size(axis))])


def normalize(traces):
    data = traces.astype(jnp.float32)
    scale = lax.rsqrt(jnp.mean(data * data, axis=-1, keepdims=True) + 1e-06)
    return (data * scale).astype(jnp.bfloat16)


def source_toeplitz(source):
    blocks = source.reshape(-1, block_width)
    padded = jnp.concatenate(
        [blocks, jnp.zeros((blocks.shape[0], block_width + 1), blocks.dtype)], axis=1
    )
    tiled = jnp.tile(padded, (1, block_width))
    return tiled[:, : 2 * block_width * block_width].reshape(
        blocks.shape[0], block_width, 2 * block_width
    )


def correlate(receivers, toeplitz_list):
    wins, chans, samples = receivers.shape
    quota = samples // block_width
    lag_blocks = 2 * LAG // block_width
    extended = jnp.pad(receivers, ((0, 0), (0, 0), (LAG, LAG + block_width)))
    cells = extended.reshape(wins, chans, -1, block_width)
    doubled = jnp.concatenate([cells[:, :, :-1], cells[:, :, 1:]], axis=-1)
    results = []
    for toeplitz in toeplitz_list:
        parts = [
            jnp.einsum(
                "acqw,aqrw->cr",
                doubled[:, :, p : p + quota],
                toeplitz,
                preferred_element_type=jnp.float32,
            )
            for p in range(lag_blocks)
        ]
        results.append(jnp.concatenate(parts, axis=-1))
    return jnp.stack(results)


def body(traces, round_masks, row_owner, row_slot):
    wins, chans, samples = traces.shape
    normed = normalize(traces)
    stride = chans // SRC
    sources = normed[:, ::stride, :]
    toeplitz_list = [jax.vmap(source_toeplitz)(sources[:, k, :]) for k in range(SRC)]
    blocks = [correlate(normed, toeplitz_list)]
    bits = lax.axis_size("chan").bit_length() - 1
    for step in range(ROUNDS):
        mask = round_masks[step]
        moved = normed
        for bit in range(bits):
            swapped = partner(moved, "chan", bit)
            moved = jnp.where(jnp.bitwise_and(jnp.right_shift(mask, bit), 1) == 1, swapped, moved)
        blocks.append(correlate(moved, toeplitz_list))
    rows = jnp.stack(blocks).reshape(-1, 2 * LAG) / jnp.sqrt(jnp.float32(samples))
    owner = row_owner[:, 0]
    owners_total = lax.axis_size("chan")
    rows = lax.psum_scatter(rows, "win", scatter_dimension=1, tiled=True)
    rows_total = rows.shape[0]
    capacity = max(2, 2 * rows_total // owners_total)
    marks = (owner[:, None] == jnp.arange(owners_total, dtype=jnp.int32)[None, :]).astype(jnp.int32)
    rank = jnp.sum((jnp.cumsum(marks, axis=0) - marks) * marks, axis=1)
    place = owner * capacity + rank
    outgoing = jnp.zeros((owners_total * capacity, rows.shape[1]), jnp.float32).at[place].set(rows)
    labels = (
        jnp.full((owners_total * capacity,), -1.0, jnp.float32)
        .at[place]
        .set(row_slot.astype(jnp.float32))
    )
    arrived, arrived_labels = (
        lax.all_to_all(outgoing, "chan", split_axis=0, concat_axis=0, tiled=True),
        lax.all_to_all(labels, "chan", split_axis=0, concat_axis=0, tiled=True),
    )
    picks = (arrived_labels[None, :] == jnp.arange(BINCAP, dtype=jnp.float32)[:, None]).astype(
        jnp.float32
    )
    sums = jnp.dot(
        picks, arrived, precision=lax.Precision.HIGHEST, preferred_element_type=jnp.float32
    )
    counts = jnp.sum(picks, axis=1)
    return sums / jnp.sqrt(jnp.maximum(counts, 1.0))[:, None]


def solution(mesh):
    return jax.shard_map(
        body,
        mesh=mesh,
        in_specs=(P("win", "chan", None), P(), P("chan", None), P("chan")),
        out_specs=P("chan", "win"),
        check_vma=False,
    )
```

profile of v0, /device:TPU:1, one launch (start us, length us, event | category | flops | bytes accessed | tf_op | source)
XLA Modules:
  0.0 280.7 jit_solution(5233637802494801844)
XLA Ops:
  6.5 1.1 fusion.48
  7.7 1.1 fusion.49
  8.7 8.7 %collective-permute-start = (bf16[1,64,2048]{2,1,0:T(8,128)(2,1)S(1)}, bf16[1,64,2048]{2,1,0:T(8,128)(2,1)}, u32[]{:S(2)}, u32[]{:S(2)}) collective-permute-start(bf16[1,64,2048]{2,1,0:T(8,128)(2,1)S(1)} %fusion.49), channel_id=1, source_target_pairs={{0,4},{4,0},{8,12},{12,8},{16,20},{20,16},{24,28},{28,24},{32,36},... | collective-permute-start | bytes 786440 | tf_op jit(solution)/shard_map/ppermute | solution.py:16
  17.5 1.4 fusion.64
  28.5 1.8 tile.24
  30.7 1.3 tile.26
  32.0 3.1 %tile.27 = bf16[1,16,32896]{2,1,0:T(8,128)(2,1)S(1)} reshape(bf16[16,128,257]{2,1,0:T(8,128)(2,1)} %tile.26) | data formatting | bytes 2105344 | tf_op jit(solution)/shard_map/vmap()/tile | solution.py:30
  37.0 0.5 fusion.45
  37.9 0.5 fusion.43
  38.4 0.5 fusion.42
  39.4 0.5 fusion.40
  43.2 1.1 broadcast_select_fusion.7
  44.4 1.9 collective-permute-start.1
  46.8 3.4 %collective-permute-start.7 = (bf16[1,64,2048]{2,1,0:T(8,128)(2,1)S(1)}, bf16[1,64,2048]{2,1,0:T(8,128)(2,1)S(1)}, u32[]{:S(2)}, u32[]{:S(2)}) collective-permute-start(bf16[1,64,2048]{2,1,0:T(8,128)(2,1)S(1)} %get-tuple-element.12), channel_id=1, source_target_pairs={{0,8},{4,12},{8,0},{12,4},{16,24},{20,28},{24,16},{28,20},{32,40},... | collective-permute-start | bytes 786440 | tf_op jit(solution)/shard_map/ppermute | solution.py:16
  50.2 4.0 %collective-permute-done.1 = bf16[1,64,2048]{2,1,0:T(8,128)(2,1)S(1)} collective-permute-done((bf16[1,64,2048]{2,1,0:T(8,128)(2,1)S(1)}, bf16[1,64,2048]{2,1,0:T(8,128)(2,1)S(1)}, u32[]{:S(2)}, u32[]{:S(2)}) %collective-permute-start.1) | collective-permute-done | bytes 262176 | tf_op jit(solution)/shard_map/ppermute | solution.py:16
  54.2 1.9 collective-permute-start.2
  56.1 3.7 %collective-permute-done.7 = bf16[1,64,2048]{2,1,0:T(8,128)(2,1)S(1)} collective-permute-done((bf16[1,64,2048]{2,1,0:T(8,128)(2,1)S(1)}, bf16[1,64,2048]{2,1,0:T(8,128)(2,1)S(1)}, u32[]{:S(2)}, u32[]{:S(2)}) %collective-permute-start.7) | collective-permute-done | bytes 262176 | tf_op jit(solution)/shard_map/ppermute | solution.py:16
  59.8 1.9 collective-permute-start.8
  61.7 14.7 %collective-permute-done.2 = bf16[1,64,2048]{2,1,0:T(8,128)(2,1)S(1)} collective-permute-done((bf16[1,64,2048]{2,1,0:T(8,128)(2,1)S(1)}, bf16[1,64,2048]{2,1,0:T(8,128)(2,1)S(1)}, u32[]{:S(2)}, u32[]{:S(2)}) %collective-permute-start.2) | collective-permute-done | bytes 262176 | tf_op jit(solution)/shard_map/ppermute | solution.py:16
  76.5 1.9 collective-permute-start.3
  78.4 26.3 %collective-permute-done.8 = bf16[1,64,2048]{2,1,0:T(8,128)(2,1)S(1)} collective-permute-done((bf16[1,64,2048]{2,1,0:T(8,128)(2,1)S(1)}, bf16[1,64,2048]{2,1,0:T(8,128)(2,1)S(1)}, u32[]{:S(2)}, u32[]{:S(2)}) %collective-permute-start.8) | collective-permute-done | bytes 262176 | tf_op jit(solution)/shard_map/ppermute | solution.py:16
  104.8 1.9 collective-permute-start.9
  106.8 1.9 collective-permute-start.4
  108.7 9.3 %collective-permute-done.9 = bf16[1,64,2048]{2,1,0:T(8,128)(2,1)S(1)} collective-permute-done((bf16[1,64,2048]{2,1,0:T(8,128)(2,1)S(1)}, bf16[1,64,2048]{2,1,0:T(8,128)(2,1)S(1)}, u32[]{:S(2)}, u32[]{:S(2)}) %collective-permute-start.9) | collective-permute-done | bytes 262176 | tf_op jit(solution)/shard_map/ppermute | solution.py:16
  118.0 1.9 collective-permute-start.10
  119.9 1.9 collective-permute-start.5
  121.9 5.7 %collective-permute-done.10 = bf16[1,64,2048]{2,1,0:T(8,128)(2,1)S(1)} collective-permute-done((bf16[1,64,2048]{2,1,0:T(8,128)(2,1)S(1)}, bf16[1,64,2048]{2,1,0:T(8,128)(2,1)S(1)}, u32[]{:S(2)}, u32[]{:S(2)}) %collective-permute-start.10) | collective-permute-done | bytes 262176 | tf_op jit(solution)/shard_map/ppermute | solution.py:16
  127.6 1.9 collective-permute-start.11
  129.6 14.4 %collective-permute-done.5 = bf16[1,64,2048]{2,1,0:T(8,128)(2,1)S(1)} collective-permute-done((bf16[1,64,2048]{2,1,0:T(8,128)(2,1)S(1)}, bf16[1,64,2048]{2,1,0:T(8,128)(2,1)S(1)}, u32[]{:S(2)}, u32[]{:S(2)}) %collective-permute-start.5) | collective-permute-done | bytes 262176 | tf_op jit(solution)/shard_map/ppermute | solution.py:16
  144.0 1.9 collective-permute-start.6
  145.9 20.3 %collective-permute-done.11 = bf16[1,64,2048]{2,1,0:T(8,128)(2,1)S(1)} collective-permute-done((bf16[1,64,2048]{2,1,0:T(8,128)(2,1)S(1)}, bf16[1,64,2048]{2,1,0:T(8,128)(2,1)S(1)}, u32[]{:S(2)}, u32[]{:S(2)}) %collective-permute-start.11) | collective-permute-done | bytes 262176 | tf_op jit(solution)/shard_map/ppermute | solution.py:16
  166.3 2.1 collective-permute-start.12
  169.1 1.1 fusion.31
  170.2 1.1 fusion.23
  171.3 9.6 %collective-permute-done.12 = bf16[1,64,2048]{2,1,0:T(8,128)(2,1)S(1)} collective-permute-done((bf16[1,64,2048]{2,1,0:T(8,128)(2,1)S(1)}, bf16[1,64,2048]{2,1,0:T(8,128)(2,1)S(1)}, u32[]{:S(2)}, u32[]{:S(2)}) %collective-permute-start.12) | collective-permute-done | bytes 262176 | tf_op jit(solution)/shard_map/ppermute | solution.py:16
  180.9 0.8 pad.14
  181.6 1.2 reshape.367
  185.2 0.5 fusion.28
  185.7 0.5 fusion.27
  187.6 0.5 fusion.22
  188.1 0.5 fusion.21
  188.5 0.5 fusion.20
  189.5 0.5 fusion.18
  190.0 0.5 fusion.17
  190.9 0.5 fusion.14
  191.4 0.5 fusion.13
  192.4 0.5 fusion.11
  192.9 0.5 fusion.10
  193.8 0.5 fusion.8
  194.3 0.5 fusion.6
  195.7 0.5 fusion.3
  198.3 1.4 maximum_multiply_fusion
  199.8 0.7 copy-done.7
  201.2 2.9 %scatter_custom_fusion = f32[768]{0:T(1024)S(1)} fusion(s32[384]{0:T(512)S(1)} %fusion.60, f32[384]{0:T(512)S(1)} %convert_element_type.25, f32[]{:T(128)} %constant.67.clone.1), kind=kCustom, calls=%fused_computation.171 | custom fusion | bytes 3076 | tf_op jit(solution)/shard_map/scatter | solution.py:86
  204.1 0.8 all_to_all.14
  204.9 8.4 %all-to-all-start = ((f32[128,6,1]{1,2,0:T(1,128)}), f32[128,6,1]{1,2,0:T(1,128)S(1)}, u32[]{:S(2)}, u32[]{:S(2)}) async-start(f32[128,6,1]{1,2,0:T(1,128)} %bitcast.3), calls=%async_computation | async-start | bytes 131072 | tf_op jit(solution)/shard_map/all_to_all | solution.py:90
  213.3 9.8 %reduce-scatter.2.cloned.1.call-done = f32[384,256]{1,0:T(8,128)} async-done(((f32[384,1024]{1,0:T(8,128)}), f32[384,256]{1,0:T(8,128)}) %reduce-scatter.2.cloned.1.call-update) | async-done | bytes 393232 | tf_op jit(solution)/shard_map/reduce_scatter | solution.py:76
  223.1 2.5 scatter_custom_fusion.1
  225.6 1.1 all_to_all.16
  226.7 15.1 %all-to-all-start.1 = ((f32[128,6,256]{2,1,0:T(8,128)}), f32[128,6,256]{2,1,0:T(8,128)S(1)}, u32[]{:S(2)}, u32[]{:S(2)}) async-start(f32[128,6,256]{2,1,0:T(8,128)} %all_to_all.16), calls=%async_computation.2 | async-start | bytes 2097152 | tf_op jit(solution)/shard_map/all_to_all | solution.py:89
  241.8 0.5 broadcast.80
  242.3 0.8 reduce.12
  243.4 29.4 %all-to-all-done.1 = f32[128,6,256]{2,1,0:T(8,128)S(1)} async-done(((f32[128,6,256]{2,1,0:T(8,128)}), f32[128,6,256]{2,1,0:T(8,128)S(1)}, u32[]{:S(2)}, u32[]{:S(2)}) %all-to-all-start.1) | async-done | bytes 786464 | tf_op jit(solution)/shard_map/all_to_all | solution.py:89
  272.9 1.0 convolution_divide_fusion
  (103 shorter events, 17.8 us)
Async XLA Ops:
  6.5 216.6 %reduce-scatter.2.cloned.1.call-start = ((), (), s32[]{:S(2)}) async-start(), calls=%async_computation.3 | async-start | bytes 1966080 | tf_op jit(solution)/shard_map/reduce_scatter | solution.py:76
  8.7 34.5 %collective-permute-start = (bf16[1,64,2048]{2,1,0:T(8,128)(2,1)S(1)}, bf16[1,64,2048]{2,1,0:T(8,128)(2,1)}, u32[]{:S(2)}, u32[]{:S(2)}) collective-permute-start(bf16[1,64,2048]{2,1,0:T(8,128)(2,1)S(1)} %fusion.49), channel_id=1, source_target_pairs={{0,4},{4,0},{8,12},{12,8},{16,20},{20,16},{24,28},{28,24},{32,36},... | collective-permute-start | bytes 786440 | tf_op jit(solution)/shard_map/ppermute | solution.py:16
  39.8 1.0 copy-start.3
  42.2 1.0 copy-start
  44.4 9.7 %collective-permute-start.1 = (bf16[1,64,2048]{2,1,0:T(8,128)(2,1)S(1)}, bf16[1,64,2048]{2,1,0:T(8,128)(2,1)S(1)}, u32[]{:S(2)}, u32[]{:S(2)}) collective-permute-start(bf16[1,64,2048]{2,1,0:T(8,128)(2,1)S(1)} %get-tuple-element.11), channel_id=1, source_target_pairs={{0,8},{4,12},{8,0},{12,4},{16,24},{20,28},{24,16},{28,20},{32,40},... | collective-permute-start | bytes 786440 | tf_op jit(solution)/shard_map/ppermute | solution.py:16
  46.8 58.0 %copy-start.5 = (f32[64,1024]{1,0:T(8,128)}, f32[64,1024]{1,0:T(8,128)S(1)}, u32[]{:S(2)}) copy-start(f32[64,1024]{1,0:T(8,128)S(1)} %fusion.32) | copy-start | bytes 786436
  46.8 13.0 %collective-permute-start.7 = (bf16[1,64,2048]{2,1,0:T(8,128)(2,1)S(1)}, bf16[1,64,2048]{2,1,0:T(8,128)(2,1)S(1)}, u32[]{:S(2)}, u32[]{:S(2)}) collective-permute-start(bf16[1,64,2048]{2,1,0:T(8,128)(2,1)S(1)} %get-tuple-element.12), channel_id=1, source_target_pairs={{0,8},{4,12},{8,0},{12,4},{16,24},{20,28},{24,16},{28,20},{32,40},... | collective-permute-start | bytes 786440 | tf_op jit(solution)/shard_map/ppermute | solution.py:16
  54.2 22.2 %collective-permute-start.2 = (bf16[1,64,2048]{2,1,0:T(8,128)(2,1)S(1)}, bf16[1,64,2048]{2,1,0:T(8,128)(2,1)S(1)}, u32[]{:S(2)}, u32[]{:S(2)}) collective-permute-start(bf16[1,64,2048]{2,1,0:T(8,128)(2,1)S(1)} %broadcast_select_fusion.8), channel_id=1, source_target_pairs={{0,16},{4,20},{8,24},{12,28},{16,0},{20,4},{24,8},{28,12},{32,48},... | collective-permute-start | bytes 786440 | tf_op jit(solution)/shard_map/ppermute | solution.py:16
  59.8 44.9 %collective-permute-start.8 = (bf16[1,64,2048]{2,1,0:T(8,128)(2,1)S(1)}, bf16[1,64,2048]{2,1,0:T(8,128)(2,1)S(1)}, u32[]{:S(2)}, u32[]{:S(2)}) collective-permute-start(bf16[1,64,2048]{2,1,0:T(8,128)(2,1)S(1)} %broadcast_select_fusion.1), channel_id=1, source_target_pairs={{0,16},{4,20},{8,24},{12,28},{16,0},{20,4},{24,8},{28,12},{32,48},... | collective-permute-start | bytes 786440 | tf_op jit(solution)/shard_map/ppermute | solution.py:16
  76.5 30.2 %collective-permute-start.3 = (bf16[1,64,2048]{2,1,0:T(8,128)(2,1)S(1)}, bf16[1,64,2048]{2,1,0:T(8,128)(2,1)S(1)}, u32[]{:S(2)}, u32[]{:S(2)}) collective-permute-start(bf16[1,64,2048]{2,1,0:T(8,128)(2,1)S(1)} %broadcast_select_fusion.9), channel_id=1, source_target_pairs={{0,32},{4,36},{8,40},{12,44},{16,48},{20,52},{24,56},{28,60},{32,0... | collective-permute-start | bytes 786440 | tf_op jit(solution)/shard_map/ppermute | solution.py:16
  104.8 13.2 %collective-permute-start.9 = (bf16[1,64,2048]{2,1,0:T(8,128)(2,1)S(1)}, bf16[1,64,2048]{2,1,0:T(8,128)(2,1)S(1)}, u32[]{:S(2)}, u32[]{:S(2)}) collective-permute-start(bf16[1,64,2048]{2,1,0:T(8,128)(2,1)S(1)} %broadcast_select_fusion.2), channel_id=1, source_target_pairs={{0,32},{4,36},{8,40},{12,44},{16,48},{20,52},{24,56},{28,60},{32,0... | collective-permute-start | bytes 786440 | tf_op jit(solution)/shard_map/ppermute | solution.py:16
  106.8 13.1 %collective-permute-start.4 = (bf16[1,64,2048]{2,1,0:T(8,128)(2,1)S(1)}, bf16[1,64,2048]{2,1,0:T(8,128)(2,1)S(1)}, u32[]{:S(2)}, u32[]{:S(2)}) collective-permute-start(bf16[1,64,2048]{2,1,0:T(8,128)(2,1)S(1)} %broadcast_select_fusion.10), channel_id=1, source_target_pairs={{0,64},{4,68},{8,72},{12,76},{16,80},{20,84},{24,88},{28,92},{32,9... | collective-permute-start | bytes 786440 | tf_op jit(solution)/shard_map/ppermute | solution.py:16
  118.0 9.6 %collective-permute-start.10 = (bf16[1,64,2048]{2,1,0:T(8,128)(2,1)S(1)}, bf16[1,64,2048]{2,1,0:T(8,128)(2,1)S(1)}, u32[]{:S(2)}, u32[]{:S(2)}) collective-permute-start(bf16[1,64,2048]{2,1,0:T(8,128)(2,1)S(1)} %broadcast_select_fusion.3), channel_id=1, source_target_pairs={{0,64},{4,68},{8,72},{12,76},{16,80},{20,84},{24,88},{28,92},{32,9... | collective-permute-start | bytes 786440 | tf_op jit(solution)/shard_map/ppermute | solution.py:16
  119.9 24.0 %collective-permute-start.5 = (bf16[1,64,2048]{2,1,0:T(8,128)(2,1)S(1)}, bf16[1,64,2048]{2,1,0:T(8,128)(2,1)S(1)}, u32[]{:S(2)}, u32[]{:S(2)}) collective-permute-start(bf16[1,64,2048]{2,1,0:T(8,128)(2,1)S(1)} %broadcast_select_fusion.11), channel_id=1, source_target_pairs={{0,128},{4,132},{8,136},{12,140},{16,144},{20,148},{24,152},{28,15... | collective-permute-start | bytes 786440 | tf_op jit(solution)/shard_map/ppermute | solution.py:16
  127.6 38.6 %collective-permute-start.11 = (bf16[1,64,2048]{2,1,0:T(8,128)(2,1)S(1)}, bf16[1,64,2048]{2,1,0:T(8,128)(2,1)S(1)}, u32[]{:S(2)}, u32[]{:S(2)}) collective-permute-start(bf16[1,64,2048]{2,1,0:T(8,128)(2,1)S(1)} %broadcast_select_fusion.4), channel_id=1, source_target_pairs={{0,128},{4,132},{8,136},{12,140},{16,144},{20,148},{24,152},{28,15... | collective-permute-start | bytes 786440 | tf_op jit(solution)/shard_map/ppermute | solution.py:16
  144.0 24.4 %collective-permute-start.6 = (bf16[1,64,2048]{2,1,0:T(8,128)(2,1)S(1)}, bf16[1,64,2048]{2,1,0:T(8,128)(2,1)S(1)}, u32[]{:S(2)}, u32[]{:S(2)}) collective-permute-start(bf16[1,64,2048]{2,1,0:T(8,128)(2,1)S(1)} %broadcast_select_fusion.12), channel_id=1, source_target_pairs={{0,256},{4,260},{8,264},{12,268},{16,272},{20,276},{24,280},{28,28... | collective-permute-start | bytes 786440 | tf_op jit(solution)/shard_map/ppermute | solution.py:16
  166.3 14.6 %collective-permute-start.12 = (bf16[1,64,2048]{2,1,0:T(8,128)(2,1)S(1)}, bf16[1,64,2048]{2,1,0:T(8,128)(2,1)S(1)}, u32[]{:S(2)}, u32[]{:S(2)}) collective-permute-start(bf16[1,64,2048]{2,1,0:T(8,128)(2,1)S(1)} %broadcast_select_fusion.5), channel_id=1, source_target_pairs={{0,256},{4,260},{8,264},{12,268},{16,272},{20,276},{24,280},{28,28... | collective-permute-start | bytes 786440 | tf_op jit(solution)/shard_map/ppermute | solution.py:16
  183.3 1.0 copy-start.2
  186.6 1.0 copy-start.1
  197.2 1.0 copy-start.4
  197.2 1.0 copy-start.6
  199.8 0.7 copy-start.7
  199.8 1.1 copy-start.8
  204.9 21.8 %all-to-all-start = ((f32[128,6,1]{1,2,0:T(1,128)}), f32[128,6,1]{1,2,0:T(1,128)S(1)}, u32[]{:S(2)}, u32[]{:S(2)}) async-start(f32[128,6,1]{1,2,0:T(1,128)} %bitcast.3), calls=%async_computation | async-start | bytes 131072 | tf_op jit(solution)/shard_map/all_to_all | solution.py:90
  226.7 46.0 %all-to-all-start.1 = ((f32[128,6,256]{2,1,0:T(8,128)}), f32[128,6,256]{2,1,0:T(8,128)S(1)}, u32[]{:S(2)}, u32[]{:S(2)}) async-start(f32[128,6,256]{2,1,0:T(8,128)} %all_to_all.16), calls=%async_computation.2 | async-start | bytes 2097152 | tf_op jit(solution)/shard_map/all_to_all | solution.py:89
Sparse Core Ops, SparseCore 0:
  199.9 23.1 reduce-scatter.1
where the time goes:
time: 282 us; the launch traced here: 281 us
  waiting for transfers between devices  147 us (52%)
  starting transfers between devices  56.9 us (20%)
  matrix products  24.9 us (9%)
  between operations  23.6 us (8%)
  local copies, waits for them, and re-layouts  21.4 us (8%)
  other arithmetic  6.75 us (2%)
    ppermute x13, waiting for transfers between devices, partner(): lax.ppermute(x, axis, [(i, i ^ 1 << bit) for i in range(lax.axis_size(axi...  108 us
    ppermute x13, starting transfers between devices, partner(): lax.ppermute(x, axis, [(i, i ^ 1 << bit) for i in range(lax.axis_size(axi...  33.4 us
    all_to_all x1, waiting for transfers between devices, body(): lax.all_to_all(outgoing, 'chan', split_axis=0, concat_axis=0, tiled=True)  29.4 us
    dot_general x48, matrix products, correlate(): jnp.einsum('acqw,aqrw->cr', doubled[:, :, p:p + quota], toeplitz, preferr...  23.9 us
    all_to_all x1, starting transfers between devices, body(): lax.all_to_all(outgoing, 'chan', split_axis=0, concat_axis=0, tiled=True)  15.1 us
    reduce_scatter x1, waiting for transfers between devices, body(): rows = lax.psum_scatter(rows, 'win', scatter_dimension=1, tiled=True)  9.84 us
    all_to_all x1, starting transfers between devices, body(): lax.all_to_all(labels, 'chan', split_axis=0, concat_axis=0, tiled=True)  8.41 us
    another operation x6, local copies, waits for them, and re-layouts, source_toeplitz(): tiled = jnp.tile(padded, (1, block_width))  6.36 us
  transfers between devices with their start and end apart: 16, of which 11 were waited for; matrix products, arithmetic and copies ran while one was open for 10% of the time, Pallas kernels for 0%

commit v1 on v0

v1 whole, which is shorter than its diff:
```python
import jax
import jax.numpy as jnp
from jax import lax
from jax.sharding import PartitionSpec as P

LAG = 512
SRC = 2
ROUNDS = 2
BINCAP = 4


block_width = 128


def normalize(traces):
    data = traces.astype(jnp.float32)
    scale = lax.rsqrt(jnp.mean(data * data, axis=-1, keepdims=True) + 1e-06)
    return (data * scale).astype(jnp.bfloat16)


def source_toeplitz(source):
    blocks = source.reshape(-1, block_width)
    padded = jnp.concatenate(
        [blocks, jnp.zeros((blocks.shape[0], block_width + 1), blocks.dtype)], axis=1
    )
    tiled = jnp.tile(padded, (1, block_width))
    return tiled[:, : 2 * block_width * block_width].reshape(
        blocks.shape[0], block_width, 2 * block_width
    )


def correlate(receivers, toeplitz):
    chans, samples = receivers.shape
    quota = samples // block_width
    lag_blocks = 2 * LAG // block_width
    extended = jnp.pad(receivers, ((0, 0), (LAG, LAG + block_width)))
    cells = extended.reshape(chans, -1, block_width)
    doubled = jnp.concatenate([cells[:, :-1], cells[:, 1:]], axis=-1)
    parts = [
        jnp.einsum(
            "cqw,sqrw->scr",
            doubled[:, p : p + quota],
            toeplitz,
            preferred_element_type=jnp.float32,
        )
        for p in range(lag_blocks)
    ]
    return jnp.concatenate(parts, axis=-1)


def bit_groups(bits):
    groups = [(0, 1)] if bits > 0 else []
    start = 1
    while start < bits:
        width = min(3, bits - start)
        groups.append((start, width))
        start += width
    return groups[1:] + groups[:1]


def exchange(payload, masks, axis):
    n = lax.axis_size(axis)
    bits = n.bit_length() - 1
    for shift, width in bit_groups(bits):
        options = [payload]
        for d in range(1, 1 << width):
            step = d << shift
            options.append(lax.ppermute(payload, axis, [(i, i ^ step) for i in range(n)]))
        stacked = jnp.stack(options)
        picks = jnp.bitwise_and(jnp.right_shift(masks, shift), (1 << width) - 1)
        payload = jnp.stack([stacked[picks[r], r] for r in range(masks.shape[0])])
    return payload


def body(traces, round_masks, row_owner, row_slot):
    wins, chans, samples = traces.shape
    rows_set = SRC * chans
    normed = normalize(traces)[0]
    stride = chans // SRC
    sources = normed[::stride, :]
    owner = row_owner[:, 0]
    slot = row_slot
    label_rows = []
    for r in range(ROUNDS):
        part = slice((r + 1) * rows_set, (r + 2) * rows_set)
        row = jnp.concatenate([owner[part], slot[part]]).astype(jnp.bfloat16)
        row = jnp.pad(row, (0, samples - row.shape[0]))
        label_rows.append(jnp.concatenate([sources, row[None, :]], axis=0))
    payload = jnp.stack(label_rows)
    arrived = exchange(payload, round_masks, "chan")
    all_sources = jnp.concatenate([sources] + [arrived[r, :SRC] for r in range(ROUNDS)], axis=0)
    toeplitz = jax.vmap(source_toeplitz)(all_sources)
    rows = correlate(normed, toeplitz).reshape(-1, 2 * LAG) / jnp.sqrt(jnp.float32(samples))
    rows = lax.psum_scatter(rows, "win", scatter_dimension=1, tiled=True)
    owners_total = lax.axis_size("chan")
    nbins = owners_total * BINCAP
    bins_parts = [owner[:rows_set] * BINCAP + slot[:rows_set]]
    for r in range(ROUNDS):
        got = arrived[r, SRC].astype(jnp.int32)
        bins_parts.append(got[:rows_set] * BINCAP + got[rows_set : 2 * rows_set])
    bins = jnp.concatenate(bins_parts)
    picks = (bins[None, :] == jnp.arange(nbins, dtype=jnp.int32)[:, None]).astype(jnp.float32)
    local = jnp.dot(picks, rows, precision=lax.Precision.HIGHEST, preferred_element_type=jnp.float32)
    sums = lax.psum_scatter(local, "chan", scatter_dimension=0, tiled=True)
    own_bins = owner * BINCAP + slot
    own_counts = jnp.sum(
        (own_bins[None, :] == jnp.arange(nbins, dtype=jnp.int32)[:, None]).astype(jnp.float32), axis=1
    )
    counts = lax.psum_scatter(own_counts, "chan", scatter_dimension=0, tiled=True)
    return sums / jnp.sqrt(jnp.maximum(counts, 1.0))[:, None]


def solution(mesh):
    return jax.shard_map(
        body,
        mesh=mesh,
        in_specs=(P("win", "chan", None), P(), P("chan", None), P("chan")),
        out_specs=P("chan", "win"),
        check_vma=False,
    )
```

time: 282 us -> 431 us (1.53)
  blocking collectives: 0 us -> 249 us
  waiting for transfers between devices: 147 us -> 31.9 us
  starting transfers between devices: 56.9 us -> 65.4 us
  local copies, waits for them, and re-layouts: 21.4 us -> 28.3 us
  matrix products: 24.9 us -> 18.4 us
    unnamed x0 -> x1, blocking collectives: none -> 249 us
    ppermute x13 -> x15, waiting for transfers between devices: 108 us -> 8.33 us  [exchange(): lax.ppermute(payload, axis, [(i, i ^ step) for i in range(n)])]
    ppermute x13 -> x15, starting transfers between devices: 33.4 us -> 65.4 us  [exchange(): lax.ppermute(payload, axis, [(i, i ^ step) for i in range(n)])]
    all_to_all x2 -> x0, waiting for transfers between devices: 29.4 us -> none  [the longest x1 29.4 us: body(): lax.all_to_all(outgoing, 'chan', split_axis=0, concat_axis=0, tiled=True)]
    all_to_all x2 -> x0, starting transfers between devices: 23.5 us -> none  [the longest x1 15.1 us: body(): lax.all_to_all(outgoing, 'chan', split_axis=0, concat_axis=0, tiled=True)]
    reduce_scatter x1, waiting for transfers between devices: 9.84 us -> 23.5 us  [body(): rows = lax.psum_scatter(rows, 'win', scatter_dimension=1, tiled=True)]
    another operation x6 -> x2, local copies, waits for them, and re-layouts: 6.36 us -> 20 us  [source_toeplitz(): tiled = jnp.tile(padded, (1, block_width))]
    dot_general x49 -> x9, matrix products: 24.9 us -> 18.4 us  [the longest x8 16 us: correlate(): jnp.einsum('cqw,sqrw->scr', doubled[:, p:p + quota], toeplitz, preferred_...]
  transfers between devices with their start and end apart: 16 -> 17, of which waited for: 11 -> 3; matrix products, arithmetic and copies ran while one was open for 10% -> 1% of each run, Pallas kernels for 0% -> 0%
where the time goes in v1:
time: 431 us; the launch traced here: 427 us
  blocking collectives  249 us (58%)
  starting transfers between devices  65.4 us (15%)
  waiting for transfers between devices  31.9 us (7%)
  local copies, waits for them, and re-layouts  28.3 us (7%)
  between operations  25.9 us (6%)
  matrix products  18.4 us (4%)
  other arithmetic  8.35 us (2%)
    unnamed x1, blocking collectives  249 us
    ppermute x15, starting transfers between devices, exchange(): lax.ppermute(payload, axis, [(i, i ^ step) for i in range(n)])  65.4 us
    reduce_scatter x1, waiting for transfers between devices, body(): rows = lax.psum_scatter(rows, 'win', scatter_dimension=1, tiled=True)  23.5 us
    another operation x2, local copies, waits for them, and re-layouts, source_toeplitz(): tiled = jnp.tile(padded, (1, block_width))  20 us
    dot_general x8, matrix products, correlate(): jnp.einsum('cqw,sqrw->scr', doubled[:, p:p + quota], toeplitz, preferred_...  16 us
  transfers between devices with their start and end apart: 17, of which 3 were waited for; matrix products, arithmetic and copies ran while one was open for 1% of the time, Pallas kernels for 0%

profile of v1, /device:TPU:1, one launch (start us, length us, event | category | flops | bytes accessed | tf_op | source)
XLA Modules:
  0.0 427.2 jit_solution(17713541522185132424)
XLA Ops:
  6.5 0.8 multiply_reduce_fusion
  7.3 0.8 fusion.91
  8.1 1.1 fusion.65
  9.2 1.1 fusion.68
  10.4 4.0 collective-permute-start
  14.5 4.2 collective-permute-start.1
  18.7 1.9 collective-permute-start.2
  20.6 7.4 %collective-permute-start.3 = (bf16[2,3,2048]{2,1,0:T(4,128)(2,1)S(1)}, bf16[2,3,2048]{2,1,0:T(4,128)(2,1)S(1)}, u32[]{:S(2)}, u32[]{:S(2)}) collective-permute-start(bf16[2,3,2048]{2,1,0:T(4,128)(2,1)S(1)} %pad_maximum_fusion), channel_id=1, source_target_pairs={{0,32},{4,36},{8,40},{12,44},{16,48},{20,52},{24,56},{28,60},{32,0... | collective-permute-start | bytes 73736 | tf_op jit(solution)/shard_map/ppermute | solution.py:68
  28.0 1.9 collective-permute-start.4
  30.0 0.7 shift-right-arithmetic_and_fusion.1
  30.7 0.2 reshape.57
  30.9 0.2 fusion.90
  31.1 0.1 copy_dynamic-update-slice_fusion.1
  31.1 0.7 fusion.93
  31.8 0.6 fusion.95
  39.8 0.0 collective-permute-done
  39.8 4.9 %collective-permute-start.5 = (bf16[2,3,2048]{2,1,0:T(4,128)(2,1)S(1)}, bf16[2,3,2048]{2,1,0:T(4,128)(2,1)S(1)}, u32[]{:S(2)}, u32[]{:S(2)}) collective-permute-start(bf16[2,3,2048]{2,1,0:T(4,128)(2,1)S(1)} %pad_maximum_fusion), channel_id=1, source_target_pairs={{0,48},{4,52},{8,56},{12,60},{16,32},{20,36},{24,40},{28,44},{32,1... | collective-permute-start | bytes 73736 | tf_op jit(solution)/shard_map/ppermute | solution.py:68
  44.7 0.0 collective-permute-done.1
  44.7 1.9 collective-permute-start.6
  46.7 0.0 collective-permute-done.2
  46.7 0.0 collective-permute-done.3
  46.8 0.0 collective-permute-done.4
  46.8 0.0 collective-permute-done.5
  46.8 3.8 collective-permute-done.6
  50.7 4.0 collective-permute-start.7
  54.7 5.8 %collective-permute-start.8 = (bf16[2,3,2048]{2,1,0:T(4,128)(2,1)S(1)}, bf16[2,3,2048]{2,1,0:T(4,128)(2,1)S(1)}, u32[]{:S(2)}, u32[]{:S(2)}) collective-permute-start(bf16[2,3,2048]{2,1,0:T(4,128)(2,1)S(1)} %pad_maximum_fusion.1), channel_id=1, source_target_pairs={{0,128},{4,132},{8,136},{12,140},{16,144},{20,148},{24,152},{28,15... | collective-permute-start | bytes 73736 | tf_op jit(solution)/shard_map/ppermute | solution.py:68
  60.5 1.9 collective-permute-start.9
  62.5 8.2 %collective-permute-start.10 = (bf16[2,3,2048]{2,1,0:T(4,128)(2,1)S(1)}, bf16[2,3,2048]{2,1,0:T(4,128)(2,1)S(1)}, u32[]{:S(2)}, u32[]{:S(2)}) collective-permute-start(bf16[2,3,2048]{2,1,0:T(4,128)(2,1)S(1)} %pad_maximum_fusion.1), channel_id=1, source_target_pairs={{0,256},{4,260},{8,264},{12,268},{16,272},{20,276},{24,280},{28,28... | collective-permute-start | bytes 73736 | tf_op jit(solution)/shard_map/ppermute | solution.py:68
  70.7 1.9 collective-permute-start.11
  72.6 0.0 collective-permute-done.7
  72.6 7.3 %collective-permute-start.12 = (bf16[2,3,2048]{2,1,0:T(4,128)(2,1)S(1)}, bf16[2,3,2048]{2,1,0:T(4,128)(2,1)S(1)}, u32[]{:S(2)}, u32[]{:S(2)}) collective-permute-start(bf16[2,3,2048]{2,1,0:T(4,128)(2,1)S(1)} %pad_maximum_fusion.1), channel_id=1, source_target_pairs={{0,384},{4,388},{8,392},{12,396},{16,400},{20,404},{24,408},{28,41... | collective-permute-start | bytes 73736 | tf_op jit(solution)/shard_map/ppermute | solution.py:68
  79.9 0.0 collective-permute-done.8
  79.9 1.9 collective-permute-start.13
  81.9 0.0 collective-permute-done.9
  81.9 0.0 collective-permute-done.10
  82.0 4.5 %collective-permute-done.13 = bf16[2,3,2048]{2,1,0:T(4,128)(2,1)S(1)} collective-permute-done((bf16[2,3,2048]{2,1,0:T(4,128)(2,1)S(1)}, bf16[2,3,2048]{2,1,0:T(4,128)(2,1)S(1)}, u32[]{:S(2)}, u32[]{:S(2)}) %collective-permute-start.13) | collective-permute-done | bytes 24608 | tf_op jit(solution)/shard_map/ppermute | solution.py:68
  86.7 8.0 %collective-permute-start.14 = (bf16[2,3,2048]{2,1,0:T(4,128)(2,1)S(1)}, bf16[2,3,2048]{2,1,0:T(4,128)(2,1)S(1)}, u32[]{:S(2)}, u32[]{:S(2)}) collective-permute-start(bf16[2,3,2048]{2,1,0:T(4,128)(2,1)S(1)} %get-tuple-element.14), channel_id=1, source_target_pairs={{0,4},{4,0},{8,12},{12,8},{16,20},{20,16},{24,28},{28,24},{32,36},... | collective-permute-start | bytes 73736 | tf_op jit(solution)/shard_map/ppermute | solution.py:68
  94.7 0.1 copy_dynamic-update-slice_fusion
  98.8 0.0 collective-permute-done.14
  98.9 0.1 fusion.78
  99.0 4.5 %tile.4 = bf16[6,16,128,257]{3,2,1,0:T(8,128)(2,1)} broadcast(bf16[6,16,257]{2,1,0:T(8,128)(2,1)S(1)} %fusion.73), dimensions={0,1,3} | broadcast | bytes 6365376 | tf_op jit(solution)/shard_map/vmap()/tile | solution.py:26
  103.5 15.5 %tile.10 = bf16[6,16,32896]{2,1,0:T(8,128)(2,1)} reshape(bf16[6,16,128,257]{3,2,1,0:T(8,128)(2,1)} %tile.4) | data formatting | bytes 12632064 | tf_op jit(solution)/shard_map/vmap()/tile | solution.py:26
  119.0 2.8 slice-done
  121.8 1.9 copy.24
  123.7 2.0 fusion.19
  125.7 2.0 fusion.25
  127.7 2.0 fusion.31
  129.7 2.0 fusion.37
  131.7 2.0 fusion.43
  133.7 2.0 fusion.49
  135.7 2.0 fusion.55
  137.7 2.0 fusion.61
  139.7 1.4 broadcast_multiply_fusion
  141.1 0.0 reduce-scatter.2.cloned.1.call-update
  141.1 0.0 all-reduce.8.cloned.1.call-start
  141.2 0.7 bitcast_add_fusion
  141.9 23.5 %reduce-scatter.2.cloned.1.call-done = f32[384,256]{1,0:T(8,128)} async-done(((f32[384,1024]{1,0:T(8,128)}), f32[384,256]{1,0:T(8,128)}) %reduce-scatter.2.cloned.1.call-update) | async-done | bytes 393232 | tf_op jit(solution)/shard_map/reduce_scatter | solution.py:94
  165.5 2.4 fusion.64
  167.9 0.0 all-reduce.8.cloned.1.call-update
  167.9 1.3 dynamic-slice
  169.8 0.2 convert_reduce_fusion
  170.0 248.9 %all-reduce.5 = f32[512]{0:T(512)S(1)} all-reduce(f32[512]{0:T(512)S(1)} %convert_reduce_fusion), channel_id=4, replica_groups=mesh['chan'=128,'win'=4] {'chan'}, use_global_device_ids=true, to_apply=%region_4.5.clone | all-reduce | flops 512 | bytes 4096
  418.9 0.1 fusion.88
  419.0 1.4 dynamic-slice_divide_fusion
  (46 shorter events, 0.7 us)
Async XLA Ops:
  6.5 158.9 %reduce-scatter.2.cloned.1.call-start = ((), (), s32[]{:S(2)}) async-start(), calls=%async_computation.1 | async-start | bytes 1966080 | tf_op jit(solution)/shard_map/reduce_scatter | solution.py:94
  10.4 29.3 %collective-permute-start = (bf16[2,3,2048]{2,1,0:T(4,128)(2,1)S(1)}, bf16[2,3,2048]{2,1,0:T(4,128)(2,1)S(1)}, u32[]{:S(2)}, u32[]{:S(2)}) collective-permute-start(bf16[2,3,2048]{2,1,0:T(4,128)(2,1)S(1)} %pad_maximum_fusion), channel_id=1, source_target_pairs={{0,8},{4,12},{8,0},{12,4},{16,24},{20,28},{24,16},{28,20},{32,40},... | collective-permute-start | bytes 73736 | tf_op jit(solution)/shard_map/ppermute | solution.py:68
  14.5 30.3 %collective-permute-start.1 = (bf16[2,3,2048]{2,1,0:T(4,128)(2,1)S(1)}, bf16[2,3,2048]{2,1,0:T(4,128)(2,1)S(1)}, u32[]{:S(2)}, u32[]{:S(2)}) collective-permute-start(bf16[2,3,2048]{2,1,0:T(4,128)(2,1)S(1)} %pad_maximum_fusion), channel_id=1, source_target_pairs={{0,16},{4,20},{8,24},{12,28},{16,0},{20,4},{24,8},{28,12},{32,48},... | collective-permute-start | bytes 73736 | tf_op jit(solution)/shard_map/ppermute | solution.py:68
  18.7 28.0 %collective-permute-start.2 = (bf16[2,3,2048]{2,1,0:T(4,128)(2,1)S(1)}, bf16[2,3,2048]{2,1,0:T(4,128)(2,1)S(1)}, u32[]{:S(2)}, u32[]{:S(2)}) collective-permute-start(bf16[2,3,2048]{2,1,0:T(4,128)(2,1)S(1)} %pad_maximum_fusion), channel_id=1, source_target_pairs={{0,24},{4,28},{8,16},{12,20},{16,8},{20,12},{24,0},{28,4},{32,56},... | collective-permute-start | bytes 73736 | tf_op jit(solution)/shard_map/ppermute | solution.py:68
  20.6 26.1 %collective-permute-start.3 = (bf16[2,3,2048]{2,1,0:T(4,128)(2,1)S(1)}, bf16[2,3,2048]{2,1,0:T(4,128)(2,1)S(1)}, u32[]{:S(2)}, u32[]{:S(2)}) collective-permute-start(bf16[2,3,2048]{2,1,0:T(4,128)(2,1)S(1)} %pad_maximum_fusion), channel_id=1, source_target_pairs={{0,32},{4,36},{8,40},{12,44},{16,48},{20,52},{24,56},{28,60},{32,0... | collective-permute-start | bytes 73736 | tf_op jit(solution)/shard_map/ppermute | solution.py:68
  28.0 18.7 %collective-permute-start.4 = (bf16[2,3,2048]{2,1,0:T(4,128)(2,1)S(1)}, bf16[2,3,2048]{2,1,0:T(4,128)(2,1)S(1)}, u32[]{:S(2)}, u32[]{:S(2)}) collective-permute-start(bf16[2,3,2048]{2,1,0:T(4,128)(2,1)S(1)} %pad_maximum_fusion), channel_id=1, source_target_pairs={{0,40},{4,44},{8,32},{12,36},{16,56},{20,60},{24,48},{28,52},{32,8... | collective-permute-start | bytes 73736 | tf_op jit(solution)/shard_map/ppermute | solution.py:68
  39.8 7.0 %collective-permute-start.5 = (bf16[2,3,2048]{2,1,0:T(4,128)(2,1)S(1)}, bf16[2,3,2048]{2,1,0:T(4,128)(2,1)S(1)}, u32[]{:S(2)}, u32[]{:S(2)}) collective-permute-start(bf16[2,3,2048]{2,1,0:T(4,128)(2,1)S(1)} %pad_maximum_fusion), channel_id=1, source_target_pairs={{0,48},{4,52},{8,56},{12,60},{16,32},{20,36},{24,40},{28,44},{32,1... | collective-permute-start | bytes 73736 | tf_op jit(solution)/shard_map/ppermute | solution.py:68
  44.7 5.9 %collective-permute-start.6 = (bf16[2,3,2048]{2,1,0:T(4,128)(2,1)S(1)}, bf16[2,3,2048]{2,1,0:T(4,128)(2,1)S(1)}, u32[]{:S(2)}, u32[]{:S(2)}) collective-permute-start(bf16[2,3,2048]{2,1,0:T(4,128)(2,1)S(1)} %pad_maximum_fusion), channel_id=1, source_target_pairs={{0,56},{4,60},{8,48},{12,52},{16,40},{20,44},{24,32},{28,36},{32,2... | collective-permute-start | bytes 73736 | tf_op jit(solution)/shard_map/ppermute | solution.py:68
  50.7 21.9 %collective-permute-start.7 = (bf16[2,3,2048]{2,1,0:T(4,128)(2,1)S(1)}, bf16[2,3,2048]{2,1,0:T(4,128)(2,1)S(1)}, u32[]{:S(2)}, u32[]{:S(2)}) collective-permute-start(bf16[2,3,2048]{2,1,0:T(4,128)(2,1)S(1)} %pad_maximum_fusion.1), channel_id=1, source_target_pairs={{0,64},{4,68},{8,72},{12,76},{16,80},{20,84},{24,88},{28,92},{32,9... | collective-permute-start | bytes 73736 | tf_op jit(solution)/shard_map/ppermute | solution.py:68
  54.7 25.2 %collective-permute-start.8 = (bf16[2,3,2048]{2,1,0:T(4,128)(2,1)S(1)}, bf16[2,3,2048]{2,1,0:T(4,128)(2,1)S(1)}, u32[]{:S(2)}, u32[]{:S(2)}) collective-permute-start(bf16[2,3,2048]{2,1,0:T(4,128)(2,1)S(1)} %pad_maximum_fusion.1), channel_id=1, source_target_pairs={{0,128},{4,132},{8,136},{12,140},{16,144},{20,148},{24,152},{28,15... | collective-permute-start | bytes 73736 | tf_op jit(solution)/shard_map/ppermute | solution.py:68
  60.5 21.4 %collective-permute-start.9 = (bf16[2,3,2048]{2,1,0:T(4,128)(2,1)S(1)}, bf16[2,3,2048]{2,1,0:T(4,128)(2,1)S(1)}, u32[]{:S(2)}, u32[]{:S(2)}) collective-permute-start(bf16[2,3,2048]{2,1,0:T(4,128)(2,1)S(1)} %pad_maximum_fusion.1), channel_id=1, source_target_pairs={{0,192},{4,196},{8,200},{12,204},{16,208},{20,212},{24,216},{28,22... | collective-permute-start | bytes 73736 | tf_op jit(solution)/shard_map/ppermute | solution.py:68
  62.5 19.5 %collective-permute-start.10 = (bf16[2,3,2048]{2,1,0:T(4,128)(2,1)S(1)}, bf16[2,3,2048]{2,1,0:T(4,128)(2,1)S(1)}, u32[]{:S(2)}, u32[]{:S(2)}) collective-permute-start(bf16[2,3,2048]{2,1,0:T(4,128)(2,1)S(1)} %pad_maximum_fusion.1), channel_id=1, source_target_pairs={{0,256},{4,260},{8,264},{12,268},{16,272},{20,276},{24,280},{28,28... | collective-permute-start | bytes 73736 | tf_op jit(solution)/shard_map/ppermute | solution.py:68
  70.7 11.3 %collective-permute-start.11 = (bf16[2,3,2048]{2,1,0:T(4,128)(2,1)S(1)}, bf16[2,3,2048]{2,1,0:T(4,128)(2,1)S(1)}, u32[]{:S(2)}, u32[]{:S(2)}) collective-permute-start(bf16[2,3,2048]{2,1,0:T(4,128)(2,1)S(1)} %pad_maximum_fusion.1), channel_id=1, source_target_pairs={{0,320},{4,324},{8,328},{12,332},{16,336},{20,340},{24,344},{28,34... | collective-permute-start | bytes 73736 | tf_op jit(solution)/shard_map/ppermute | solution.py:68
  72.6 9.4 %collective-permute-start.12 = (bf16[2,3,2048]{2,1,0:T(4,128)(2,1)S(1)}, bf16[2,3,2048]{2,1,0:T(4,128)(2,1)S(1)}, u32[]{:S(2)}, u32[]{:S(2)}) collective-permute-start(bf16[2,3,2048]{2,1,0:T(4,128)(2,1)S(1)} %pad_maximum_fusion.1), channel_id=1, source_target_pairs={{0,384},{4,388},{8,392},{12,396},{16,400},{20,404},{24,408},{28,41... | collective-permute-start | bytes 73736 | tf_op jit(solution)/shard_map/ppermute | solution.py:68
  79.9 6.6 %collective-permute-start.13 = (bf16[2,3,2048]{2,1,0:T(4,128)(2,1)S(1)}, bf16[2,3,2048]{2,1,0:T(4,128)(2,1)S(1)}, u32[]{:S(2)}, u32[]{:S(2)}) collective-permute-start(bf16[2,3,2048]{2,1,0:T(4,128)(2,1)S(1)} %pad_maximum_fusion.1), channel_id=1, source_target_pairs={{0,448},{4,452},{8,456},{12,460},{16,464},{20,468},{24,472},{28,47... | collective-permute-start | bytes 73736 | tf_op jit(solution)/shard_map/ppermute | solution.py:68
  86.7 12.2 %collective-permute-start.14 = (bf16[2,3,2048]{2,1,0:T(4,128)(2,1)S(1)}, bf16[2,3,2048]{2,1,0:T(4,128)(2,1)S(1)}, u32[]{:S(2)}, u32[]{:S(2)}) collective-permute-start(bf16[2,3,2048]{2,1,0:T(4,128)(2,1)S(1)} %get-tuple-element.14), channel_id=1, source_target_pairs={{0,4},{4,0},{8,12},{12,8},{16,20},{20,16},{24,28},{28,24},{32,36},... | collective-permute-start | bytes 73736 | tf_op jit(solution)/shard_map/ppermute | solution.py:68
  119.0 2.8 slice-start
  141.1 277.9 %all-reduce.8.cloned.1.call-start = ((), (), s32[]{:S(2)}) async-start(), calls=%async_computation.2 | async-start | bytes 1048576
Sparse Core Ops, SparseCore 0:
  141.2 24.1 reduce-scatter.1
  168.7 193.7 all-reduce.7

commit v2 on v1

--- a/solution.py
+++ b/solution.py
@@ -48,28 +48,33 @@
     return jnp.concatenate(parts, axis=-1)
 
 
-def bit_groups(bits):
-    groups = [(0, 1)] if bits > 0 else []
-    start = 1
-    while start < bits:
-        width = min(3, bits - start)
-        groups.append((start, width))
-        start += width
-    return groups[1:] + groups[:1]
+def xor_permute(x, mask, axis, shift, width):
+    n = lax.axis_size(axis)
+
+    def moved(step):
+        return lambda v: lax.ppermute(v, axis, [(i, i ^ step) for i in range(n)])
+
+    branches = [lambda v: v] + [moved(d << shift) for d in range(1, 1 << width)]
+    part = jnp.bitwise_and(jnp.right_shift(mask, shift), (1 << width) - 1)
+    return lax.switch(part, branches, x)
 
 
 def exchange(payload, masks, axis):
     n = lax.axis_size(axis)
     bits = n.bit_length() - 1
-    for shift, width in bit_groups(bits):
-        options = [payload]
-        for d in range(1, 1 << width):
-            step = d << shift
-            options.append(lax.ppermute(payload, axis, [(i, i ^ step) for i in range(n)]))
-        stacked = jnp.stack(options)
-        picks = jnp.bitwise_and(jnp.right_shift(masks, shift), (1 << width) - 1)
-        payload = jnp.stack([stacked[picks[r], r] for r in range(masks.shape[0])])
-    return payload
+    full = n - 1
+    first_full = masks[0] == full
+    other = jnp.bitwise_xor(jnp.bitwise_xor(masks[0], masks[1]), full)
+    fixed = jnp.where(first_full, payload[0], payload[1])
+    free = jnp.where(first_full, payload[1], payload[0])
+    fixed = lax.ppermute(fixed, axis, [(i, i ^ full) for i in range(n)])
+    low = min(bits, 4)
+    free = xor_permute(free, other, axis, 0, low)
+    if bits > low:
+        free = xor_permute(free, other, axis, low, bits - low)
+    return jnp.stack(
+        [jnp.where(first_full, fixed, free), jnp.where(first_full, free, fixed)]
+    )
 
 
 def body(traces, round_masks, row_owner, row_slot):
@@ -101,12 +106,14 @@
     bins = jnp.concatenate(bins_parts)
     picks = (bins[None, :] == jnp.arange(nbins, dtype=jnp.int32)[:, None]).astype(jnp.float32)
     local = jnp.dot(picks, rows, precision=lax.Precision.HIGHEST, preferred_element_type=jnp.float32)
-    sums = lax.psum_scatter(local, "chan", scatter_dimension=0, tiled=True)
+    arrived_sums = lax.all_to_all(local, "chan", split_axis=0, concat_axis=0, tiled=True)
+    sums = jnp.sum(arrived_sums.reshape(owners_total, BINCAP, -1), axis=0)
     own_bins = owner * BINCAP + slot
     own_counts = jnp.sum(
         (own_bins[None, :] == jnp.arange(nbins, dtype=jnp.int32)[:, None]).astype(jnp.float32), axis=1
     )
-    counts = lax.psum_scatter(own_counts, "chan", scatter_dimension=0, tiled=True)
+    arrived_counts = lax.all_to_all(own_counts, "chan", split_axis=0, concat_axis=0, tiled=True)
+    counts = jnp.sum(arrived_counts.reshape(owners_total, BINCAP), axis=0)
     return sums / jnp.sqrt(jnp.maximum(counts, 1.0))[:, None]
 
 

time: 431 us -> 154 us (0.36)
  blocking collectives: 249 us -> 0 us
  starting transfers between devices: 65.4 us -> 43.5 us
  between operations: 25.9 us -> 15.5 us
  waiting for transfers between devices: 31.9 us -> 41 us
    unnamed x1 -> x0, blocking collectives: 249 us -> none
    ppermute x15 -> x3, starting transfers between devices: 65.4 us -> 18.8 us  [the longest x1 15 us: exchange(): fixed = lax.ppermute(fixed, axis, [(i, i ^ full) for i in range(n)])]
    all_to_all x0 -> x2, starting transfers between devices: none -> 24.7 us  [the longest x1 15.1 us: body(): lax.all_to_all(local, 'chan', split_axis=0, concat_axis=0, tiled=True)]
    all_to_all x0 -> x2, waiting for transfers between devices: none -> 20.4 us  [the longest x1 20.4 us: body(): lax.all_to_all(local, 'chan', split_axis=0, concat_axis=0, tiled=True)]
    reduce_scatter x1, waiting for transfers between devices: 23.5 us -> 15.7 us  [body(): rows = lax.psum_scatter(rows, 'win', scatter_dimension=1, tiled=True)]
  transfers between devices with their start and end apart: 17 -> 6, of which waited for: 3 -> 4; matrix products, arithmetic and copies ran while one was open for 1% -> 2% of each run, Pallas kernels for 0% -> 0%
where the time goes in v2:
time: 154 us; the launch traced here: 153 us
  starting transfers between devices  43.5 us (28%)
  waiting for transfers between devices  41 us (27%)
  local copies, waits for them, and re-layouts  28.4 us (18%)
  matrix products  17.6 us (11%)
  between operations  15.5 us (10%)
  other arithmetic  7.06 us (5%)
    all_to_all x1, waiting for transfers between devices, body(): lax.all_to_all(local, 'chan', split_axis=0, concat_axis=0, tiled=True)  20.4 us
    another operation x2, local copies, waits for them, and re-layouts, source_toeplitz(): tiled = jnp.tile(padded, (1, block_width))  20 us
    dot_general x8, matrix products, correlate(): jnp.einsum('cqw,sqrw->scr', doubled[:, p:p + quota], toeplitz, preferred_...  16 us
    reduce_scatter x1, waiting for transfers between devices, body(): rows = lax.psum_scatter(rows, 'win', scatter_dimension=1, tiled=True)  15.7 us
    all_to_all x1, starting transfers between devices, body(): lax.all_to_all(local, 'chan', split_axis=0, concat_axis=0, tiled=True)  15.1 us
    ppermute x1, starting transfers between devices, exchange(): fixed = lax.ppermute(fixed, axis, [(i, i ^ full) for i in range(n)])  15 us
    all_to_all x1, starting transfers between devices, body(): lax.all_to_all(own_counts, 'chan', split_axis=0, concat_axis=0, tiled=True)  9.63 us
    ppermute x2, waiting for transfers between devices, moved(): return lambda v: lax.ppermute(v, axis, [(i, i ^ step) for i in range(n)])  4.91 us
  transfers between devices with their start and end apart: 6, of which 4 were waited for; matrix products, arithmetic and copies ran while one was open for 2% of the time, Pallas kernels for 0%

profile of v2, /device:TPU:1, one launch (start us, length us, event | category | flops | bytes accessed | tf_op | source)
XLA Modules:
  0.0 153.4 jit_solution(11332535798507993273)
XLA Ops:
  6.5 0.0 reduce-scatter.2.cloned.1.call-start
  6.5 0.8 multiply_reduce_fusion
  7.3 0.8 fusion.83
  8.1 1.3 fusion.85
  9.4 1.1 fusion.65
  10.6 1.1 fusion.68
  12.3 15.0 %collective-permute-start.22 = (bf16[3,2048]{1,0:T(4,128)(2,1)S(1)}, bf16[3,2048]{1,0:T(4,128)(2,1)S(1)}, u32[]{:S(2)}, u32[]{:S(2)}) collective-permute-start(bf16[3,2048]{1,0:T(4,128)(2,1)S(1)} %get-tuple-element.59), channel_id=1, source_target_pairs={{0,508},{4,504},{8,500},{12,496},{16,492},{20,488},{24,484},{28,48... | collective-permute-start | bytes 36872 | tf_op jit(solution)/shard_map/ppermute | solution.py:70
  27.3 0.2 reshape.81
  27.5 0.2 fusion.82
  27.7 0.1 copy_dynamic-update-slice_fusion.1
  27.8 0.1 copy_dynamic-update-slice_fusion
  29.2 3.1 %conditional.2 = (bf16[3,2048]{1,0:T(4,128)(2,1)S(1)}) conditional(s32[]{:T(128)} %bitcast.6, bf16[3,2048]{1,0:T(4,128)(2,1)S(1)} %get-tuple-element.60, bf16[3,2048]{1,0:T(4,128)(2,1)S(1)} %get-tuple-element.60, bf16[3,2048]{1,0:T(4,128)(2,1)S(1)} %get-tuple-element.60, ...), branch_computations={%region_1.2_spmd, %region_2.3_spmd, %region_3.4_spmd, %region_4.5_... | conditional | bytes 73776 | solution.py:59
  29.2 1.9 %collective-permute-start = (bf16[3,2048]{1,0:T(4,128)(2,1)S(1)}, bf16[3,2048]{1,0:T(4,128)(2,1)S(1)}, u32[]{:S(2)}, u32[]{:S(2)}) collective-permute-start(bf16[3,2048]{1,0:T(4,128)(2,1)S(1)} %param.1), channel_id=1, source_target_pairs={{0,4},{4,0},{8,12},{12,8},{16,20},{20,16},{24,28},{28,24},{32,36},... | collective-permute-start | bytes 36872 | tf_op jit(solution)/shard_map/cond/branch_1_fun/ppermute | solution.py:55
  31.1 1.1 collective-permute-done
  32.3 5.9 %conditional.3 = (bf16[3,2048]{1,0:T(4,128)(2,1)S(1)}) conditional(s32[]{:T(128)} %bitcast.5, bf16[3,2048]{1,0:T(4,128)(2,1)S(1)} %get-tuple-element.73, bf16[3,2048]{1,0:T(4,128)(2,1)S(1)} %get-tuple-element.73, bf16[3,2048]{1,0:T(4,128)(2,1)S(1)} %get-tuple-element.73, ...), branch_computations={%region_17.18_spmd, %region_18.19_spmd, %region_19.20_spmd, %regio... | conditional | bytes 73776 | solution.py:59
  32.4 1.9 %collective-permute-start.21 = (bf16[3,2048]{1,0:T(4,128)(2,1)S(1)}, bf16[3,2048]{1,0:T(4,128)(2,1)S(1)}, u32[]{:S(2)}, u32[]{:S(2)}) collective-permute-start(bf16[3,2048]{1,0:T(4,128)(2,1)S(1)} %param.23), channel_id=1, source_target_pairs={{0,448},{4,452},{8,456},{12,460},{16,464},{20,468},{24,472},{28,47... | collective-permute-start | bytes 36872 | tf_op jit(solution)/shard_map/cond/branch_7_fun/ppermute | solution.py:55
  34.3 3.8 %collective-permute-done.21 = bf16[3,2048]{1,0:T(4,128)(2,1)S(1)} collective-permute-done((bf16[3,2048]{1,0:T(4,128)(2,1)S(1)}, bf16[3,2048]{1,0:T(4,128)(2,1)S(1)}, u32[]{:S(2)}, u32[]{:S(2)}) %collective-permute-start.21) | collective-permute-done | bytes 12320 | tf_op jit(solution)/shard_map/cond/branch_7_fun/ppermute | solution.py:55
  38.2 0.0 collective-permute-done.22
  38.4 4.5 %tile.4 = bf16[6,16,128,257]{3,2,1,0:T(8,128)(2,1)} broadcast(bf16[6,16,257]{2,1,0:T(8,128)(2,1)S(1)} %fusion.73), dimensions={0,1,3} | broadcast | bytes 6365376 | tf_op jit(solution)/shard_map/vmap()/tile | solution.py:26
  42.9 15.5 %tile.10 = bf16[6,16,32896]{2,1,0:T(8,128)(2,1)} reshape(bf16[6,16,128,257]{3,2,1,0:T(8,128)(2,1)} %tile.4) | data formatting | bytes 12632064 | tf_op jit(solution)/shard_map/vmap()/tile | solution.py:26
  58.4 0.0 slice-start
  58.4 2.8 %slice-done = bf16[6,16,32768]{2,1,0:T(8,128)(2,1)S(1)} async-done(((bf16[6,16,32896]{2,1,0:T(8,128)(2,1)}), bf16[6,16,32768]{2,1,0:T(8,128)(2,1)S(1)}, s32[]{:S(2)}) %slice-start) | async-done | bytes 6291480 | tf_op jit(solution)/shard_map/vmap()/slice | solution.py:27
  61.2 1.9 %copy.26 = bf16[12,8,128,256]{3,2,1,0:T(8,128)(2,1)S(1)} copy(bf16[12,8,128,256]{3,1,2,0:T(8,128)(2,1)S(1)} %bitcast.196) | data formatting | bytes 12582912
  63.1 2.0 %fusion.19 = f32[6,64,1024]{2,1,0:T(8,128)S(1)} fusion(bf16[64,24,256]{2,0,1:T(8,128)(2,1)S(1)} %copy_dynamic-update-slice_fusion, bf16[6,16,128,256]{3,2,1,0:T(8,128)(2,1)S(1)} %bitcast.188), kind=kOutput, calls=%fused_computation.17 | convolution fusion | flops 402653184 | bytes 7012352 | tf_op jit(solution)/shard_map/cqw,sqrw->scr/dot_general | solution.py:40
  65.1 2.0 %fusion.25 = f32[6,64,1024]{2,1,0:T(8,128)S(1)} fusion(f32[6,64,1024]{2,1,0:T(8,128)S(1)} %fusion.19, bf16[64,24,256]{2,0,1:T(8,128)(2,1)S(1)} %copy_dynamic-update-slice_fusion, bf16[6,16,128,256]{3,2,1,0:T(8,128)(2,1)S(1)} %bitcast.189), kind=kOutput, calls=%fused_computation.19 | convolution fusion | flops 402653184 | bytes 7012352 | tf_op jit(solution)/shard_map/cqw,sqrw->scr/dot_general | solution.py:40
  67.1 2.0 %fusion.31 = f32[6,64,1024]{2,1,0:T(8,128)S(1)} fusion(f32[6,64,1024]{2,1,0:T(8,128)S(1)} %fusion.25, bf16[64,24,256]{2,0,1:T(8,128)(2,1)S(1)} %copy_dynamic-update-slice_fusion, bf16[6,16,128,256]{3,2,1,0:T(8,128)(2,1)S(1)} %bitcast.190), kind=kOutput, calls=%fused_computation.21 | convolution fusion | flops 402653184 | bytes 7012352 | tf_op jit(solution)/shard_map/cqw,sqrw->scr/dot_general | solution.py:40
  69.1 2.0 %fusion.37 = f32[6,64,1024]{2,1,0:T(8,128)S(1)} fusion(f32[6,64,1024]{2,1,0:T(8,128)S(1)} %fusion.31, bf16[64,24,256]{2,0,1:T(8,128)(2,1)S(1)} %copy_dynamic-update-slice_fusion, bf16[6,16,128,256]{3,2,1,0:T(8,128)(2,1)S(1)} %bitcast.191), kind=kOutput, calls=%fused_computation.23 | convolution fusion | flops 402653184 | bytes 7012352 | tf_op jit(solution)/shard_map/cqw,sqrw->scr/dot_general | solution.py:40
  71.1 2.0 %fusion.43 = f32[6,64,1024]{2,1,0:T(8,128)S(1)} fusion(f32[6,64,1024]{2,1,0:T(8,128)S(1)} %fusion.37, bf16[64,24,256]{2,0,1:T(8,128)(2,1)S(1)} %copy_dynamic-update-slice_fusion, bf16[6,16,128,256]{3,2,1,0:T(8,128)(2,1)S(1)} %bitcast.192), kind=kOutput, calls=%fused_computation.25 | convolution fusion | flops 402653184 | bytes 7012352 | tf_op jit(solution)/shard_map/cqw,sqrw->scr/dot_general | solution.py:40
  73.1 2.0 %fusion.49 = f32[6,64,1024]{2,1,0:T(8,128)S(1)} fusion(f32[6,64,1024]{2,1,0:T(8,128)S(1)} %fusion.43, bf16[64,24,256]{2,0,1:T(8,128)(2,1)S(1)} %copy_dynamic-update-slice_fusion, bf16[6,16,128,256]{3,2,1,0:T(8,128)(2,1)S(1)} %bitcast.193), kind=kOutput, calls=%fused_computation.27 | convolution fusion | flops 402653184 | bytes 7012352 | tf_op jit(solution)/shard_map/cqw,sqrw->scr/dot_general | solution.py:40
  75.1 2.0 %fusion.55 = f32[6,64,1024]{2,1,0:T(8,128)S(1)} fusion(f32[6,64,1024]{2,1,0:T(8,128)S(1)} %fusion.49, bf16[64,24,256]{2,0,1:T(8,128)(2,1)S(1)} %copy_dynamic-update-slice_fusion, bf16[6,16,128,256]{3,2,1,0:T(8,128)(2,1)S(1)} %bitcast.194), kind=kOutput, calls=%fused_computation.29 | convolution fusion | flops 402653184 | bytes 7012352 | tf_op jit(solution)/shard_map/cqw,sqrw->scr/dot_general | solution.py:40
  77.1 2.0 %fusion.61 = f32[6,64,1024]{2,1,0:T(8,128)S(1)} fusion(f32[6,64,1024]{2,1,0:T(8,128)S(1)} %fusion.55, bf16[64,24,256]{2,0,1:T(8,128)(2,1)S(1)} %copy_dynamic-update-slice_fusion, bf16[6,16,128,256]{3,2,1,0:T(8,128)(2,1)S(1)} %bitcast.195), kind=kOutput, calls=%fused_computation.31 | convolution fusion | flops 402653184 | bytes 7012352 | tf_op jit(solution)/shard_map/cqw,sqrw->scr/dot_general | solution.py:40
  79.1 1.4 broadcast_multiply_fusion
  80.5 0.0 reduce-scatter.2.cloned.1.call-update
  80.5 0.2 convert_reduce_fusion
  80.7 0.7 all_to_all.14
  81.4 9.6 %all-to-all-start.1 = ((f32[128,4,1]{1,2,0:T(1,128)}), f32[128,4,1]{1,2,0:T(1,128)S(1)}, u32[]{:S(2)}, u32[]{:S(2)}) async-start(f32[128,4,1]{1,2,0:T(1,128)} %bitcast.44), calls=%async_computation.2 | async-start | bytes 131072 | tf_op jit(solution)/shard_map/all_to_all | solution.py:115
  91.0 0.7 bitcast_add_fusion
  91.8 15.7 %reduce-scatter.2.cloned.1.call-done = f32[384,256]{1,0:T(8,128)} async-done(((f32[384,1024]{1,0:T(8,128)}), f32[384,256]{1,0:T(8,128)}) %reduce-scatter.2.cloned.1.call-update) | async-done | bytes 393232 | tf_op jit(solution)/shard_map/reduce_scatter | solution.py:99
  107.5 1.6 %fusion.64 = f32[512,256]{1,0:T(8,128)S(1)} fusion(f32[384,256]{1,0:T(8,128)} %reduce-scatter.2.cloned.1.call-done, s32[384]{0:T(512)S(1)} %pad_add_fusion), kind=kOutput, calls=%fused_computation.36 | convolution fusion | flops 604176384 | bytes 919040 | tf_op jit(solution)/shard_map/dot_general | solution.py:108
  109.1 1.0 all_to_all.12
  110.1 0.0 all-to-all-done.1
  110.1 15.1 %all-to-all-start = ((f32[128,4,256]{2,1,0:T(4,128)}), f32[128,4,256]{2,1,0:T(4,128)S(1)}, u32[]{:S(2)}, u32[]{:S(2)}) async-start(f32[128,4,256]{2,1,0:T(4,128)} %all_to_all.12), calls=%async_computation.1 | async-start | bytes 1048576 | tf_op jit(solution)/shard_map/all_to_all | solution.py:109
  125.2 0.2 reduce_sum.39
  125.3 20.4 %all-to-all-done = f32[128,4,256]{2,1,0:T(4,128)S(1)} async-done(((f32[128,4,256]{2,1,0:T(4,128)}), f32[128,4,256]{2,1,0:T(4,128)S(1)}, u32[]{:S(2)}, u32[]{:S(2)}) %all-to-all-start) | async-done | bytes 524320 | tf_op jit(solution)/shard_map/all_to_all | solution.py:109
  145.7 0.1 reduce_sum.37
  145.9 0.7 broadcast_divide_fusion
  (24 shorter events, 0.3 us)
Async XLA Ops:
  6.5 101.0 %reduce-scatter.2.cloned.1.call-start = ((), (), s32[]{:S(2)}) async-start(), calls=%async_computation.3 | async-start | bytes 1966080 | tf_op jit(solution)/shard_map/reduce_scatter | solution.py:99
  12.3 25.9 %collective-permute-start.22 = (bf16[3,2048]{1,0:T(4,128)(2,1)S(1)}, bf16[3,2048]{1,0:T(4,128)(2,1)S(1)}, u32[]{:S(2)}, u32[]{:S(2)}) collective-permute-start(bf16[3,2048]{1,0:T(4,128)(2,1)S(1)} %get-tuple-element.59), channel_id=1, source_target_pairs={{0,508},{4,504},{8,500},{12,496},{16,492},{20,488},{24,484},{28,48... | collective-permute-start | bytes 36872 | tf_op jit(solution)/shard_map/ppermute | solution.py:70
  29.2 3.1 %collective-permute-start = (bf16[3,2048]{1,0:T(4,128)(2,1)S(1)}, bf16[3,2048]{1,0:T(4,128)(2,1)S(1)}, u32[]{:S(2)}, u32[]{:S(2)}) collective-permute-start(bf16[3,2048]{1,0:T(4,128)(2,1)S(1)} %param.1), channel_id=1, source_target_pairs={{0,4},{4,0},{8,12},{12,8},{16,20},{20,16},{24,28},{28,24},{32,36},... | collective-permute-start | bytes 36872 | tf_op jit(solution)/shard_map/cond/branch_1_fun/ppermute | solution.py:55
  32.4 5.7 %collective-permute-start.21 = (bf16[3,2048]{1,0:T(4,128)(2,1)S(1)}, bf16[3,2048]{1,0:T(4,128)(2,1)S(1)}, u32[]{:S(2)}, u32[]{:S(2)}) collective-permute-start(bf16[3,2048]{1,0:T(4,128)(2,1)S(1)} %param.23), channel_id=1, source_target_pairs={{0,448},{4,452},{8,456},{12,460},{16,464},{20,468},{24,472},{28,47... | collective-permute-start | bytes 36872 | tf_op jit(solution)/shard_map/cond/branch_7_fun/ppermute | solution.py:55
  58.4 2.8 %slice-start = ((bf16[6,16,32896]{2,1,0:T(8,128)(2,1)}), bf16[6,16,32768]{2,1,0:T(8,128)(2,1)S(1)}, s32[]{:S(2)}) async-start(bf16[6,16,32896]{2,1,0:T(8,128)(2,1)} %tile.10), calls=%async_computation.4 | async-start | bytes 12582912 | tf_op jit(solution)/shard_map/vmap()/slice | solution.py:27
  81.4 28.7 %all-to-all-start.1 = ((f32[128,4,1]{1,2,0:T(1,128)}), f32[128,4,1]{1,2,0:T(1,128)S(1)}, u32[]{:S(2)}, u32[]{:S(2)}) async-start(f32[128,4,1]{1,2,0:T(1,128)} %bitcast.44), calls=%async_computation.2 | async-start | bytes 131072 | tf_op jit(solution)/shard_map/all_to_all | solution.py:115
  110.1 35.7 %all-to-all-start = ((f32[128,4,256]{2,1,0:T(4,128)}), f32[128,4,256]{2,1,0:T(4,128)S(1)}, u32[]{:S(2)}, u32[]{:S(2)}) async-start(f32[128,4,256]{2,1,0:T(4,128)} %all_to_all.12), calls=%async_computation.1 | async-start | bytes 1048576 | tf_op jit(solution)/shard_map/all_to_all | solution.py:109
Sparse Core Ops, SparseCore 0:
  80.6 26.8 reduce-scatter.1

commit v3 on v2

--- a/solution.py
+++ b/solution.py
@@ -2,6 +2,8 @@
 import jax.numpy as jnp
 from jax import lax
 from jax.sharding import PartitionSpec as P
+from jax.experimental import pallas as pl
+from jax.experimental.pallas import tpu as pltpu
 
 LAG = 512
 SRC = 2
@@ -18,34 +20,39 @@
     return (data * scale).astype(jnp.bfloat16)
 
 
-def source_toeplitz(source):
-    blocks = source.reshape(-1, block_width)
-    padded = jnp.concatenate(
-        [blocks, jnp.zeros((blocks.shape[0], block_width + 1), blocks.dtype)], axis=1
-    )
-    tiled = jnp.tile(padded, (1, block_width))
-    return tiled[:, : 2 * block_width * block_width].reshape(
-        blocks.shape[0], block_width, 2 * block_width
-    )
+def toeplitz_kernel(src_ref, out_ref):
+    for q in range(out_ref.shape[1]):
+        row = src_ref[0, q : q + 1, :].astype(jnp.float32)
+        row = jnp.concatenate([row, jnp.zeros_like(row)], axis=1)
+        band = jnp.broadcast_to(row, (block_width, 2 * block_width))
+        out_ref[0, q] = pltpu.roll(band, 0, 1, stride=1, stride_axis=0).astype(out_ref.dtype)
 
 
-def correlate(receivers, toeplitz):
+def source_toeplitz(sources):
+    n, samples = sources.shape
+    quota = samples // block_width
+    blocks = sources.reshape(n, quota, block_width)
+    return pl.pallas_call(
+        toeplitz_kernel,
+        grid=(n,),
+        in_specs=[pl.BlockSpec((1, quota, block_width), lambda s: (s, 0, 0))],
+        out_specs=pl.BlockSpec((1, quota, block_width, 2 * block_width), lambda s: (s, 0, 0, 0)),
+        out_shape=jax.ShapeDtypeStruct((n, quota, block_width, 2 * block_width), sources.dtype),
+    )(blocks)
+
+
+def receiver_windows(receivers):
     chans, samples = receivers.shape
     quota = samples // block_width
     lag_blocks = 2 * LAG // block_width
     extended = jnp.pad(receivers, ((0, 0), (LAG, LAG + block_width)))
     cells = extended.reshape(chans, -1, block_width)
     doubled = jnp.concatenate([cells[:, :-1], cells[:, 1:]], axis=-1)
-    parts = [
-        jnp.einsum(
-            "cqw,sqrw->scr",
-            doubled[:, p : p + quota],
-            toeplitz,
-            preferred_element_type=jnp.float32,
-        )
-        for p in range(lag_blocks)
-    ]
-    return jnp.concatenate(parts, axis=-1)
+    return jnp.stack([doubled[:, p : p + quota] for p in range(lag_blocks)], axis=1)
+
+
+def correlate(windows, toeplitz):
+    return jnp.einsum("cpqw,sqrw->scpr", windows, toeplitz, preferred_element_type=jnp.float32)
 
 
 def xor_permute(x, mask, axis, shift, width):
@@ -93,9 +100,13 @@
         label_rows.append(jnp.concatenate([sources, row[None, :]], axis=0))
     payload = jnp.stack(label_rows)
     arrived = exchange(payload, round_masks, "chan")
-    all_sources = jnp.concatenate([sources] + [arrived[r, :SRC] for r in range(ROUNDS)], axis=0)
-    toeplitz = jax.vmap(source_toeplitz)(all_sources)
-    rows = correlate(normed, toeplitz).reshape(-1, 2 * LAG) / jnp.sqrt(jnp.float32(samples))
+    windows = receiver_windows(normed)
+    scale = 1.0 / jnp.sqrt(jnp.float32(samples))
+    own = correlate(windows, source_toeplitz(sources))
+    partners = jnp.concatenate([arrived[r, :SRC] for r in range(ROUNDS)], axis=0)
+    far = correlate(windows, source_toeplitz(partners))
+    rows = jnp.concatenate([own, far], axis=0) * scale
+    rows = rows.reshape(-1, 2 * LAG)
     rows = lax.psum_scatter(rows, "win", scatter_dimension=1, tiled=True)
     owners_total = lax.axis_size("chan")
     nbins = owners_total * BINCAP

time: 154 us -> 140 us (0.909)
  local copies, waits for them, and re-layouts: 28.4 us -> 8.4 us
  matrix products: 17.6 us -> 11.1 us
  Pallas kernels: 0 us -> 6.25 us
  waiting for transfers between devices: 41 us -> 46.7 us
    another operation x2 -> x1, local copies, waits for them, and re-layouts: 20 us -> 0.04 us  [receiver_windows(): jnp.stack([doubled[:, p:p + quota] for p in range(lag_blocks)], axis=1)]
    dot_general x8 -> x2, matrix products: 16 us -> 9.51 us  [correlate(): jnp.einsum('cpqw,sqrw->scpr', windows, toeplitz, preferred_element_type=j...]
    pallas_call x0 -> x2, Pallas kernels: none -> 6.25 us  [source_toeplitz(): pl.pallas_call(toeplitz_kernel, grid=(n,), in_specs=[pl.BlockSpec((1, quo...]
    ppermute x2, waiting for transfers between devices: 4.91 us -> 10.6 us  [moved(): return lambda v: lax.ppermute(v, axis, [(i, i ^ step) for i in range(n)])]
    slice x3 -> x1, local copies, waits for them, and re-layouts: 2.96 us -> 0.17 us  [receiver_windows(): doubled = jnp.concatenate([cells[:, :-1], cells[:, 1:]], axis=-1)]
    ppermute x2, starting transfers between devices: 3.84 us -> 6.35 us  [moved(): return lambda v: lax.ppermute(v, axis, [(i, i ^ step) for i in range(n)])]
    unnamed x7 -> x16, local copies, waits for them, and re-layouts: 2.01 us -> 3.82 us
  transfers between devices with their start and end apart: 6 -> 6, of which waited for: 4 -> 4; matrix products, arithmetic and copies ran while one was open for 2% -> 6% of each run, Pallas kernels for 0% -> 2%
where the time goes in v3:
time: 140 us
  waiting for transfers between devices  46.7 us (33%)
  starting transfers between devices  44.8 us (32%)
  between operations  15.7 us (11%)
  matrix products  11.1 us (8%)
  local copies, waits for them, and re-layouts  8.4 us (6%)
  other arithmetic  6.43 us (5%)
  Pallas kernels  6.25 us (4%)
    all_to_all x1, waiting for transfers between devices, body(): lax.all_to_all(local, 'chan', split_axis=0, concat_axis=0, tiled=True)  20.4 us
    reduce_scatter x1, waiting for transfers between devices, body(): rows = lax.psum_scatter(rows, 'win', scatter_dimension=1, tiled=True)  15.7 us
    all_to_all x1, starting transfers between devices, body(): lax.all_to_all(local, 'chan', split_axis=0, concat_axis=0, tiled=True)  15 us
    ppermute x1, starting transfers between devices, exchange(): fixed = lax.ppermute(fixed, axis, [(i, i ^ full) for i in range(n)])  15 us
    ppermute x2, waiting for transfers between devices, moved(): return lambda v: lax.ppermute(v, axis, [(i, i ^ step) for i in range(n)])  10.6 us
    dot_general x2, matrix products, correlate(): jnp.einsum('cpqw,sqrw->scpr', windows, toeplitz, preferred_element_type=j...  9.51 us
    all_to_all x1, starting transfers between devices, body(): lax.all_to_all(own_counts, 'chan', split_axis=0, concat_axis=0, tiled=True)  8.52 us
    ppermute x2, starting transfers between devices, moved(): return lambda v: lax.ppermute(v, axis, [(i, i ^ step) for i in range(n)])  6.35 us
  transfers between devices with their start and end apart: 6, of which 4 were waited for; matrix products, arithmetic and copies ran while one was open for 6% of the time, Pallas kernels for 2%

profile of v3, /device:TPU:1, one launch (start us, length us, event | category | flops | bytes accessed | tf_op | source)
XLA Modules:
  0.0 139.6 jit_solution(14309586774032051508)
XLA Ops:
  6.5 0.0 reduce-scatter.2.cloned.1.call-start
  6.5 1.1 fusion.17
  7.7 1.1 fusion.28
  8.7 1.3 fusion.40
  10.1 0.8 multiply_reduce_fusion
  10.8 0.8 fusion.38
  12.4 15.0 %collective-permute-start.22 = (bf16[3,2048]{1,0:T(4,128)(2,1)S(1)}, bf16[3,2048]{1,0:T(4,128)(2,1)S(1)}, u32[]{:S(2)}, u32[]{:S(2)}) collective-permute-start(bf16[3,2048]{1,0:T(4,128)(2,1)S(1)} %get-tuple-element.59), channel_id=1, source_target_pairs={{0,508},{4,504},{8,500},{12,496},{16,492},{20,488},{24,484},{28,48... | collective-permute-start | bytes 36872 | tf_op jit(solution)/shard_map/ppermute | solution.py:77
  27.4 0.2 reshape.77
  27.6 0.2 fusion.37
  27.8 0.1 copy_dynamic-update-slice_fusion.1
  27.9 0.1 copy_dynamic-update-slice_fusion
  28.4 0.0 copy-start
  28.5 0.6 copy.35
  29.1 1.3 copy-done
  30.4 2.3 %shard_map.46 = bf16[2,16,128,256]{3,2,1,0:T(8,128)(2,1)} custom-call(bf16[2,16,128]{2,1,0:T(8,128)(2,1)} %bitcast.110), custom_call_target="tpu_custom_call" | custom-call | tf_op jit(solution)/shard_map/pallas_call | solution.py:35
  32.7 4.1 %fusion.11 = f32[2,64,8,128]{3,1,2,0:T(8,128)S(1)} fusion(bf16[64,8,16,256]{3,0,2,1:T(8,128)(2,1)} %copy-done, bf16[2,16,128,256]{3,2,1,0:T(8,128)(2,1)} %shard_map.46), kind=kOutput, calls=%fused_computation.9 | convolution fusion | flops 1073741824 | bytes 6815744 | tf_op jit(solution)/shard_map/cpqw,sqrw->scpr/dot_general | solution.py:55
  38.1 8.5 %conditional.2 = (bf16[3,2048]{1,0:T(4,128)(2,1)S(1)}) conditional(s32[]{:T(128)} %bitcast.6, bf16[3,2048]{1,0:T(4,128)(2,1)S(1)} %get-tuple-element.60, bf16[3,2048]{1,0:T(4,128)(2,1)S(1)} %get-tuple-element.60, bf16[3,2048]{1,0:T(4,128)(2,1)S(1)} %get-tuple-element.60, ...), branch_computations={%region_1.2_spmd, %region_2.3_spmd, %region_3.4_spmd, %region_4.5_... | conditional | bytes 73776 | solution.py:66
  38.2 4.4 %collective-permute-start.7 = (bf16[3,2048]{1,0:T(4,128)(2,1)S(1)}, bf16[3,2048]{1,0:T(4,128)(2,1)S(1)}, u32[]{:S(2)}, u32[]{:S(2)}) collective-permute-start(bf16[3,2048]{1,0:T(4,128)(2,1)S(1)} %param.8), channel_id=1, source_target_pairs={{0,32},{4,36},{8,40},{12,44},{16,48},{20,52},{24,56},{28,60},{32,0... | collective-permute-start | bytes 36872 | tf_op jit(solution)/shard_map/cond/branch_8_fun/ppermute | solution.py:62
  42.6 3.9 %collective-permute-done.7 = bf16[3,2048]{1,0:T(4,128)(2,1)S(1)} collective-permute-done((bf16[3,2048]{1,0:T(4,128)(2,1)S(1)}, bf16[3,2048]{1,0:T(4,128)(2,1)S(1)}, u32[]{:S(2)}, u32[]{:S(2)}) %collective-permute-start.7) | collective-permute-done | bytes 12320 | tf_op jit(solution)/shard_map/cond/branch_8_fun/ppermute | solution.py:62
  46.6 8.6 %conditional.3 = (bf16[3,2048]{1,0:T(4,128)(2,1)S(1)}) conditional(s32[]{:T(128)} %bitcast.5, bf16[3,2048]{1,0:T(4,128)(2,1)S(1)} %get-tuple-element.73, bf16[3,2048]{1,0:T(4,128)(2,1)S(1)} %get-tuple-element.73, bf16[3,2048]{1,0:T(4,128)(2,1)S(1)} %get-tuple-element.73, ...), branch_computations={%region_17.18_spmd, %region_18.19_spmd, %region_19.20_spmd, %regio... | conditional | bytes 73776 | solution.py:66
  46.6 1.9 %collective-permute-start.18 = (bf16[3,2048]{1,0:T(4,128)(2,1)S(1)}, bf16[3,2048]{1,0:T(4,128)(2,1)S(1)}, u32[]{:S(2)}, u32[]{:S(2)}) collective-permute-start(bf16[3,2048]{1,0:T(4,128)(2,1)S(1)} %param.20), channel_id=1, source_target_pairs={{0,256},{4,260},{8,264},{12,268},{16,272},{20,276},{24,280},{28,28... | collective-permute-start | bytes 36872 | tf_op jit(solution)/shard_map/cond/branch_4_fun/ppermute | solution.py:62
  48.6 6.6 %collective-permute-done.18 = bf16[3,2048]{1,0:T(4,128)(2,1)S(1)} collective-permute-done((bf16[3,2048]{1,0:T(4,128)(2,1)S(1)}, bf16[3,2048]{1,0:T(4,128)(2,1)S(1)}, u32[]{:S(2)}, u32[]{:S(2)}) %collective-permute-start.18) | collective-permute-done | bytes 12320 | tf_op jit(solution)/shard_map/cond/branch_4_fun/ppermute | solution.py:62
  55.2 0.0 collective-permute-done.22
  55.3 0.6 pad_maximum_fusion.2.src_ref
  55.9 4.0 %shard_map.47 = bf16[4,16,128,256]{3,2,1,0:T(8,128)(2,1)} custom-call(bf16[4,16,128]{2,1,0:T(8,128)(2,1)} %pad_maximum_fusion.2.src_ref), custom_call_target="tpu_custom_call" | custom-call | tf_op jit(solution)/shard_map/pallas_call | solution.py:35
  59.9 5.4 %fusion.6 = f32[4,64,8,128]{3,1,2,0:T(8,128)S(1)} fusion(bf16[64,8,16,256]{3,0,2,1:T(8,128)(2,1)} %copy-done, bf16[4,16,128,256]{3,2,1,0:T(8,128)(2,1)} %shard_map.47), kind=kOutput, calls=%fused_computation.8 | convolution fusion | flops 2147483648 | bytes 9437184 | tf_op jit(solution)/shard_map/cpqw,sqrw->scpr/dot_general | solution.py:55
  65.3 0.2 maximum_multiply_fusion
  65.4 0.9 copy.14
  66.3 1.5 %copy.32 = f32[48,8,8,128]{3,1,2,0:T(8,128)} copy(f32[48,8,8,128]{3,2,1,0:T(8,128)S(1)} %bitcast.108) | data formatting | bytes 3145728
  67.8 0.0 reduce-scatter.2.cloned.1.call-update
  67.9 0.2 convert_reduce_fusion
  68.0 0.7 all_to_all.14
  68.7 8.5 %all-to-all-start.1 = ((f32[128,4,1]{1,2,0:T(1,128)}), f32[128,4,1]{1,2,0:T(1,128)S(1)}, u32[]{:S(2)}, u32[]{:S(2)}) async-start(f32[128,4,1]{1,2,0:T(1,128)} %bitcast.30), calls=%async_computation.2 | async-start | bytes 131072 | tf_op jit(solution)/shard_map/all_to_all | solution.py:126
  77.3 0.7 bitcast_add_fusion
  78.1 15.7 %reduce-scatter.2.cloned.1.call-done = f32[384,256]{1,0:T(8,128)} async-done(((f32[384,1024]{1,0:T(8,128)}), f32[384,256]{1,0:T(8,128)}) %reduce-scatter.2.cloned.1.call-update) | async-done | bytes 393232 | tf_op jit(solution)/shard_map/reduce_scatter | solution.py:110
  93.8 1.6 %fusion.16 = f32[512,256]{1,0:T(8,128)S(1)} fusion(f32[384,256]{1,0:T(8,128)} %reduce-scatter.2.cloned.1.call-done, s32[384]{0:T(512)S(1)} %pad_add_fusion), kind=kOutput, calls=%fused_computation.13 | convolution fusion | flops 604176384 | bytes 919040 | tf_op jit(solution)/shard_map/dot_general | solution.py:119
  95.4 1.0 all_to_all.12
  96.4 0.0 all-to-all-done.1
  96.4 15.0 %all-to-all-start = ((f32[128,4,256]{2,1,0:T(4,128)}), f32[128,4,256]{2,1,0:T(4,128)S(1)}, u32[]{:S(2)}, u32[]{:S(2)}) async-start(f32[128,4,256]{2,1,0:T(4,128)} %all_to_all.12), calls=%async_computation.1 | async-start | bytes 1048576 | tf_op jit(solution)/shard_map/all_to_all | solution.py:120
  111.4 0.2 reduce_sum.39
  111.5 20.4 %all-to-all-done = f32[128,4,256]{2,1,0:T(4,128)S(1)} async-done(((f32[128,4,256]{2,1,0:T(4,128)}), f32[128,4,256]{2,1,0:T(4,128)S(1)}, u32[]{:S(2)}, u32[]{:S(2)}) %all-to-all-start) | async-done | bytes 524320 | tf_op jit(solution)/shard_map/all_to_all | solution.py:120
  131.9 0.1 reduce_sum.37
  132.1 0.7 broadcast_divide_fusion
  (30 shorter events, 0.6 us)
Async XLA Ops:
  6.5 87.3 %reduce-scatter.2.cloned.1.call-start = ((), (), s32[]{:S(2)}) async-start(), calls=%async_computation.3 | async-start | bytes 1966080 | tf_op jit(solution)/shard_map/reduce_scatter | solution.py:110
  12.4 42.8 %collective-permute-start.22 = (bf16[3,2048]{1,0:T(4,128)(2,1)S(1)}, bf16[3,2048]{1,0:T(4,128)(2,1)S(1)}, u32[]{:S(2)}, u32[]{:S(2)}) collective-permute-start(bf16[3,2048]{1,0:T(4,128)(2,1)S(1)} %get-tuple-element.59), channel_id=1, source_target_pairs={{0,508},{4,504},{8,500},{12,496},{16,492},{20,488},{24,484},{28,48... | collective-permute-start | bytes 36872 | tf_op jit(solution)/shard_map/ppermute | solution.py:77
  28.4 1.9 %copy-start = (bf16[64,8,16,256]{3,0,2,1:T(8,128)(2,1)}, bf16[64,8,16,256]{3,0,2,1:T(8,128)(2,1)S(1)}, u32[]{:S(2)}) copy-start(bf16[64,8,16,256]{3,0,2,1:T(8,128)(2,1)S(1)} %fusion.19) | copy-start | bytes 12582916
  38.2 8.4 %collective-permute-start.7 = (bf16[3,2048]{1,0:T(4,128)(2,1)S(1)}, bf16[3,2048]{1,0:T(4,128)(2,1)S(1)}, u32[]{:S(2)}, u32[]{:S(2)}) collective-permute-start(bf16[3,2048]{1,0:T(4,128)(2,1)S(1)} %param.8), channel_id=1, source_target_pairs={{0,32},{4,36},{8,40},{12,44},{16,48},{20,52},{24,56},{28,60},{32,0... | collective-permute-start | bytes 36872 | tf_op jit(solution)/shard_map/cond/branch_8_fun/ppermute | solution.py:62
  46.6 8.5 %collective-permute-start.18 = (bf16[3,2048]{1,0:T(4,128)(2,1)S(1)}, bf16[3,2048]{1,0:T(4,128)(2,1)S(1)}, u32[]{:S(2)}, u32[]{:S(2)}) collective-permute-start(bf16[3,2048]{1,0:T(4,128)(2,1)S(1)} %param.20), channel_id=1, source_target_pairs={{0,256},{4,260},{8,264},{12,268},{16,272},{20,276},{24,280},{28,28... | collective-permute-start | bytes 36872 | tf_op jit(solution)/shard_map/cond/branch_4_fun/ppermute | solution.py:62
  68.7 27.6 %all-to-all-start.1 = ((f32[128,4,1]{1,2,0:T(1,128)}), f32[128,4,1]{1,2,0:T(1,128)S(1)}, u32[]{:S(2)}, u32[]{:S(2)}) async-start(f32[128,4,1]{1,2,0:T(1,128)} %bitcast.30), calls=%async_computation.2 | async-start | bytes 131072 | tf_op jit(solution)/shard_map/all_to_all | solution.py:126
  96.4 35.6 %all-to-all-start = ((f32[128,4,256]{2,1,0:T(4,128)}), f32[128,4,256]{2,1,0:T(4,128)S(1)}, u32[]{:S(2)}, u32[]{:S(2)}) async-start(f32[128,4,256]{2,1,0:T(4,128)} %all_to_all.12), calls=%async_computation.1 | async-start | bytes 1048576 | tf_op jit(solution)/shard_map/all_to_all | solution.py:120
Sparse Core Ops, SparseCore 0:
  68.0 25.7 reduce-scatter.1

commit v4 on v3

--- a/solution.py
+++ b/solution.py
@@ -102,12 +102,12 @@
     arrived = exchange(payload, round_masks, "chan")
     windows = receiver_windows(normed)
     scale = 1.0 / jnp.sqrt(jnp.float32(samples))
-    own = correlate(windows, source_toeplitz(sources))
+    own_band = source_toeplitz(sources)
+    chunks = 2
+    chunk_windows = [windows[:, h::chunks] for h in range(chunks)]
+    own = [correlate(w, own_band) for w in chunk_windows]
     partners = jnp.concatenate([arrived[r, :SRC] for r in range(ROUNDS)], axis=0)
-    far = correlate(windows, source_toeplitz(partners))
-    rows = jnp.concatenate([own, far], axis=0) * scale
-    rows = rows.reshape(-1, 2 * LAG)
-    rows = lax.psum_scatter(rows, "win", scatter_dimension=1, tiled=True)
+    far_band = source_toeplitz(partners)
     owners_total = lax.axis_size("chan")
     nbins = owners_total * BINCAP
     bins_parts = [owner[:rows_set] * BINCAP + slot[:rows_set]]
@@ -116,9 +116,18 @@
         bins_parts.append(got[:rows_set] * BINCAP + got[rows_set : 2 * rows_set])
     bins = jnp.concatenate(bins_parts)
     picks = (bins[None, :] == jnp.arange(nbins, dtype=jnp.int32)[:, None]).astype(jnp.float32)
-    local = jnp.dot(picks, rows, precision=lax.Precision.HIGHEST, preferred_element_type=jnp.float32)
-    arrived_sums = lax.all_to_all(local, "chan", split_axis=0, concat_axis=0, tiled=True)
-    sums = jnp.sum(arrived_sums.reshape(owners_total, BINCAP, -1), axis=0)
+    reduced = []
+    for h in range(chunks):
+        far = correlate(chunk_windows[h], far_band)
+        rows = jnp.concatenate([own[h], far], axis=0) * scale
+        rows = rows.reshape(-1, rows.shape[2] * rows.shape[3])
+        reduced.append(lax.psum_scatter(rows, "win", scatter_dimension=1, tiled=True))
+    parts = []
+    for h in range(chunks):
+        local = jnp.dot(picks, reduced[h], precision=lax.Precision.HIGHEST, preferred_element_type=jnp.float32)
+        arrived_sums = lax.all_to_all(local, "chan", split_axis=0, concat_axis=0, tiled=True)
+        parts.append(jnp.sum(arrived_sums.reshape(owners_total, BINCAP, -1), axis=0))
+    sums = jnp.concatenate(parts, axis=1)
     own_bins = owner * BINCAP + slot
     own_counts = jnp.sum(
         (own_bins[None, :] == jnp.arange(nbins, dtype=jnp.int32)[:, None]).astype(jnp.float32), axis=1

time: 140 us -> 155 us (1.11)
  starting transfers between devices: 44.8 us -> 60.8 us
  waiting for transfers between devices: 46.7 us -> 39.6 us
  matrix products: 11.1 us -> 16.7 us
    all_to_all x1 -> x2, starting transfers between devices: 15 us -> 31.5 us  [body(): lax.all_to_all(local, 'chan', split_axis=0, concat_axis=0, tiled=True)]
    all_to_all x1 -> x2, waiting for transfers between devices: 20.4 us -> 15.6 us  [body(): lax.all_to_all(local, 'chan', split_axis=0, concat_axis=0, tiled=True)]
    ppermute x2, waiting for transfers between devices: 10.6 us -> 7.23 us  [moved(): return lambda v: lax.ppermute(v, axis, [(i, i ^ step) for i in range(n)])]
    dot_general x2 -> x4, matrix products: 9.51 us -> 12.5 us  [correlate(): jnp.einsum('cpqw,sqrw->scpr', windows, toeplitz, preferred_element_type=j...]
    dot_general x1 -> x2, matrix products: 1.61 us -> 4.21 us  [body(): jnp.dot(picks, reduced[h], precision=lax.Precision.HIGHEST, preferred_ele...]
    reduce_scatter x1 -> x2, waiting for transfers between devices: 15.7 us -> 16.7 us  [body(): lax.psum_scatter(rows, 'win', scatter_dimension=1, tiled=True)]
    unnamed x16 -> x21, local copies, waits for them, and re-layouts: 3.82 us -> 4.22 us
  transfers between devices with their start and end apart: 6 -> 8, of which waited for: 4 -> 6; matrix products, arithmetic and copies ran while one was open for 6% -> 11% of each run, Pallas kernels for 2% -> 2%
where the time goes in v4:
time: 155 us; the launch traced here: 154 us
  starting transfers between devices  60.8 us (39%)
  waiting for transfers between devices  39.6 us (26%)
  matrix products  16.7 us (11%)
  between operations  15.7 us (10%)
  local copies, waits for them, and re-layouts  7.96 us (5%)
  other arithmetic  6.72 us (4%)
  Pallas kernels  6.34 us (4%)
    all_to_all x2, starting transfers between devices, body(): lax.all_to_all(local, 'chan', split_axis=0, concat_axis=0, tiled=True)  31.5 us
    reduce_scatter x2, waiting for transfers between devices, body(): lax.psum_scatter(rows, 'win', scatter_dimension=1, tiled=True)  16.7 us
    all_to_all x2, waiting for transfers between devices, body(): lax.all_to_all(local, 'chan', split_axis=0, concat_axis=0, tiled=True)  15.6 us
    ppermute x1, starting transfers between devices, exchange(): fixed = lax.ppermute(fixed, axis, [(i, i ^ full) for i in range(n)])  15 us
    dot_general x4, matrix products, correlate(): jnp.einsum('cpqw,sqrw->scpr', windows, toeplitz, preferred_element_type=j...  12.5 us
    all_to_all x1, starting transfers between devices, body(): lax.all_to_all(own_counts, 'chan', split_axis=0, concat_axis=0, tiled=True)  7.72 us
    ppermute x2, waiting for transfers between devices, moved(): return lambda v: lax.ppermute(v, axis, [(i, i ^ step) for i in range(n)])  7.23 us
    ppermute x2, starting transfers between devices, moved(): return lambda v: lax.ppermute(v, axis, [(i, i ^ step) for i in range(n)])  6.58 us
  transfers between devices with their start and end apart: 8, of which 6 were waited for; matrix products, arithmetic and copies ran while one was open for 11% of the time, Pallas kernels for 2%

profile of v4, /device:TPU:1, one launch (start us, length us, event | category | flops | bytes accessed | tf_op | source)
XLA Modules:
  0.0 153.9 jit_solution(9004881024095909503)
XLA Ops:
  6.5 0.0 reduce-scatter.5.cloned.1.call-start
  6.5 1.1 fusion.38
  7.7 1.1 fusion.50
  8.7 1.3 fusion.62
  10.0 0.8 multiply_reduce_fusion
  10.8 0.8 fusion.60
  12.4 15.0 %collective-permute-start.22 = (bf16[3,2048]{1,0:T(4,128)(2,1)S(1)}, bf16[3,2048]{1,0:T(4,128)(2,1)S(1)}, u32[]{:S(2)}, u32[]{:S(2)}) collective-permute-start(bf16[3,2048]{1,0:T(4,128)(2,1)S(1)} %get-tuple-element.59), channel_id=1, source_target_pairs={{0,508},{4,504},{8,500},{12,496},{16,492},{20,488},{24,484},{28,48... | collective-permute-start | bytes 36872 | tf_op jit(solution)/shard_map/ppermute | solution.py:77
  27.4 0.2 reshape.85
  27.6 0.2 fusion.59
  27.8 0.1 copy_dynamic-update-slice_fusion.1
  27.8 0.1 copy_dynamic-update-slice_fusion
  28.4 0.0 copy-start.2
  28.4 0.6 copy.43
  29.0 1.3 copy-done.2
  30.3 2.4 %shard_map.46 = bf16[2,16,128,256]{3,2,1,0:T(8,128)(2,1)} custom-call(bf16[2,16,128]{2,1,0:T(8,128)(2,1)} %bitcast.147), custom_call_target="tpu_custom_call" | custom-call | tf_op jit(solution)/shard_map/pallas_call | solution.py:35
  32.7 3.0 %fusion.31 = f32[2,64,4,128]{3,1,2,0:T(8,128)S(1)} fusion(bf16[64,8,16,256]{3,0,2,1:T(8,128)(2,1)} %copy-done.2, bf16[2,16,128,256]{3,2,1,0:T(8,128)(2,1)} %shard_map.46), kind=kOutput, calls=%fused_computation.19 | convolution fusion | flops 536870912 | bytes 4456448 | tf_op jit(solution)/shard_map/cpqw,sqrw->scpr/dot_general | solution.py:55
  37.0 6.3 %conditional.2 = (bf16[3,2048]{1,0:T(4,128)(2,1)S(1)}) conditional(s32[]{:T(128)} %bitcast.6, bf16[3,2048]{1,0:T(4,128)(2,1)S(1)} %get-tuple-element.60, bf16[3,2048]{1,0:T(4,128)(2,1)S(1)} %get-tuple-element.60, bf16[3,2048]{1,0:T(4,128)(2,1)S(1)} %get-tuple-element.60, ...), branch_computations={%region_1.2_spmd, %region_2.3_spmd, %region_3.4_spmd, %region_4.5_... | conditional | bytes 73776 | solution.py:66
  37.0 4.7 %collective-permute-start.3 = (bf16[3,2048]{1,0:T(4,128)(2,1)S(1)}, bf16[3,2048]{1,0:T(4,128)(2,1)S(1)}, u32[]{:S(2)}, u32[]{:S(2)}) collective-permute-start(bf16[3,2048]{1,0:T(4,128)(2,1)S(1)} %param.4), channel_id=1, source_target_pairs={{0,16},{4,20},{8,24},{12,28},{16,0},{20,4},{24,8},{28,12},{32,48},... | collective-permute-start | bytes 36872 | tf_op jit(solution)/shard_map/cond/branch_4_fun/ppermute | solution.py:62
  41.7 1.6 %collective-permute-done.3 = bf16[3,2048]{1,0:T(4,128)(2,1)S(1)} collective-permute-done((bf16[3,2048]{1,0:T(4,128)(2,1)S(1)}, bf16[3,2048]{1,0:T(4,128)(2,1)S(1)}, u32[]{:S(2)}, u32[]{:S(2)}) %collective-permute-start.3) | collective-permute-done | bytes 12320 | tf_op jit(solution)/shard_map/cond/branch_4_fun/ppermute | solution.py:62
  43.3 7.6 %conditional.3 = (bf16[3,2048]{1,0:T(4,128)(2,1)S(1)}) conditional(s32[]{:T(128)} %bitcast.5, bf16[3,2048]{1,0:T(4,128)(2,1)S(1)} %get-tuple-element.73, bf16[3,2048]{1,0:T(4,128)(2,1)S(1)} %get-tuple-element.73, bf16[3,2048]{1,0:T(4,128)(2,1)S(1)} %get-tuple-element.73, ...), branch_computations={%region_17.18_spmd, %region_18.19_spmd, %region_19.20_spmd, %regio... | conditional | bytes 73776 | solution.py:66
  43.3 1.9 %collective-permute-start.19 = (bf16[3,2048]{1,0:T(4,128)(2,1)S(1)}, bf16[3,2048]{1,0:T(4,128)(2,1)S(1)}, u32[]{:S(2)}, u32[]{:S(2)}) collective-permute-start(bf16[3,2048]{1,0:T(4,128)(2,1)S(1)} %param.21), channel_id=1, source_target_pairs={{0,320},{4,324},{8,328},{12,332},{16,336},{20,340},{24,344},{28,34... | collective-permute-start | bytes 36872 | tf_op jit(solution)/shard_map/cond/branch_5_fun/ppermute | solution.py:62
  45.2 5.7 %collective-permute-done.19 = bf16[3,2048]{1,0:T(4,128)(2,1)S(1)} collective-permute-done((bf16[3,2048]{1,0:T(4,128)(2,1)S(1)}, bf16[3,2048]{1,0:T(4,128)(2,1)S(1)}, u32[]{:S(2)}, u32[]{:S(2)}) %collective-permute-start.19) | collective-permute-done | bytes 12320 | tf_op jit(solution)/shard_map/cond/branch_5_fun/ppermute | solution.py:62
  50.9 0.0 collective-permute-done.22
  51.0 0.6 pad_maximum_fusion.2.src_ref
  51.6 4.0 %shard_map.47 = bf16[4,16,128,256]{3,2,1,0:T(8,128)(2,1)} custom-call(bf16[4,16,128]{2,1,0:T(8,128)(2,1)} %pad_maximum_fusion.2.src_ref), custom_call_target="tpu_custom_call" | custom-call | tf_op jit(solution)/shard_map/pallas_call | solution.py:35
  55.6 4.1 %fusion.21 = f32[4,64,4,128]{3,1,2,0:T(8,128)S(1)} fusion(bf16[64,8,16,256]{3,0,2,1:T(8,128)(2,1)} %copy-done.2, bf16[4,16,128,256]{3,2,1,0:T(8,128)(2,1)} %shard_map.47), kind=kOutput, calls=%fused_computation.17 | convolution fusion | flops 1073741824 | bytes 6815744 | tf_op jit(solution)/shard_map/cpqw,sqrw->scpr/dot_general | solution.py:55
  59.7 0.0 copy-start.1
  59.7 0.1 maximum_multiply_fusion.1
  59.8 0.5 copy.17
  60.3 0.9 copy.39
  61.3 0.0 reduce-scatter.5.cloned.1.call-update
  61.3 0.2 convert_reduce_fusion
  61.5 0.7 all_to_all.22
  62.2 7.7 %all-to-all-start.2 = ((f32[128,4,1]{1,2,0:T(1,128)}), f32[128,4,1]{1,2,0:T(1,128)S(1)}, u32[]{:S(2)}, u32[]{:S(2)}) async-start(f32[128,4,1]{1,2,0:T(1,128)} %bitcast.41), calls=%async_computation.4 | async-start | bytes 131072 | tf_op jit(solution)/shard_map/all_to_all | solution.py:135
  69.9 0.0 reduce-scatter.3.cloned.1.call-start
  70.0 0.0 copy-start
  70.0 0.8 bitcast_add_fusion
  70.8 0.0 copy-done.1
  70.8 2.6 %fusion.26 = f32[2,64,4,128]{3,1,2,0:T(8,128)S(1)} fusion(bf16[64,8,16,256]{3,0,2,1:T(8,128)(2,1)} %copy-done.2, bf16[2,16,128,256]{3,2,1,0:T(8,128)(2,1)S(1)} %copy-done.1), kind=kOutput, calls=%fused_computation.18 | convolution fusion | flops 536870912 | bytes 4456448 | tf_op jit(solution)/shard_map/cpqw,sqrw->scpr/dot_general | solution.py:55
  73.4 0.0 copy-done
  73.4 2.9 %fusion.16 = f32[4,64,4,128]{3,1,2,0:T(8,128)S(1)} fusion(bf16[64,8,16,256]{3,0,2,1:T(8,128)(2,1)} %copy-done.2, bf16[4,16,128,256]{3,2,1,0:T(8,128)(2,1)S(1)} %copy-done), kind=kOutput, calls=%fused_computation.16 | convolution fusion | flops 1073741824 | bytes 6815744 | tf_op jit(solution)/shard_map/cpqw,sqrw->scpr/dot_general | solution.py:55
  76.3 0.1 maximum_multiply_fusion
  76.4 0.5 copy.16
  76.9 0.9 copy.40
  77.8 0.0 reduce-scatter.3.cloned.1.call-update
  77.9 4.3 %reduce-scatter.5.cloned.1.call-done = f32[384,128]{1,0:T(8,128)} async-done(((f32[384,512]{1,0:T(8,128)}), f32[384,128]{1,0:T(8,128)}) %reduce-scatter.5.cloned.1.call-update) | async-done | bytes 196624 | tf_op jit(solution)/shard_map/reduce_scatter | solution.py:124
  82.2 2.1 %fusion.36 = f32[512,128]{1,0:T(8,128)} fusion(f32[384,128]{1,0:T(8,128)} %reduce-scatter.5.cloned.1.call-done, s32[384]{0:T(512)S(1)} %pad_add_fusion), kind=kOutput, calls=%fused_computation.27 | convolution fusion | flops 302186496 | bytes 460288 | tf_op jit(solution)/shard_map/dot_general | solution.py:127
  84.3 0.0 all-to-all-done.2
  84.3 16.2 %all-to-all-start.1 = ((f32[128,4,128]{2,1,0:T(4,128)}), f32[128,4,128]{2,1,0:T(4,128)S(1)}, u32[]{:S(2)}, u32[]{:S(2)}) async-start(f32[128,4,128]{2,1,0:T(4,128)} %bitcast.40), calls=%async_computation.3 | async-start | bytes 524288 | tf_op jit(solution)/shard_map/all_to_all | solution.py:128
  100.5 12.4 %reduce-scatter.3.cloned.1.call-done = f32[384,128]{1,0:T(8,128)} async-done(((f32[384,512]{1,0:T(8,128)}), f32[384,128]{1,0:T(8,128)}) %reduce-scatter.3.cloned.1.call-update) | async-done | bytes 196624 | tf_op jit(solution)/shard_map/reduce_scatter | solution.py:124
  112.9 2.1 %fusion.37 = f32[512,128]{1,0:T(8,128)} fusion(f32[384,128]{1,0:T(8,128)} %reduce-scatter.3.cloned.1.call-done, s32[384]{0:T(512)S(1)} %pad_add_fusion), kind=kOutput, calls=%fused_computation.28 | convolution fusion | flops 302186496 | bytes 460288 | tf_op jit(solution)/shard_map/dot_general | solution.py:127
  115.0 0.7 all-to-all-done.1
  115.7 15.3 %all-to-all-start = ((f32[128,4,128]{2,1,0:T(4,128)}), f32[128,4,128]{2,1,0:T(4,128)S(1)}, u32[]{:S(2)}, u32[]{:S(2)}) async-start(f32[128,4,128]{2,1,0:T(4,128)} %bitcast.30), calls=%async_computation.1 | async-start | bytes 524288 | tf_op jit(solution)/shard_map/all_to_all | solution.py:128
  131.0 0.2 reduce_sum.49
  131.2 0.1 reduce_sum.47
  131.3 14.9 %all-to-all-done = f32[128,4,128]{2,1,0:T(4,128)S(1)} async-done(((f32[128,4,128]{2,1,0:T(4,128)}), f32[128,4,128]{2,1,0:T(4,128)S(1)}, u32[]{:S(2)}, u32[]{:S(2)}) %all-to-all-start) | async-done | bytes 262176 | tf_op jit(solution)/shard_map/all_to_all | solution.py:128
  146.3 0.1 reduce_sum.46
  146.4 0.7 maximum_divide_fusion
  (30 shorter events, 0.6 us)
Async XLA Ops:
  6.5 75.6 %reduce-scatter.5.cloned.1.call-start = ((), (), s32[]{:S(2)}) async-start(), calls=%async_computation.6 | async-start | bytes 983040 | tf_op jit(solution)/shard_map/reduce_scatter | solution.py:124
  12.4 38.5 %collective-permute-start.22 = (bf16[3,2048]{1,0:T(4,128)(2,1)S(1)}, bf16[3,2048]{1,0:T(4,128)(2,1)S(1)}, u32[]{:S(2)}, u32[]{:S(2)}) collective-permute-start(bf16[3,2048]{1,0:T(4,128)(2,1)S(1)} %get-tuple-element.59), channel_id=1, source_target_pairs={{0,508},{4,504},{8,500},{12,496},{16,492},{20,488},{24,484},{28,48... | collective-permute-start | bytes 36872 | tf_op jit(solution)/shard_map/ppermute | solution.py:77
  28.4 1.9 %copy-start.2 = (bf16[64,8,16,256]{3,0,2,1:T(8,128)(2,1)}, bf16[64,8,16,256]{3,0,2,1:T(8,128)(2,1)S(1)}, u32[]{:S(2)}) copy-start(bf16[64,8,16,256]{3,0,2,1:T(8,128)(2,1)S(1)} %fusion.40) | copy-start | bytes 12582916
  37.0 6.2 %collective-permute-start.3 = (bf16[3,2048]{1,0:T(4,128)(2,1)S(1)}, bf16[3,2048]{1,0:T(4,128)(2,1)S(1)}, u32[]{:S(2)}, u32[]{:S(2)}) collective-permute-start(bf16[3,2048]{1,0:T(4,128)(2,1)S(1)} %param.4), channel_id=1, source_target_pairs={{0,16},{4,20},{8,24},{12,28},{16,0},{20,4},{24,8},{28,12},{32,48},... | collective-permute-start | bytes 36872 | tf_op jit(solution)/shard_map/cond/branch_4_fun/ppermute | solution.py:62
  43.3 7.6 %collective-permute-start.19 = (bf16[3,2048]{1,0:T(4,128)(2,1)S(1)}, bf16[3,2048]{1,0:T(4,128)(2,1)S(1)}, u32[]{:S(2)}, u32[]{:S(2)}) collective-permute-start(bf16[3,2048]{1,0:T(4,128)(2,1)S(1)} %param.21), channel_id=1, source_target_pairs={{0,320},{4,324},{8,328},{12,332},{16,336},{20,340},{24,344},{28,34... | collective-permute-start | bytes 36872 | tf_op jit(solution)/shard_map/cond/branch_5_fun/ppermute | solution.py:62
  59.7 11.1 %copy-start.1 = (bf16[2,16,128,256]{3,2,1,0:T(8,128)(2,1)S(1)}, bf16[2,16,128,256]{3,2,1,0:T(8,128)(2,1)}, u32[]{:S(2)}) copy-start(bf16[2,16,128,256]{3,2,1,0:T(8,128)(2,1)} %shard_map.46) | copy-start | bytes 6291460
  62.2 22.1 %all-to-all-start.2 = ((f32[128,4,1]{1,2,0:T(1,128)}), f32[128,4,1]{1,2,0:T(1,128)S(1)}, u32[]{:S(2)}, u32[]{:S(2)}) async-start(f32[128,4,1]{1,2,0:T(1,128)} %bitcast.41), calls=%async_computation.4 | async-start | bytes 131072 | tf_op jit(solution)/shard_map/all_to_all | solution.py:135
  69.9 43.0 %reduce-scatter.3.cloned.1.call-start = ((), (), s32[]{:S(2)}) async-start(), calls=%async_computation.5 | async-start | bytes 983040 | tf_op jit(solution)/shard_map/reduce_scatter | solution.py:124
  70.0 3.4 %copy-start = (bf16[4,16,128,256]{3,2,1,0:T(8,128)(2,1)S(1)}, bf16[4,16,128,256]{3,2,1,0:T(8,128)(2,1)}, u32[]{:S(2)}) copy-start(bf16[4,16,128,256]{3,2,1,0:T(8,128)(2,1)} %shard_map.47) | copy-start | bytes 12582916
  84.3 31.4 %all-to-all-start.1 = ((f32[128,4,128]{2,1,0:T(4,128)}), f32[128,4,128]{2,1,0:T(4,128)S(1)}, u32[]{:S(2)}, u32[]{:S(2)}) async-start(f32[128,4,128]{2,1,0:T(4,128)} %bitcast.40), calls=%async_computation.3 | async-start | bytes 524288 | tf_op jit(solution)/shard_map/all_to_all | solution.py:128
  115.7 30.5 %all-to-all-start = ((f32[128,4,128]{2,1,0:T(4,128)}), f32[128,4,128]{2,1,0:T(4,128)S(1)}, u32[]{:S(2)}, u32[]{:S(2)}) async-start(f32[128,4,128]{2,1,0:T(4,128)} %bitcast.30), calls=%async_computation.1 | async-start | bytes 524288 | tf_op jit(solution)/shard_map/all_to_all | solution.py:128
Sparse Core Ops, SparseCore 0:
  61.4 20.7 reduce-scatter.4
  85.0 27.8 reduce-scatter.2

commit v5 on v3

--- a/solution.py
+++ b/solution.py
@@ -117,14 +117,19 @@
     bins = jnp.concatenate(bins_parts)
     picks = (bins[None, :] == jnp.arange(nbins, dtype=jnp.int32)[:, None]).astype(jnp.float32)
     local = jnp.dot(picks, rows, precision=lax.Precision.HIGHEST, preferred_element_type=jnp.float32)
-    arrived_sums = lax.all_to_all(local, "chan", split_axis=0, concat_axis=0, tiled=True)
-    sums = jnp.sum(arrived_sums.reshape(owners_total, BINCAP, -1), axis=0)
+    local = local.reshape(owners_total, BINCAP, -1)
     own_bins = owner * BINCAP + slot
     own_counts = jnp.sum(
         (own_bins[None, :] == jnp.arange(nbins, dtype=jnp.int32)[:, None]).astype(jnp.float32), axis=1
     )
-    arrived_counts = lax.all_to_all(own_counts, "chan", split_axis=0, concat_axis=0, tiled=True)
-    counts = jnp.sum(arrived_counts.reshape(owners_total, BINCAP), axis=0)
+    count_row = jnp.pad(
+        own_counts.reshape(owners_total, 1, BINCAP), ((0, 0), (0, 0), (0, local.shape[2] - BINCAP))
+    )
+    outgoing = jnp.concatenate([local, count_row], axis=1)
+    arrived_sums = lax.all_to_all(outgoing, "chan", split_axis=0, concat_axis=0, tiled=True)
+    arrived_sums = jnp.sum(arrived_sums, axis=0)
+    sums = arrived_sums[:BINCAP]
+    counts = arrived_sums[BINCAP, :BINCAP]
     return sums / jnp.sqrt(jnp.maximum(counts, 1.0))[:, None]
 
 

time: 140 us -> 149 us (1.064)
  blocking collectives: 0 us -> 45.9 us
  starting transfers between devices: 44.8 us -> 21.3 us
  waiting for transfers between devices: 46.7 us -> 34.5 us
    all_to_all x0 -> x1, blocking collectives: none -> 45.9 us  [body(): lax.all_to_all(outgoing, 'chan', split_axis=0, concat_axis=0, tiled=True)]
    all_to_all x2 -> x0, starting transfers between devices: 23.5 us -> none  [the longest x1 15 us: body(): lax.all_to_all(local, 'chan', split_axis=0, concat_axis=0, tiled=True)]
    all_to_all x2 -> x0, waiting for transfers between devices: 20.4 us -> none  [the longest x1 20.4 us: body(): lax.all_to_all(local, 'chan', split_axis=0, concat_axis=0, tiled=True)]
    reduce_scatter x1, waiting for transfers between devices: 15.7 us -> 26.7 us  [body(): rows = lax.psum_scatter(rows, 'win', scatter_dimension=1, tiled=True)]
    ppermute x2, waiting for transfers between devices: 10.6 us -> 7.71 us  [moved(): return lambda v: lax.ppermute(v, axis, [(i, i ^ step) for i in range(n)])]
    all_to_all x2 -> x0, local copies, waits for them, and re-layouts: 1.68 us -> none  [the longest x1 0.96 us: body(): lax.all_to_all(local, 'chan', split_axis=0, concat_axis=0, tiled=True)]
    another operation x0 -> x2, other arithmetic: none -> 1.53 us
  transfers between devices with their start and end apart: 6 -> 4, of which waited for: 4 -> 3; matrix products, arithmetic and copies ran while one was open for 6% -> 5% of each run, Pallas kernels for 2% -> 2%
where the time goes in v5:
time: 149 us; the launch traced here: 148 us
  blocking collectives  45.9 us (31%)
  waiting for transfers between devices  34.5 us (23%)
  starting transfers between devices  21.3 us (14%)
  between operations  15.6 us (10%)
  matrix products  11.1 us (7%)
  local copies, waits for them, and re-layouts  6.96 us (5%)
  other arithmetic  6.45 us (4%)
  Pallas kernels  6.24 us (4%)
    all_to_all x1, blocking collectives, body(): lax.all_to_all(outgoing, 'chan', split_axis=0, concat_axis=0, tiled=True)  45.9 us
    reduce_scatter x1, waiting for transfers between devices, body(): rows = lax.psum_scatter(rows, 'win', scatter_dimension=1, tiled=True)  26.7 us
    ppermute x1, starting transfers between devices, exchange(): fixed = lax.ppermute(fixed, axis, [(i, i ^ full) for i in range(n)])  15 us
    dot_general x2, matrix products, correlate(): jnp.einsum('cpqw,sqrw->scpr', windows, toeplitz, preferred_element_type=j...  9.51 us
    ppermute x2, waiting for transfers between devices, moved(): return lambda v: lax.ppermute(v, axis, [(i, i ^ step) for i in range(n)])  7.71 us
    ppermute x2, starting transfers between devices, moved(): return lambda v: lax.ppermute(v, axis, [(i, i ^ step) for i in range(n)])  6.35 us
    pallas_call x2, Pallas kernels, source_toeplitz(): pl.pallas_call(toeplitz_kernel, grid=(n,), in_specs=[pl.BlockSpec((1, quo...  6.24 us
    unnamed x16, local copies, waits for them, and re-layouts  3.81 us
  transfers between devices with their start and end apart: 4, of which 3 were waited for; matrix products, arithmetic and copies ran while one was open for 5% of the time, Pallas kernels for 2%

profile of v5, /device:TPU:1, one launch (start us, length us, event | category | flops | bytes accessed | tf_op | source)
XLA Modules:
  0.0 148.2 jit_solution(8438918682049903978)
XLA Ops:
  6.5 0.0 reduce-scatter.2.cloned.1.call-start
  6.5 0.8 fusion.41
  7.3 1.1 fusion.17
  8.4 1.1 fusion.28
  9.5 1.3 fusion.43
  10.8 0.8 fusion.40
  12.4 15.0 %collective-permute-start.22 = (bf16[3,2048]{1,0:T(4,128)(2,1)S(1)}, bf16[3,2048]{1,0:T(4,128)(2,1)S(1)}, u32[]{:S(2)}, u32[]{:S(2)}) collective-permute-start(bf16[3,2048]{1,0:T(4,128)(2,1)S(1)} %get-tuple-element.59), channel_id=1, source_target_pairs={{0,508},{4,504},{8,500},{12,496},{16,492},{20,488},{24,484},{28,48... | collective-permute-start | bytes 36872 | tf_op jit(solution)/shard_map/ppermute | solution.py:77
  27.3 0.2 reshape.80
  27.6 0.2 fusion.39
  27.7 0.1 copy_dynamic-update-slice_fusion.1
  27.8 0.1 copy_dynamic-update-slice_fusion
  28.4 0.0 copy-start
  28.4 0.6 copy.33
  29.0 1.3 copy-done
  30.3 2.3 %shard_map.46 = bf16[2,16,128,256]{3,2,1,0:T(8,128)(2,1)} custom-call(bf16[2,16,128]{2,1,0:T(8,128)(2,1)} %bitcast.113), custom_call_target="tpu_custom_call" | custom-call | tf_op jit(solution)/shard_map/pallas_call | solution.py:35
  32.6 4.1 %fusion.11 = f32[2,64,8,128]{3,1,2,0:T(8,128)S(1)} fusion(bf16[64,8,16,256]{3,0,2,1:T(8,128)(2,1)} %copy-done, bf16[2,16,128,256]{3,2,1,0:T(8,128)(2,1)} %shard_map.46), kind=kOutput, calls=%fused_computation.9 | convolution fusion | flops 1073741824 | bytes 6815744 | tf_op jit(solution)/shard_map/cpqw,sqrw->scpr/dot_general | solution.py:55
  38.0 8.5 %conditional.2 = (bf16[3,2048]{1,0:T(4,128)(2,1)S(1)}) conditional(s32[]{:T(128)} %bitcast.6, bf16[3,2048]{1,0:T(4,128)(2,1)S(1)} %get-tuple-element.60, bf16[3,2048]{1,0:T(4,128)(2,1)S(1)} %get-tuple-element.60, bf16[3,2048]{1,0:T(4,128)(2,1)S(1)} %get-tuple-element.60, ...), branch_computations={%region_1.2_spmd, %region_2.3_spmd, %region_3.4_spmd, %region_4.5_... | conditional | bytes 73776 | solution.py:66
  38.0 4.4 %collective-permute-start.7 = (bf16[3,2048]{1,0:T(4,128)(2,1)S(1)}, bf16[3,2048]{1,0:T(4,128)(2,1)S(1)}, u32[]{:S(2)}, u32[]{:S(2)}) collective-permute-start(bf16[3,2048]{1,0:T(4,128)(2,1)S(1)} %param.8), channel_id=1, source_target_pairs={{0,32},{4,36},{8,40},{12,44},{16,48},{20,52},{24,56},{28,60},{32,0... | collective-permute-start | bytes 36872 | tf_op jit(solution)/shard_map/cond/branch_8_fun/ppermute | solution.py:62
  42.5 3.9 %collective-permute-done.7 = bf16[3,2048]{1,0:T(4,128)(2,1)S(1)} collective-permute-done((bf16[3,2048]{1,0:T(4,128)(2,1)S(1)}, bf16[3,2048]{1,0:T(4,128)(2,1)S(1)}, u32[]{:S(2)}, u32[]{:S(2)}) %collective-permute-start.7) | collective-permute-done | bytes 12320 | tf_op jit(solution)/shard_map/cond/branch_8_fun/ppermute | solution.py:62
  46.5 5.7 %conditional.3 = (bf16[3,2048]{1,0:T(4,128)(2,1)S(1)}) conditional(s32[]{:T(128)} %bitcast.5, bf16[3,2048]{1,0:T(4,128)(2,1)S(1)} %get-tuple-element.73, bf16[3,2048]{1,0:T(4,128)(2,1)S(1)} %get-tuple-element.73, bf16[3,2048]{1,0:T(4,128)(2,1)S(1)} %get-tuple-element.73, ...), branch_computations={%region_17.18_spmd, %region_18.19_spmd, %region_19.20_spmd, %regio... | conditional | bytes 73776 | solution.py:66
  46.5 1.9 %collective-permute-start.21 = (bf16[3,2048]{1,0:T(4,128)(2,1)S(1)}, bf16[3,2048]{1,0:T(4,128)(2,1)S(1)}, u32[]{:S(2)}, u32[]{:S(2)}) collective-permute-start(bf16[3,2048]{1,0:T(4,128)(2,1)S(1)} %param.23), channel_id=1, source_target_pairs={{0,448},{4,452},{8,456},{12,460},{16,464},{20,468},{24,472},{28,47... | collective-permute-start | bytes 36872 | tf_op jit(solution)/shard_map/cond/branch_7_fun/ppermute | solution.py:62
  48.4 3.8 %collective-permute-done.21 = bf16[3,2048]{1,0:T(4,128)(2,1)S(1)} collective-permute-done((bf16[3,2048]{1,0:T(4,128)(2,1)S(1)}, bf16[3,2048]{1,0:T(4,128)(2,1)S(1)}, u32[]{:S(2)}, u32[]{:S(2)}) %collective-permute-start.21) | collective-permute-done | bytes 12320 | tf_op jit(solution)/shard_map/cond/branch_7_fun/ppermute | solution.py:62
  52.2 0.0 collective-permute-done.22
  52.3 0.6 pad_maximum_fusion.2.src_ref
  52.9 3.9 %shard_map.47 = bf16[4,16,128,256]{3,2,1,0:T(8,128)(2,1)} custom-call(bf16[4,16,128]{2,1,0:T(8,128)(2,1)} %pad_maximum_fusion.2.src_ref), custom_call_target="tpu_custom_call" | custom-call | tf_op jit(solution)/shard_map/pallas_call | solution.py:35
  56.9 5.4 %fusion.6 = f32[4,64,8,128]{3,1,2,0:T(8,128)S(1)} fusion(bf16[64,8,16,256]{3,0,2,1:T(8,128)(2,1)} %copy-done, bf16[4,16,128,256]{3,2,1,0:T(8,128)(2,1)} %shard_map.47), kind=kOutput, calls=%fused_computation.8 | convolution fusion | flops 2147483648 | bytes 9437184 | tf_op jit(solution)/shard_map/cpqw,sqrw->scpr/dot_general | solution.py:55
  62.3 0.2 maximum_multiply_fusion
  62.4 0.9 copy.11
  63.4 1.5 %copy.30 = f32[48,8,8,128]{3,1,2,0:T(8,128)} copy(f32[48,8,8,128]{3,2,1,0:T(8,128)S(1)} %bitcast.110) | data formatting | bytes 3145728
  64.8 0.0 reduce-scatter.2.cloned.1.call-update
  64.9 0.2 convert_reduce_fusion
  65.0 0.1 reshape.82
  65.1 0.7 bitcast_add_fusion
  65.9 26.7 %reduce-scatter.2.cloned.1.call-done = f32[384,256]{1,0:T(8,128)} async-done(((f32[384,1024]{1,0:T(8,128)}), f32[384,256]{1,0:T(8,128)}) %reduce-scatter.2.cloned.1.call-update) | async-done | bytes 393232 | tf_op jit(solution)/shard_map/reduce_scatter | solution.py:110
  92.7 1.6 %fusion.16 = f32[512,256]{1,0:T(8,128)S(1)} fusion(f32[384,256]{1,0:T(8,128)} %reduce-scatter.2.cloned.1.call-done, s32[384]{0:T(512)S(1)} %pad_add_fusion), kind=kOutput, calls=%fused_computation.15 | convolution fusion | flops 604176384 | bytes 919040 | tf_op jit(solution)/shard_map/dot_general | solution.py:119
  94.3 0.1 reshape.81
  94.4 0.2 select_maximum_fusion
  94.6 45.9 %all_to_all.5 = f32[128,5,256]{2,1,0:T(8,128)S(1)} all-to-all(f32[128,5,256]{2,1,0:T(8,128)S(1)} %select_maximum_fusion), channel_id=1, replica_groups=mesh['chan'=128,'win'=4] {'chan'}, dimensions={0} | all-to-all | bytes 1310720 | tf_op jit(solution)/shard_map/all_to_all | solution.py:129
  140.5 0.1 reduce_sum.29
  140.7 0.7 slice_divide_fusion
  (30 shorter events, 0.6 us)
Async XLA Ops:
  6.5 86.1 %reduce-scatter.2.cloned.1.call-start = ((), (), s32[]{:S(2)}) async-start(), calls=%async_computation.2 | async-start | bytes 1966080 | tf_op jit(solution)/shard_map/reduce_scatter | solution.py:110
  12.4 39.9 %collective-permute-start.22 = (bf16[3,2048]{1,0:T(4,128)(2,1)S(1)}, bf16[3,2048]{1,0:T(4,128)(2,1)S(1)}, u32[]{:S(2)}, u32[]{:S(2)}) collective-permute-start(bf16[3,2048]{1,0:T(4,128)(2,1)S(1)} %get-tuple-element.59), channel_id=1, source_target_pairs={{0,508},{4,504},{8,500},{12,496},{16,492},{20,488},{24,484},{28,48... | collective-permute-start | bytes 36872 | tf_op jit(solution)/shard_map/ppermute | solution.py:77
  28.4 1.9 %copy-start = (bf16[64,8,16,256]{3,0,2,1:T(8,128)(2,1)}, bf16[64,8,16,256]{3,0,2,1:T(8,128)(2,1)S(1)}, u32[]{:S(2)}) copy-start(bf16[64,8,16,256]{3,0,2,1:T(8,128)(2,1)S(1)} %fusion.19) | copy-start | bytes 12582916
  38.0 8.4 %collective-permute-start.7 = (bf16[3,2048]{1,0:T(4,128)(2,1)S(1)}, bf16[3,2048]{1,0:T(4,128)(2,1)S(1)}, u32[]{:S(2)}, u32[]{:S(2)}) collective-permute-start(bf16[3,2048]{1,0:T(4,128)(2,1)S(1)} %param.8), channel_id=1, source_target_pairs={{0,32},{4,36},{8,40},{12,44},{16,48},{20,52},{24,56},{28,60},{32,0... | collective-permute-start | bytes 36872 | tf_op jit(solution)/shard_map/cond/branch_8_fun/ppermute | solution.py:62
  46.5 5.7 %collective-permute-start.21 = (bf16[3,2048]{1,0:T(4,128)(2,1)S(1)}, bf16[3,2048]{1,0:T(4,128)(2,1)S(1)}, u32[]{:S(2)}, u32[]{:S(2)}) collective-permute-start(bf16[3,2048]{1,0:T(4,128)(2,1)S(1)} %param.23), channel_id=1, source_target_pairs={{0,448},{4,452},{8,456},{12,460},{16,464},{20,468},{24,472},{28,47... | collective-permute-start | bytes 36872 | tf_op jit(solution)/shard_map/cond/branch_7_fun/ppermute | solution.py:62
Sparse Core Ops, SparseCore 0:
  65.0 27.6 reduce-scatter.1

commit v6 on v3

--- a/solution.py
+++ b/solution.py
@@ -99,10 +99,11 @@
         row = jnp.pad(row, (0, samples - row.shape[0]))
         label_rows.append(jnp.concatenate([sources, row[None, :]], axis=0))
     payload = jnp.stack(label_rows)
-    arrived = exchange(payload, round_masks, "chan")
     windows = receiver_windows(normed)
     scale = 1.0 / jnp.sqrt(jnp.float32(samples))
     own = correlate(windows, source_toeplitz(sources))
+    own, payload = lax.optimization_barrier((own, payload))
+    arrived = exchange(payload, round_masks, "chan")
     partners = jnp.concatenate([arrived[r, :SRC] for r in range(ROUNDS)], axis=0)
     far = correlate(windows, source_toeplitz(partners))
     rows = jnp.concatenate([own, far], axis=0) * scale

time: 140 us -> 133 us (0.950)
  waiting for transfers between devices: 46.7 us -> 41.7 us
  other arithmetic: 6.43 us -> 4.27 us
    ppermute x2, waiting for transfers between devices: 10.6 us -> 4.94 us  [moved(): return lambda v: lax.ppermute(v, axis, [(i, i ^ step) for i in range(n)])]
    unnamed x16 -> x22, local copies, waits for them, and re-layouts: 3.82 us -> 4.46 us
  transfers between devices with their start and end apart: 6 -> 6, of which waited for: 4 -> 4; matrix products, arithmetic and copies ran while one was open for 6% -> 2% of each run, Pallas kernels for 2% -> 0%
where the time goes in v6:
time: 133 us; the launch traced here: 132 us
  starting transfers between devices  44.8 us (34%)
  waiting for transfers between devices  41.7 us (31%)
  between operations  15.8 us (12%)
  matrix products  11.1 us (8%)
  local copies, waits for them, and re-layouts  8.32 us (6%)
  Pallas kernels  6.3 us (5%)
  other arithmetic  4.27 us (3%)
    all_to_all x1, waiting for transfers between devices, body(): lax.all_to_all(local, 'chan', split_axis=0, concat_axis=0, tiled=True)  20.4 us
    reduce_scatter x1, waiting for transfers between devices, body(): rows = lax.psum_scatter(rows, 'win', scatter_dimension=1, tiled=True)  16.3 us
    all_to_all x1, starting transfers between devices, body(): lax.all_to_all(local, 'chan', split_axis=0, concat_axis=0, tiled=True)  15.1 us
    ppermute x1, starting transfers between devices, exchange(): fixed = lax.ppermute(fixed, axis, [(i, i ^ full) for i in range(n)])  14.9 us
    dot_general x2, matrix products, correlate(): jnp.einsum('cpqw,sqrw->scpr', windows, toeplitz, preferred_element_type=j...  9.52 us
    all_to_all x1, starting transfers between devices, body(): lax.all_to_all(own_counts, 'chan', split_axis=0, concat_axis=0, tiled=True)  7.34 us
    ppermute x2, starting transfers between devices, moved(): return lambda v: lax.ppermute(v, axis, [(i, i ^ step) for i in range(n)])  7.34 us
    pallas_call x2, Pallas kernels, source_toeplitz(): pl.pallas_call(toeplitz_kernel, grid=(n,), in_specs=[pl.BlockSpec((1, quo...  6.3 us
  transfers between devices with their start and end apart: 6, of which 4 were waited for; matrix products, arithmetic and copies ran while one was open for 2% of the time, Pallas kernels for 0%

profile of v6, /device:TPU:1, one launch (start us, length us, event | category | flops | bytes accessed | tf_op | source)
XLA Modules:
  0.0 132.4 jit_solution(11101834050994330588)
XLA Ops:
  6.5 0.0 reduce-scatter.2.cloned.1.call-start
  6.5 1.1 fusion.17
  7.7 1.1 fusion.28
  8.8 0.2 reshape.81
  9.0 0.2 fusion.39
  9.2 0.1 copy_dynamic-update-slice_fusion.1
  9.3 0.1 copy_dynamic-update-slice_fusion
  9.5 0.0 copy-start.3
  9.5 0.0 copy-start.1
  9.9 0.0 copy-start
  9.9 1.9 %copy-done = bf16[64,8,16,256]{3,0,2,1:T(8,128)(2,1)} copy-done((bf16[64,8,16,256]{3,0,2,1:T(8,128)(2,1)}, bf16[64,8,16,256]{3,0,2,1:T(8,128)(2,1)S(1)}, u32[]{:S(2)}) %copy-start) | copy-done | bytes 4194328
  11.8 0.6 copy.35
  12.4 2.3 %shard_map.46 = bf16[2,16,128,256]{3,2,1,0:T(8,128)(2,1)} custom-call(bf16[2,16,128]{2,1,0:T(8,128)(2,1)} %bitcast.118), custom_call_target="tpu_custom_call" | custom-call | tf_op jit(solution)/shard_map/pallas_call | solution.py:35
  14.7 0.0 copy-done.3
  14.7 0.0 copy-done.1
  14.8 0.0 copy-start.2
  14.8 4.1 %fusion.11 = f32[2,64,8,128]{3,1,2,0:T(8,128)S(1)} fusion(bf16[64,8,16,256]{3,0,2,1:T(8,128)(2,1)} %copy-done, bf16[2,16,128,256]{3,2,1,0:T(8,128)(2,1)} %shard_map.46), kind=kOutput, calls=%fused_computation.9 | convolution fusion | flops 1073741824 | bytes 6815744 | tf_op jit(solution)/shard_map/cpqw,sqrw->scpr/dot_general | solution.py:55
  19.0 0.0 copy-done.2
  19.0 0.6 fusion.42
  20.3 14.9 %collective-permute-start.22 = (bf16[3,2048]{1,0:T(4,128)(2,1)S(1)}, bf16[3,2048]{1,0:T(4,128)(2,1)S(1)}, u32[]{:S(2)}, u32[]{:S(2)}) collective-permute-start(bf16[3,2048]{1,0:T(4,128)(2,1)S(1)} %get-tuple-element.63), channel_id=1, source_target_pairs={{0,508},{4,504},{8,500},{12,496},{16,492},{20,488},{24,484},{28,48... | collective-permute-start | bytes 36872 | tf_op jit(solution)/shard_map/ppermute | solution.py:77
  36.6 7.0 %conditional.2 = (bf16[3,2048]{1,0:T(4,128)(2,1)S(1)}) conditional(s32[]{:T(128)} %bitcast.23, bf16[3,2048]{1,0:T(4,128)(2,1)S(1)} %get-tuple-element.64, bf16[3,2048]{1,0:T(4,128)(2,1)S(1)} %get-tuple-element.64, bf16[3,2048]{1,0:T(4,128)(2,1)S(1)} %get-tuple-element.64, ...), branch_computations={%region_1.2_spmd, %region_2.3_spmd, %region_3.4_spmd, %region_4.5_... | conditional | bytes 73776 | solution.py:66
  36.7 4.3 %collective-permute-start.6 = (bf16[3,2048]{1,0:T(4,128)(2,1)S(1)}, bf16[3,2048]{1,0:T(4,128)(2,1)S(1)}, u32[]{:S(2)}, u32[]{:S(2)}) collective-permute-start(bf16[3,2048]{1,0:T(4,128)(2,1)S(1)} %param.7), channel_id=1, source_target_pairs={{0,28},{4,24},{8,20},{12,16},{16,12},{20,8},{24,4},{28,0},{32,60},... | collective-permute-start | bytes 36872 | tf_op jit(solution)/shard_map/cond/branch_7_fun/ppermute | solution.py:62
  40.9 2.6 %collective-permute-done.6 = bf16[3,2048]{1,0:T(4,128)(2,1)S(1)} collective-permute-done((bf16[3,2048]{1,0:T(4,128)(2,1)S(1)}, bf16[3,2048]{1,0:T(4,128)(2,1)S(1)}, u32[]{:S(2)}, u32[]{:S(2)}) %collective-permute-start.6) | collective-permute-done | bytes 12320 | tf_op jit(solution)/shard_map/cond/branch_7_fun/ppermute | solution.py:62
  43.6 5.4 %conditional.3 = (bf16[3,2048]{1,0:T(4,128)(2,1)S(1)}) conditional(s32[]{:T(128)} %bitcast.22, bf16[3,2048]{1,0:T(4,128)(2,1)S(1)} %get-tuple-element.79, bf16[3,2048]{1,0:T(4,128)(2,1)S(1)} %get-tuple-element.79, bf16[3,2048]{1,0:T(4,128)(2,1)S(1)} %get-tuple-element.79, ...), branch_computations={%region_17.18_spmd, %region_18.19_spmd, %region_19.20_spmd, %regio... | conditional | bytes 73776 | solution.py:66
  43.6 3.1 %collective-permute-start.16 = (bf16[3,2048]{1,0:T(4,128)(2,1)S(1)}, bf16[3,2048]{1,0:T(4,128)(2,1)S(1)}, u32[]{:S(2)}, u32[]{:S(2)}) collective-permute-start(bf16[3,2048]{1,0:T(4,128)(2,1)S(1)} %param.18), channel_id=1, source_target_pairs={{0,128},{4,132},{8,136},{12,140},{16,144},{20,148},{24,152},{28,15... | collective-permute-start | bytes 36872 | tf_op jit(solution)/shard_map/cond/branch_2_fun/ppermute | solution.py:62
  46.7 2.3 %collective-permute-done.16 = bf16[3,2048]{1,0:T(4,128)(2,1)S(1)} collective-permute-done((bf16[3,2048]{1,0:T(4,128)(2,1)S(1)}, bf16[3,2048]{1,0:T(4,128)(2,1)S(1)}, u32[]{:S(2)}, u32[]{:S(2)}) %collective-permute-start.16) | collective-permute-done | bytes 12320 | tf_op jit(solution)/shard_map/cond/branch_2_fun/ppermute | solution.py:62
  49.1 0.0 collective-permute-done.22
  49.1 0.6 pad_maximum_fusion.3.src_ref
  49.7 4.0 %shard_map.47 = bf16[4,16,128,256]{3,2,1,0:T(8,128)(2,1)} custom-call(bf16[4,16,128]{2,1,0:T(8,128)(2,1)} %pad_maximum_fusion.3.src_ref), custom_call_target="tpu_custom_call" | custom-call | tf_op jit(solution)/shard_map/pallas_call | solution.py:35
  53.7 5.4 %fusion.6 = f32[4,64,8,128]{3,1,2,0:T(8,128)S(1)} fusion(bf16[64,8,16,256]{3,0,2,1:T(8,128)(2,1)} %copy-done, bf16[4,16,128,256]{3,2,1,0:T(8,128)(2,1)} %shard_map.47), kind=kOutput, calls=%fused_computation.8 | convolution fusion | flops 2147483648 | bytes 9437184 | tf_op jit(solution)/shard_map/cpqw,sqrw->scpr/dot_general | solution.py:55
  59.2 0.2 maximum_multiply_fusion
  59.3 0.9 copy.14
  60.2 1.5 %copy.32 = f32[48,8,8,128]{3,1,2,0:T(8,128)} copy(f32[48,8,8,128]{3,2,1,0:T(8,128)S(1)} %bitcast.116) | data formatting | bytes 3145728
  61.7 0.0 reduce-scatter.2.cloned.1.call-update
  61.8 0.2 convert_reduce_fusion
  61.9 0.7 all_to_all.14
  62.7 7.3 %all-to-all-start.1 = ((f32[128,4,1]{1,2,0:T(1,128)}), f32[128,4,1]{1,2,0:T(1,128)S(1)}, u32[]{:S(2)}, u32[]{:S(2)}) async-start(f32[128,4,1]{1,2,0:T(1,128)} %bitcast.34), calls=%async_computation.2 | async-start | bytes 131072 | tf_op jit(solution)/shard_map/all_to_all | solution.py:127
  70.1 16.3 %reduce-scatter.2.cloned.1.call-done = f32[384,256]{1,0:T(8,128)} async-done(((f32[384,1024]{1,0:T(8,128)}), f32[384,256]{1,0:T(8,128)}) %reduce-scatter.2.cloned.1.call-update) | async-done | bytes 393232 | tf_op jit(solution)/shard_map/reduce_scatter | solution.py:111
  86.5 1.6 %fusion.16 = f32[512,256]{1,0:T(8,128)S(1)} fusion(f32[384,256]{1,0:T(8,128)} %reduce-scatter.2.cloned.1.call-done, s32[384]{0:T(512)S(1)} %pad_add_fusion), kind=kOutput, calls=%fused_computation.13 | convolution fusion | flops 604176384 | bytes 919040 | tf_op jit(solution)/shard_map/dot_general | solution.py:120
  88.1 1.0 all_to_all.12
  89.0 0.0 all-to-all-done.1
  89.0 15.1 %all-to-all-start = ((f32[128,4,256]{2,1,0:T(4,128)}), f32[128,4,256]{2,1,0:T(4,128)S(1)}, u32[]{:S(2)}, u32[]{:S(2)}) async-start(f32[128,4,256]{2,1,0:T(4,128)} %all_to_all.12), calls=%async_computation.1 | async-start | bytes 1048576 | tf_op jit(solution)/shard_map/all_to_all | solution.py:121
  104.2 0.2 reduce_sum.39
  104.3 20.4 %all-to-all-done = f32[128,4,256]{2,1,0:T(4,128)S(1)} async-done(((f32[128,4,256]{2,1,0:T(4,128)}), f32[128,4,256]{2,1,0:T(4,128)S(1)}, u32[]{:S(2)}, u32[]{:S(2)}) %all-to-all-start) | async-done | bytes 524320 | tf_op jit(solution)/shard_map/all_to_all | solution.py:121
  124.7 0.1 reduce_sum.37
  124.9 0.7 broadcast_divide_fusion
  (35 shorter events, 0.7 us)
Async XLA Ops:
  6.5 79.9 %reduce-scatter.2.cloned.1.call-start = ((), (), s32[]{:S(2)}) async-start(), calls=%async_computation.3 | async-start | bytes 1966080 | tf_op jit(solution)/shard_map/reduce_scatter | solution.py:111
  9.5 5.2 %copy-start.3 = (s32[384,1]{0,1:T(1,128)S(1)}, s32[384,1]{0,1:T(1,128)}, u32[]{:S(2)}) copy-start(s32[384,1]{0,1:T(1,128)} %param.30) | copy-start | bytes 4612
  9.5 5.2 %copy-start.1 = (s32[384]{0:T(512)S(1)}, s32[384]{0:T(512)}, u32[]{:S(2)}) copy-start(s32[384]{0:T(512)} %param.31) | copy-start | bytes 4612
  9.9 1.9 %copy-start = (bf16[64,8,16,256]{3,0,2,1:T(8,128)(2,1)}, bf16[64,8,16,256]{3,0,2,1:T(8,128)(2,1)S(1)}, u32[]{:S(2)}) copy-start(bf16[64,8,16,256]{3,0,2,1:T(8,128)(2,1)S(1)} %fusion.19) | copy-start | bytes 12582916
  14.8 4.2 %copy-start.2 = (s32[2]{0:T(128)S(1)}, s32[2]{0:T(128)}, u32[]{:S(2)}) copy-start(s32[2]{0:T(128)} %param.29) | copy-start | bytes 28
  20.3 28.7 %collective-permute-start.22 = (bf16[3,2048]{1,0:T(4,128)(2,1)S(1)}, bf16[3,2048]{1,0:T(4,128)(2,1)S(1)}, u32[]{:S(2)}, u32[]{:S(2)}) collective-permute-start(bf16[3,2048]{1,0:T(4,128)(2,1)S(1)} %get-tuple-element.63), channel_id=1, source_target_pairs={{0,508},{4,504},{8,500},{12,496},{16,492},{20,488},{24,484},{28,48... | collective-permute-start | bytes 36872 | tf_op jit(solution)/shard_map/ppermute | solution.py:77
  36.7 6.9 %collective-permute-start.6 = (bf16[3,2048]{1,0:T(4,128)(2,1)S(1)}, bf16[3,2048]{1,0:T(4,128)(2,1)S(1)}, u32[]{:S(2)}, u32[]{:S(2)}) collective-permute-start(bf16[3,2048]{1,0:T(4,128)(2,1)S(1)} %param.7), channel_id=1, source_target_pairs={{0,28},{4,24},{8,20},{12,16},{16,12},{20,8},{24,4},{28,0},{32,60},... | collective-permute-start | bytes 36872 | tf_op jit(solution)/shard_map/cond/branch_7_fun/ppermute | solution.py:62
  43.6 5.4 %collective-permute-start.16 = (bf16[3,2048]{1,0:T(4,128)(2,1)S(1)}, bf16[3,2048]{1,0:T(4,128)(2,1)S(1)}, u32[]{:S(2)}, u32[]{:S(2)}) collective-permute-start(bf16[3,2048]{1,0:T(4,128)(2,1)S(1)} %param.18), channel_id=1, source_target_pairs={{0,128},{4,132},{8,136},{12,140},{16,144},{20,148},{24,152},{28,15... | collective-permute-start | bytes 36872 | tf_op jit(solution)/shard_map/cond/branch_2_fun/ppermute | solution.py:62
  62.7 26.4 %all-to-all-start.1 = ((f32[128,4,1]{1,2,0:T(1,128)}), f32[128,4,1]{1,2,0:T(1,128)S(1)}, u32[]{:S(2)}, u32[]{:S(2)}) async-start(f32[128,4,1]{1,2,0:T(1,128)} %bitcast.34), calls=%async_computation.2 | async-start | bytes 131072 | tf_op jit(solution)/shard_map/all_to_all | solution.py:127
  89.0 35.7 %all-to-all-start = ((f32[128,4,256]{2,1,0:T(4,128)}), f32[128,4,256]{2,1,0:T(4,128)S(1)}, u32[]{:S(2)}, u32[]{:S(2)}) async-start(f32[128,4,256]{2,1,0:T(4,128)} %all_to_all.12), calls=%async_computation.1 | async-start | bytes 1048576 | tf_op jit(solution)/shard_map/all_to_all | solution.py:121
Sparse Core Ops, SparseCore 0:
  61.9 24.5 reduce-scatter.1

commit v7 on v3

--- a/solution.py
+++ b/solution.py
@@ -55,15 +55,23 @@
     return jnp.einsum("cpqw,sqrw->scpr", windows, toeplitz, preferred_element_type=jnp.float32)
 
 
-def xor_permute(x, mask, axis, shift, width):
+def xor_level(fixed, free, mask, full, axis, shift, width):
     n = lax.axis_size(axis)
+    span = (1 << width) - 1
+    fixed_step = ((full >> shift) & span) << shift
 
     def moved(step):
-        return lambda v: lax.ppermute(v, axis, [(i, i ^ step) for i in range(n)])
+        def go(pair):
+            fixed_part, free_part = pair
+            fixed_part = lax.ppermute(fixed_part, axis, [(i, i ^ fixed_step) for i in range(n)])
+            if step:
+                free_part = lax.ppermute(free_part, axis, [(i, i ^ step) for i in range(n)])
+            return fixed_part, free_part
 
-    branches = [lambda v: v] + [moved(d << shift) for d in range(1, 1 << width)]
-    part = jnp.bitwise_and(jnp.right_shift(mask, shift), (1 << width) - 1)
-    return lax.switch(part, branches, x)
+        return go
+
+    part = jnp.bitwise_and(jnp.right_shift(mask, shift), span)
+    return lax.switch(part, [moved(d << shift) for d in range(1 << width)], (fixed, free))
 
 
 def exchange(payload, masks, axis):
@@ -74,11 +82,10 @@
     other = jnp.bitwise_xor(jnp.bitwise_xor(masks[0], masks[1]), full)
     fixed = jnp.where(first_full, payload[0], payload[1])
     free = jnp.where(first_full, payload[1], payload[0])
-    fixed = lax.ppermute(fixed, axis, [(i, i ^ full) for i in range(n)])
     low = min(bits, 4)
-    free = xor_permute(free, other, axis, 0, low)
+    fixed, free = xor_level(fixed, free, other, full, axis, 0, low)
     if bits > low:
-        free = xor_permute(free, other, axis, low, bits - low)
+        fixed, free = xor_level(fixed, free, other, full, axis, low, bits - low)
     return jnp.stack(
         [jnp.where(first_full, fixed, free), jnp.where(first_full, free, fixed)]
     )

time: 140 us -> 137 us (0.979)
  starting transfers between devices: 44.8 us -> 48.5 us
  matrix products: 11.1 us -> 8.44 us
  waiting for transfers between devices: 46.7 us -> 44.7 us
  other arithmetic: 6.43 us -> 4.97 us
    all_to_all x1, starting transfers between devices: 8.52 us -> 11.6 us  [body(): lax.all_to_all(own_counts, 'chan', split_axis=0, concat_axis=0, tiled=True)]
    dot_general x2, matrix products: 9.51 us -> 6.83 us  [correlate(): jnp.einsum('cpqw,sqrw->scpr', windows, toeplitz, preferred_element_type=j...]
    ppermute x3 -> x4, waiting for transfers between devices: 10.6 us -> 7.93 us  [the longest x2 7.93 us: go(): lax.ppermute(fixed_part, axis, [(i, i ^ fixed_step) for i in range(n)])]
    unnamed x16 -> x26, local copies, waits for them, and re-layouts: 3.82 us -> 4.49 us
    ppermute x3 -> x4, starting transfers between devices: 21.3 us -> 21.7 us  [the longest x2 17.4 us: go(): free_part = lax.ppermute(free_part, axis, [(i, i ^ step) for i in range(n)])]
  transfers between devices with their start and end apart: 6 -> 7, of which waited for: 4 -> 4; matrix products, arithmetic and copies ran while one was open for 6% -> 1% of each run, Pallas kernels for 2% -> 0%
where the time goes in v7:
time: 137 us
  starting transfers between devices  48.5 us (35%)
  waiting for transfers between devices  44.7 us (33%)
  between operations  15.7 us (11%)
  matrix products  8.44 us (6%)
  local copies, waits for them, and re-layouts  8.32 us (6%)
  Pallas kernels  6.21 us (5%)
  other arithmetic  4.97 us (4%)
    all_to_all x1, waiting for transfers between devices, body(): lax.all_to_all(local, 'chan', split_axis=0, concat_axis=0, tiled=True)  20.4 us
    ppermute x2, starting transfers between devices, go(): free_part = lax.ppermute(free_part, axis, [(i, i ^ step) for i in range(n)])  17.4 us
    reduce_scatter x1, waiting for transfers between devices, body(): rows = lax.psum_scatter(rows, 'win', scatter_dimension=1, tiled=True)  16.4 us
    all_to_all x1, starting transfers between devices, body(): lax.all_to_all(local, 'chan', split_axis=0, concat_axis=0, tiled=True)  15.1 us
    all_to_all x1, starting transfers between devices, body(): lax.all_to_all(own_counts, 'chan', split_axis=0, concat_axis=0, tiled=True)  11.6 us
    ppermute x2, waiting for transfers between devices, go(): lax.ppermute(fixed_part, axis, [(i, i ^ fixed_step) for i in range(n)])  7.93 us
    dot_general x2, matrix products, correlate(): jnp.einsum('cpqw,sqrw->scpr', windows, toeplitz, preferred_element_type=j...  6.83 us
    pallas_call x2, Pallas kernels, source_toeplitz(): pl.pallas_call(toeplitz_kernel, grid=(n,), in_specs=[pl.BlockSpec((1, quo...  6.21 us
  transfers between devices with their start and end apart: 7, of which 4 were waited for; matrix products, arithmetic and copies ran while one was open for 1% of the time, Pallas kernels for 0%

profile of v7, /device:TPU:1, one launch (start us, length us, event | category | flops | bytes accessed | tf_op | source)
XLA Modules:
  0.0 136.9 jit_solution(17326802332332771236)
XLA Ops:
  6.5 0.0 reduce-scatter.2.cloned.1.call-start
  6.5 1.1 fusion.17
  7.7 1.1 fusion.28
  8.8 0.2 reshape.77
  9.0 0.2 fusion.37
  9.2 0.1 copy_dynamic-update-slice_fusion.1
  9.3 0.1 copy_dynamic-update-slice_fusion
  9.4 0.0 copy-start.4
  9.4 0.0 copy-start.5
  9.5 0.0 copy-start.3
  9.9 0.0 copy-start.1
  9.9 2.0 %copy-done.1 = bf16[64,8,16,256]{3,0,2,1:T(8,128)(2,1)} copy-done((bf16[64,8,16,256]{3,0,2,1:T(8,128)(2,1)}, bf16[64,8,16,256]{3,0,2,1:T(8,128)(2,1)S(1)}, u32[]{:S(2)}) %copy-start.1) | copy-done | bytes 4194328
  11.8 0.0 copy-done.4
  11.8 0.6 fusion.40
  14.3 0.0 copy-done.5
  14.4 0.0 copy-done.3
  14.5 13.1 %conditional.2 = (bf16[3,2048]{1,0:T(4,128)(2,1)}, bf16[3,2048]{1,0:T(4,128)(2,1)S(1)}) conditional(s32[]{:T(128)} %bitcast.3, (bf16[3,2048]{1,0:T(4,128)(2,1)S(1)}, bf16[3,2048]{1,0:T(4,128)(2,1)S(1)}) %tuple.93, (bf16[3,2048]{1,0:T(4,128)(2,1)S(1)}, bf16[3,2048]{1,0:T(4,128)(2,1)S(1)}) %tuple.93, ...), branch_computations={%region_1.2_spmd, %region_2.3_spmd, %region_3.4_spmd, %region_4.5_... | conditional | bytes 122976 | solution.py:74
  14.6 6.7 %collective-permute-start.24 = (bf16[3,2048]{1,0:T(4,128)(2,1)S(1)}, bf16[3,2048]{1,0:T(4,128)(2,1)S(1)}, u32[]{:S(2)}, u32[]{:S(2)}) collective-permute-start(bf16[3,2048]{1,0:T(4,128)(2,1)S(1)} %get-tuple-element.126), channel_id=1, source_target_pairs={{0,48},{4,52},{8,56},{12,60},{16,32},{20,36},{24,40},{28,44},{32,1... | collective-permute-start | bytes 36872 | tf_op jit(solution)/shard_map/cond/branch_12_fun/ppermute | solution.py:68
  21.3 2.5 %collective-permute-start.23 = (bf16[3,2048]{1,0:T(4,128)(2,1)S(1)}, bf16[3,2048]{1,0:T(4,128)(2,1)}, u32[]{:S(2)}, u32[]{:S(2)}) collective-permute-start(bf16[3,2048]{1,0:T(4,128)(2,1)S(1)} %get-tuple-element.125), channel_id=1, source_target_pairs={{0,60},{4,56},{8,52},{12,48},{16,44},{20,40},{24,36},{28,32},{32,2... | collective-permute-start | bytes 36872 | tf_op jit(solution)/shard_map/cond/branch_12_fun/ppermute | solution.py:66
  23.7 0.0 collective-permute-done.24
  23.8 3.9 %collective-permute-done.23 = bf16[3,2048]{1,0:T(4,128)(2,1)} collective-permute-done((bf16[3,2048]{1,0:T(4,128)(2,1)S(1)}, bf16[3,2048]{1,0:T(4,128)(2,1)}, u32[]{:S(2)}, u32[]{:S(2)}) %collective-permute-start.23) | collective-permute-done | bytes 12320 | tf_op jit(solution)/shard_map/cond/branch_12_fun/ppermute | solution.py:66
  27.6 16.7 %conditional.3 = (bf16[3,2048]{1,0:T(4,128)(2,1)}, bf16[3,2048]{1,0:T(4,128)(2,1)S(1)}) conditional(s32[]{:T(128)} %bitcast.2, (bf16[3,2048]{1,0:T(4,128)(2,1)}, bf16[3,2048]{1,0:T(4,128)(2,1)S(1)}) %conditional.2, (bf16[3,2048]{1,0:T(4,128)(2,1)}, bf16[3,2048]{1,0:T(4,128)(2,1)S(1)}) %conditional.2, ...), branch_computations={%region_17.18_spmd, %region_18.19_spmd, %region_19.20_spmd, %regio... | conditional | bytes 122976 | solution.py:74
  27.6 10.7 %collective-permute-start.45 = (bf16[3,2048]{1,0:T(4,128)(2,1)S(1)}, bf16[3,2048]{1,0:T(4,128)(2,1)S(1)}, u32[]{:S(2)}, u32[]{:S(2)}) collective-permute-start(bf16[3,2048]{1,0:T(4,128)(2,1)S(1)} %get-tuple-element.148), channel_id=1, source_target_pairs={{0,448},{4,452},{8,456},{12,460},{16,464},{20,468},{24,472},{28,47... | collective-permute-start | bytes 36872 | tf_op jit(solution)/shard_map/cond/branch_7_fun/ppermute | solution.py:68
  38.3 1.9 %collective-permute-start.44 = (bf16[3,2048]{1,0:T(4,128)(2,1)}, bf16[3,2048]{1,0:T(4,128)(2,1)}, u32[]{:S(2)}, u32[]{:S(2)}) collective-permute-start(bf16[3,2048]{1,0:T(4,128)(2,1)} %get-tuple-element.147), channel_id=1, source_target_pairs={{0,448},{4,452},{8,456},{12,460},{16,464},{20,468},{24,472},{28,47... | collective-permute-start | bytes 36872 | tf_op jit(solution)/shard_map/cond/branch_7_fun/ppermute | solution.py:66
  40.2 0.0 collective-permute-done.45
  40.3 4.1 %collective-permute-done.44 = bf16[3,2048]{1,0:T(4,128)(2,1)} collective-permute-done((bf16[3,2048]{1,0:T(4,128)(2,1)}, bf16[3,2048]{1,0:T(4,128)(2,1)}, u32[]{:S(2)}, u32[]{:S(2)}) %collective-permute-start.44) | collective-permute-done | bytes 12320 | tf_op jit(solution)/shard_map/cond/branch_7_fun/ppermute | solution.py:66
  44.3 0.7 select_bitcast_fusion.1
  45.1 0.6 pad_maximum_fusion.2.src_ref
  45.7 3.9 %shard_map.47 = bf16[4,16,128,256]{3,2,1,0:T(8,128)(2,1)} custom-call(bf16[4,16,128]{2,1,0:T(8,128)(2,1)} %pad_maximum_fusion.2.src_ref), custom_call_target="tpu_custom_call" | custom-call | tf_op jit(solution)/shard_map/pallas_call | solution.py:35
  49.7 0.6 copy.35
  50.3 2.3 %shard_map.46 = bf16[2,16,128,256]{3,2,1,0:T(8,128)(2,1)} custom-call(bf16[2,16,128]{2,1,0:T(8,128)(2,1)} %bitcast.110), custom_call_target="tpu_custom_call" | custom-call | tf_op jit(solution)/shard_map/pallas_call | solution.py:35
  52.5 0.0 copy-start
  52.5 0.0 copy-start.2
  52.5 5.6 %fusion.6 = f32[4,64,8,128]{3,1,2,0:T(8,128)S(1)} fusion(bf16[64,8,16,256]{3,0,2,1:T(8,128)(2,1)} %copy-done.1, bf16[4,16,128,256]{3,2,1,0:T(8,128)(2,1)} %shard_map.47), kind=kOutput, calls=%fused_computation.8 | convolution fusion | flops 2147483648 | bytes 9437184 | tf_op jit(solution)/shard_map/cpqw,sqrw->scpr/dot_general | solution.py:55
  58.1 0.0 copy-done
  58.1 0.0 copy-done.2
  58.1 1.3 fusion.11
  59.4 0.2 maximum_multiply_fusion
  59.6 0.9 copy.14
  60.5 1.5 %copy.32 = f32[48,8,8,128]{3,1,2,0:T(8,128)} copy(f32[48,8,8,128]{3,2,1,0:T(8,128)S(1)} %bitcast.108) | data formatting | bytes 3145728
  62.0 0.0 reduce-scatter.2.cloned.1.call-update
  62.0 0.2 convert_reduce_fusion
  62.2 0.7 all_to_all.14
  62.9 11.6 %all-to-all-start.1 = ((f32[128,4,1]{1,2,0:T(1,128)}), f32[128,4,1]{1,2,0:T(1,128)S(1)}, u32[]{:S(2)}, u32[]{:S(2)}) async-start(f32[128,4,1]{1,2,0:T(1,128)} %bitcast.30), calls=%async_computation.2 | async-start | bytes 131072 | tf_op jit(solution)/shard_map/all_to_all | solution.py:133
  74.6 16.4 %reduce-scatter.2.cloned.1.call-done = f32[384,256]{1,0:T(8,128)} async-done(((f32[384,1024]{1,0:T(8,128)}), f32[384,256]{1,0:T(8,128)}) %reduce-scatter.2.cloned.1.call-update) | async-done | bytes 393232 | tf_op jit(solution)/shard_map/reduce_scatter | solution.py:117
  91.0 1.6 %fusion.16 = f32[512,256]{1,0:T(8,128)S(1)} fusion(f32[384,256]{1,0:T(8,128)} %reduce-scatter.2.cloned.1.call-done, s32[384]{0:T(512)S(1)} %pad_add_fusion), kind=kOutput, calls=%fused_computation.13 | convolution fusion | flops 604176384 | bytes 919040 | tf_op jit(solution)/shard_map/dot_general | solution.py:126
  92.6 0.9 all_to_all.12
  93.5 0.0 all-to-all-done.1
  93.5 15.1 %all-to-all-start = ((f32[128,4,256]{2,1,0:T(4,128)}), f32[128,4,256]{2,1,0:T(4,128)S(1)}, u32[]{:S(2)}, u32[]{:S(2)}) async-start(f32[128,4,256]{2,1,0:T(4,128)} %all_to_all.12), calls=%async_computation.1 | async-start | bytes 1048576 | tf_op jit(solution)/shard_map/all_to_all | solution.py:127
  108.7 0.2 reduce_sum.39
  108.8 20.4 %all-to-all-done = f32[128,4,256]{2,1,0:T(4,128)S(1)} async-done(((f32[128,4,256]{2,1,0:T(4,128)}), f32[128,4,256]{2,1,0:T(4,128)S(1)}, u32[]{:S(2)}, u32[]{:S(2)}) %all-to-all-start) | async-done | bytes 524320 | tf_op jit(solution)/shard_map/all_to_all | solution.py:127
  129.2 0.1 reduce_sum.37
  129.4 0.7 broadcast_divide_fusion
  (32 shorter events, 0.6 us)
Async XLA Ops:
  6.5 84.5 %reduce-scatter.2.cloned.1.call-start = ((), (), s32[]{:S(2)}) async-start(), calls=%async_computation.3 | async-start | bytes 1966080 | tf_op jit(solution)/shard_map/reduce_scatter | solution.py:117
  9.4 2.4 %copy-start.4 = (s32[2]{0:T(128)S(1)}, s32[2]{0:T(128)}, u32[]{:S(2)}) copy-start(s32[2]{0:T(128)} %param.29) | copy-start | bytes 28
  9.4 4.9 %copy-start.5 = (s32[384,1]{0,1:T(1,128)S(1)}, s32[384,1]{0,1:T(1,128)}, u32[]{:S(2)}) copy-start(s32[384,1]{0,1:T(1,128)} %param.30) | copy-start | bytes 4612
  9.5 4.9 %copy-start.3 = (s32[384]{0:T(512)S(1)}, s32[384]{0:T(512)}, u32[]{:S(2)}) copy-start(s32[384]{0:T(512)} %param.31) | copy-start | bytes 4612
  9.9 2.0 %copy-start.1 = (bf16[64,8,16,256]{3,0,2,1:T(8,128)(2,1)}, bf16[64,8,16,256]{3,0,2,1:T(8,128)(2,1)S(1)}, u32[]{:S(2)}) copy-start(bf16[64,8,16,256]{3,0,2,1:T(8,128)(2,1)S(1)} %fusion.19) | copy-start | bytes 12582916
  14.6 9.2 %collective-permute-start.24 = (bf16[3,2048]{1,0:T(4,128)(2,1)S(1)}, bf16[3,2048]{1,0:T(4,128)(2,1)S(1)}, u32[]{:S(2)}, u32[]{:S(2)}) collective-permute-start(bf16[3,2048]{1,0:T(4,128)(2,1)S(1)} %get-tuple-element.126), channel_id=1, source_target_pairs={{0,48},{4,52},{8,56},{12,60},{16,32},{20,36},{24,40},{28,44},{32,1... | collective-permute-start | bytes 36872 | tf_op jit(solution)/shard_map/cond/branch_12_fun/ppermute | solution.py:68
  21.3 6.4 %collective-permute-start.23 = (bf16[3,2048]{1,0:T(4,128)(2,1)S(1)}, bf16[3,2048]{1,0:T(4,128)(2,1)}, u32[]{:S(2)}, u32[]{:S(2)}) collective-permute-start(bf16[3,2048]{1,0:T(4,128)(2,1)S(1)} %get-tuple-element.125), channel_id=1, source_target_pairs={{0,60},{4,56},{8,52},{12,48},{16,44},{20,40},{24,36},{28,32},{32,2... | collective-permute-start | bytes 36872 | tf_op jit(solution)/shard_map/cond/branch_12_fun/ppermute | solution.py:66
  27.6 12.6 %collective-permute-start.45 = (bf16[3,2048]{1,0:T(4,128)(2,1)S(1)}, bf16[3,2048]{1,0:T(4,128)(2,1)S(1)}, u32[]{:S(2)}, u32[]{:S(2)}) collective-permute-start(bf16[3,2048]{1,0:T(4,128)(2,1)S(1)} %get-tuple-element.148), channel_id=1, source_target_pairs={{0,448},{4,452},{8,456},{12,460},{16,464},{20,468},{24,472},{28,47... | collective-permute-start | bytes 36872 | tf_op jit(solution)/shard_map/cond/branch_7_fun/ppermute | solution.py:68
  38.3 6.0 %collective-permute-start.44 = (bf16[3,2048]{1,0:T(4,128)(2,1)}, bf16[3,2048]{1,0:T(4,128)(2,1)}, u32[]{:S(2)}, u32[]{:S(2)}) collective-permute-start(bf16[3,2048]{1,0:T(4,128)(2,1)} %get-tuple-element.147), channel_id=1, source_target_pairs={{0,448},{4,452},{8,456},{12,460},{16,464},{20,468},{24,472},{28,47... | collective-permute-start | bytes 36872 | tf_op jit(solution)/shard_map/cond/branch_7_fun/ppermute | solution.py:66
  52.5 5.6 %copy-start = (bf16[2,16,128,256]{3,2,1,0:T(8,128)(2,1)S(1)}, bf16[2,16,128,256]{3,2,1,0:T(8,128)(2,1)}, u32[]{:S(2)}) copy-start(bf16[2,16,128,256]{3,2,1,0:T(8,128)(2,1)} %shard_map.46) | copy-start | bytes 6291460
  52.5 5.6 %copy-start.2 = (bf16[64,8,16,256]{3,0,2,1:T(8,128)(2,1)S(1)}, bf16[64,8,16,256]{3,0,2,1:T(8,128)(2,1)}, u32[]{:S(2)}) copy-start(bf16[64,8,16,256]{3,0,2,1:T(8,128)(2,1)} %copy-done.1) | copy-start | bytes 12582916
  62.9 30.6 %all-to-all-start.1 = ((f32[128,4,1]{1,2,0:T(1,128)}), f32[128,4,1]{1,2,0:T(1,128)S(1)}, u32[]{:S(2)}, u32[]{:S(2)}) async-start(f32[128,4,1]{1,2,0:T(1,128)} %bitcast.30), calls=%async_computation.2 | async-start | bytes 131072 | tf_op jit(solution)/shard_map/all_to_all | solution.py:133
  93.5 35.7 %all-to-all-start = ((f32[128,4,256]{2,1,0:T(4,128)}), f32[128,4,256]{2,1,0:T(4,128)S(1)}, u32[]{:S(2)}, u32[]{:S(2)}) async-start(f32[128,4,256]{2,1,0:T(4,128)} %all_to_all.12), calls=%async_computation.1 | async-start | bytes 1048576 | tf_op jit(solution)/shard_map/all_to_all | solution.py:127
Sparse Core Ops, SparseCore 0:
  62.1 28.8 reduce-scatter.1

commit v8 on v3

--- a/solution.py
+++ b/solution.py
@@ -107,7 +107,9 @@
     far = correlate(windows, source_toeplitz(partners))
     rows = jnp.concatenate([own, far], axis=0) * scale
     rows = rows.reshape(-1, 2 * LAG)
-    rows = lax.psum_scatter(rows, "win", scatter_dimension=1, tiled=True)
+    wins_total = lax.axis_size("win")
+    rows = rows.reshape(rows.shape[0], wins_total, -1)
+    rows = jnp.sum(lax.all_to_all(rows, "win", split_axis=1, concat_axis=1, tiled=True), axis=1)
     owners_total = lax.axis_size("chan")
     nbins = owners_total * BINCAP
     bins_parts = [owner[:rows_set] * BINCAP + slot[:rows_set]]

time: 140 us -> 129 us (0.921)
  between operations: 15.7 us -> 2.3 us
  starting transfers between devices: 44.8 us -> 37 us
  local copies, waits for them, and re-layouts: 8.4 us -> 14.3 us
  waiting for transfers between devices: 46.7 us -> 51.8 us
    all_to_all x0 -> x1, waiting for transfers between devices: none -> 20 us  [body(): lax.all_to_all(rows, 'win', split_axis=1, concat_axis=1, tiled=True)]
    reduce_scatter x1 -> x0, waiting for transfers between devices: 15.7 us -> none  [body(): rows = lax.psum_scatter(rows, 'win', scatter_dimension=1, tiled=True)]
    all_to_all x1, waiting for transfers between devices: 0.01 us -> 9.57 us  [body(): lax.all_to_all(own_counts, 'chan', split_axis=0, concat_axis=0, tiled=True)]
    all_to_all x1, starting transfers between devices: 15 us -> 5.73 us  [body(): lax.all_to_all(local, 'chan', split_axis=0, concat_axis=0, tiled=True)]
    ppermute x2 -> x1, waiting for transfers between devices: 10.6 us -> 1.69 us  [moved(): return lambda v: lax.ppermute(v, axis, [(i, i ^ step) for i in range(n)])]
    all_to_all x0 -> x1, starting transfers between devices: none -> 4.01 us  [body(): lax.all_to_all(rows, 'win', split_axis=1, concat_axis=1, tiled=True)]
    unnamed x16 -> x13, local copies, waits for them, and re-layouts: 3.82 us -> 6.54 us
    mul x1 -> x3, local copies, waits for them, and re-layouts: 0.9 us -> 3.1 us  [body(): rows = jnp.concatenate([own, far], axis=0) * scale]
  transfers between devices with their start and end apart: 6 -> 5, of which waited for: 4 -> 4; matrix products, arithmetic and copies ran while one was open for 6% -> 12% of each run, Pallas kernels for 2% -> 2%
where the time goes in v8:
time: 129 us; the launch traced here: 128 us
  waiting for transfers between devices  51.8 us (40%)
  starting transfers between devices  37 us (29%)
  local copies, waits for them, and re-layouts  14.3 us (11%)
  matrix products  10.1 us (8%)
  other arithmetic  6.55 us (5%)
  Pallas kernels  6.16 us (5%)
  between operations  2.3 us (2%)
    all_to_all x1, waiting for transfers between devices, body(): lax.all_to_all(local, 'chan', split_axis=0, concat_axis=0, tiled=True)  20.5 us
    all_to_all x1, waiting for transfers between devices, body(): lax.all_to_all(rows, 'win', split_axis=1, concat_axis=1, tiled=True)  20 us
    ppermute x1, starting transfers between devices, exchange(): fixed = lax.ppermute(fixed, axis, [(i, i ^ full) for i in range(n)])  15 us
    all_to_all x1, waiting for transfers between devices, body(): lax.all_to_all(own_counts, 'chan', split_axis=0, concat_axis=0, tiled=True)  9.57 us
    dot_general x2, matrix products, correlate(): jnp.einsum('cpqw,sqrw->scpr', windows, toeplitz, preferred_element_type=j...  9.51 us
    all_to_all x1, starting transfers between devices, body(): lax.all_to_all(own_counts, 'chan', split_axis=0, concat_axis=0, tiled=True)  7.96 us
    unnamed x13, local copies, waits for them, and re-layouts  6.54 us
    pallas_call x2, Pallas kernels, source_toeplitz(): pl.pallas_call(toeplitz_kernel, grid=(n,), in_specs=[pl.BlockSpec((1, quo...  6.16 us
  transfers between devices with their start and end apart: 5, of which 4 were waited for; matrix products, arithmetic and copies ran while one was open for 12% of the time, Pallas kernels for 2%

profile of v8, /device:TPU:1, one launch (start us, length us, event | category | flops | bytes accessed | tf_op | source)
XLA Modules:
  0.0 128.4 jit_solution(9828702084577708060)
XLA Ops:
  0.0 1.1 fusion.18
  1.1 1.1 fusion.31
  2.2 1.3 %fusion.43 = (s32[1]{0:T(128)}, s32[1]{0:T(128)}) fusion(s32[2]{0:T(128)} %param.29), kind=kLoop, calls=%fused_computation.78 | loop fusion | bytes 16 | tf_op jit(solution)/shard_map/slice | solution.py:74
  3.5 0.8 multiply_reduce_fusion
  4.3 0.8 fusion.41
  5.9 15.0 %collective-permute-start.22 = (bf16[3,2048]{1,0:T(4,128)(2,1)S(1)}, bf16[3,2048]{1,0:T(4,128)(2,1)S(1)}, u32[]{:S(2)}, u32[]{:S(2)}) collective-permute-start(bf16[3,2048]{1,0:T(4,128)(2,1)S(1)} %get-tuple-element.59), channel_id=1, source_target_pairs={{0,508},{4,504},{8,500},{12,496},{16,492},{20,488},{24,484},{28,48... | collective-permute-start | bytes 36872 | tf_op jit(solution)/shard_map/ppermute | solution.py:77
  20.8 0.7 bitcast_add_fusion
  21.6 0.2 reshape.91
  21.8 0.2 fusion.40
  22.0 0.1 copy_dynamic-update-slice_fusion.1
  22.0 0.1 copy_dynamic-update-slice_fusion
  22.2 0.8 fusion.27
  23.0 0.8 fusion.26
  23.9 0.8 fusion.25
  24.7 0.8 fusion.24
  25.6 0.8 fusion.23
  26.4 0.8 fusion.22
  27.2 0.8 fusion.21
  28.0 0.9 fusion.20
  28.9 0.6 copy.36
  29.5 2.3 %shard_map.46 = bf16[2,16,128,256]{3,2,1,0:T(8,128)(2,1)} custom-call(bf16[2,16,128]{2,1,0:T(8,128)(2,1)} %bitcast.107), custom_call_target="tpu_custom_call" | custom-call | tf_op jit(solution)/shard_map/pallas_call | solution.py:35
  31.8 0.2 convert_reduce_fusion
  32.0 4.1 %fusion.11 = f32[2,64,8,128]{3,1,2,0:T(8,128)S(1)} fusion(bf16[64,8,16,256]{3,0,2,1:T(8,128)(2,1)} %fusion.20, bf16[2,16,128,256]{3,2,1,0:T(8,128)(2,1)} %shard_map.46), kind=kOutput, calls=%fused_computation.8 | convolution fusion | flops 1073741824 | bytes 6815744 | tf_op jit(solution)/shard_map/cpqw,sqrw->scpr/dot_general | solution.py:55
  37.4 0.7 all_to_all.15
  38.2 6.1 %conditional.2 = (bf16[3,2048]{1,0:T(4,128)(2,1)S(1)}) conditional(s32[]{:T(128)} %bitcast.6, bf16[3,2048]{1,0:T(4,128)(2,1)S(1)} %get-tuple-element.60, bf16[3,2048]{1,0:T(4,128)(2,1)S(1)} %get-tuple-element.60, bf16[3,2048]{1,0:T(4,128)(2,1)S(1)} %get-tuple-element.60, ...), branch_computations={%region_1.2_spmd, %region_2.3_spmd, %region_3.4_spmd, %region_4.5_... | conditional | bytes 73776 | solution.py:66
  38.2 4.4 %collective-permute-start.4 = (bf16[3,2048]{1,0:T(4,128)(2,1)S(1)}, bf16[3,2048]{1,0:T(4,128)(2,1)S(1)}, u32[]{:S(2)}, u32[]{:S(2)}) collective-permute-start(bf16[3,2048]{1,0:T(4,128)(2,1)S(1)} %param.5), channel_id=1, source_target_pairs={{0,20},{4,16},{8,28},{12,24},{16,4},{20,0},{24,12},{28,8},{32,52},... | collective-permute-start | bytes 36872 | tf_op jit(solution)/shard_map/cond/branch_5_fun/ppermute | solution.py:62
  42.5 1.7 %collective-permute-done.4 = bf16[3,2048]{1,0:T(4,128)(2,1)S(1)} collective-permute-done((bf16[3,2048]{1,0:T(4,128)(2,1)S(1)}, bf16[3,2048]{1,0:T(4,128)(2,1)S(1)}, u32[]{:S(2)}, u32[]{:S(2)}) %collective-permute-start.4) | collective-permute-done | bytes 12320 | tf_op jit(solution)/shard_map/cond/branch_5_fun/ppermute | solution.py:62
  44.3 0.0 collective-permute-done.22
  44.4 0.6 pad_maximum_fusion.2.src_ref
  45.0 3.9 %shard_map.47 = bf16[4,16,128,256]{3,2,1,0:T(8,128)(2,1)} custom-call(bf16[4,16,128]{2,1,0:T(8,128)(2,1)} %pad_maximum_fusion.2.src_ref), custom_call_target="tpu_custom_call" | custom-call | tf_op jit(solution)/shard_map/pallas_call | solution.py:35
  48.9 5.4 %fusion.6 = f32[4,64,8,128]{3,1,2,0:T(8,128)S(1)} fusion(bf16[64,8,16,256]{3,0,2,1:T(8,128)(2,1)} %fusion.20, bf16[4,16,128,256]{3,2,1,0:T(8,128)(2,1)} %shard_map.47), kind=kOutput, calls=%fused_computation.7 | convolution fusion | flops 2147483648 | bytes 9437184 | tf_op jit(solution)/shard_map/cpqw,sqrw->scpr/dot_general | solution.py:55
  54.3 0.2 maximum_multiply_fusion
  54.5 0.9 copy.16
  55.4 0.7 mul.53
  56.1 1.4 %copy.17 = f32[384,4,256]{2,0,1:T(8,128)} copy(f32[384,4,256]{2,1,0:T(4,128)S(1)} %mul.53) | data formatting | bytes 3145728 | tf_op jit(solution)/shard_map/mul | solution.py:108
  57.6 4.0 %all-to-all-start = ((f32[384,4,256]{2,0,1:T(8,128)}), f32[384,4,256]{2,0,1:T(8,128)S(1)}, u32[]{:S(2)}, u32[]{:S(2)}) async-start(f32[384,4,256]{2,0,1:T(8,128)} %copy.17), calls=%async_computation | async-start | bytes 3145728 | tf_op jit(solution)/shard_map/all_to_all | solution.py:112
  61.7 20.0 %all-to-all-done = f32[384,4,256]{2,0,1:T(8,128)S(1)} async-done(((f32[384,4,256]{2,0,1:T(8,128)}), f32[384,4,256]{2,0,1:T(8,128)S(1)}, u32[]{:S(2)}, u32[]{:S(2)}) %all-to-all-start) | async-done | bytes 1572896 | tf_op jit(solution)/shard_map/all_to_all | solution.py:112
  81.7 8.0 %all-to-all-start.2 = ((f32[128,4,1]{1,2,0:T(1,128)}), f32[128,4,1]{1,2,0:T(1,128)S(1)}, u32[]{:S(2)}, u32[]{:S(2)}) async-start(f32[128,4,1]{1,2,0:T(1,128)} %bitcast.31), calls=%async_computation.2 | async-start | bytes 131072 | tf_op jit(solution)/shard_map/all_to_all | solution.py:128
  89.7 0.1 reduce_sum.46
  89.8 0.6 fusion.16
  90.4 1.1 copy.18
  91.6 9.6 %all-to-all-done.2 = f32[128,4,1]{1,2,0:T(1,128)S(1)} async-done(((f32[128,4,1]{1,2,0:T(1,128)}), f32[128,4,1]{1,2,0:T(1,128)S(1)}, u32[]{:S(2)}, u32[]{:S(2)}) %all-to-all-start.2) | async-done | bytes 2080 | tf_op jit(solution)/shard_map/all_to_all | solution.py:128
  101.1 5.7 %all-to-all-start.1 = ((f32[128,4,256]{2,1,0:T(4,128)}), f32[128,4,256]{2,1,0:T(4,128)S(1)}, u32[]{:S(2)}, u32[]{:S(2)}) async-start(f32[128,4,256]{2,1,0:T(4,128)} %copy.18), calls=%async_computation.1 | async-start | bytes 1048576 | tf_op jit(solution)/shard_map/all_to_all | solution.py:122
  106.9 0.2 reduce_sum.49
  107.0 20.5 %all-to-all-done.1 = f32[128,4,256]{2,1,0:T(4,128)S(1)} async-done(((f32[128,4,256]{2,1,0:T(4,128)}), f32[128,4,256]{2,1,0:T(4,128)S(1)}, u32[]{:S(2)}, u32[]{:S(2)}) %all-to-all-start.1) | async-done | bytes 524320 | tf_op jit(solution)/shard_map/all_to_all | solution.py:122
  127.6 0.1 reduce_sum.47
  127.7 0.7 broadcast_divide_fusion
  (23 shorter events, 0.3 us)
Async XLA Ops:
  5.9 38.4 %collective-permute-start.22 = (bf16[3,2048]{1,0:T(4,128)(2,1)S(1)}, bf16[3,2048]{1,0:T(4,128)(2,1)S(1)}, u32[]{:S(2)}, u32[]{:S(2)}) collective-permute-start(bf16[3,2048]{1,0:T(4,128)(2,1)S(1)} %get-tuple-element.59), channel_id=1, source_target_pairs={{0,508},{4,504},{8,500},{12,496},{16,492},{20,488},{24,484},{28,48... | collective-permute-start | bytes 36872 | tf_op jit(solution)/shard_map/ppermute | solution.py:77
  38.2 6.1 %collective-permute-start.4 = (bf16[3,2048]{1,0:T(4,128)(2,1)S(1)}, bf16[3,2048]{1,0:T(4,128)(2,1)S(1)}, u32[]{:S(2)}, u32[]{:S(2)}) collective-permute-start(bf16[3,2048]{1,0:T(4,128)(2,1)S(1)} %param.5), channel_id=1, source_target_pairs={{0,20},{4,16},{8,28},{12,24},{16,4},{20,0},{24,12},{28,8},{32,52},... | collective-permute-start | bytes 36872 | tf_op jit(solution)/shard_map/cond/branch_5_fun/ppermute | solution.py:62
  57.6 24.1 %all-to-all-start = ((f32[384,4,256]{2,0,1:T(8,128)}), f32[384,4,256]{2,0,1:T(8,128)S(1)}, u32[]{:S(2)}, u32[]{:S(2)}) async-start(f32[384,4,256]{2,0,1:T(8,128)} %copy.17), calls=%async_computation | async-start | bytes 3145728 | tf_op jit(solution)/shard_map/all_to_all | solution.py:112
  81.7 19.4 %all-to-all-start.2 = ((f32[128,4,1]{1,2,0:T(1,128)}), f32[128,4,1]{1,2,0:T(1,128)S(1)}, u32[]{:S(2)}, u32[]{:S(2)}) async-start(f32[128,4,1]{1,2,0:T(1,128)} %bitcast.31), calls=%async_computation.2 | async-start | bytes 131072 | tf_op jit(solution)/shard_map/all_to_all | solution.py:128
  101.1 26.4 %all-to-all-start.1 = ((f32[128,4,256]{2,1,0:T(4,128)}), f32[128,4,256]{2,1,0:T(4,128)S(1)}, u32[]{:S(2)}, u32[]{:S(2)}) async-start(f32[128,4,256]{2,1,0:T(4,128)} %copy.18), calls=%async_computation.1 | async-start | bytes 1048576 | tf_op jit(solution)/shard_map/all_to_all | solution.py:122

commit v9 on v8

--- a/solution.py
+++ b/solution.py
@@ -119,14 +119,16 @@
     bins = jnp.concatenate(bins_parts)
     picks = (bins[None, :] == jnp.arange(nbins, dtype=jnp.int32)[:, None]).astype(jnp.float32)
     local = jnp.dot(picks, rows, precision=lax.Precision.HIGHEST, preferred_element_type=jnp.float32)
-    arrived_sums = lax.all_to_all(local, "chan", split_axis=0, concat_axis=0, tiled=True)
-    sums = jnp.sum(arrived_sums.reshape(owners_total, BINCAP, -1), axis=0)
     own_bins = owner * BINCAP + slot
     own_counts = jnp.sum(
         (own_bins[None, :] == jnp.arange(nbins, dtype=jnp.int32)[:, None]).astype(jnp.float32), axis=1
     )
-    arrived_counts = lax.all_to_all(own_counts, "chan", split_axis=0, concat_axis=0, tiled=True)
-    counts = jnp.sum(arrived_counts.reshape(owners_total, BINCAP), axis=0)
+    local = local.reshape(owners_total, BINCAP, -1)
+    count_cols = jnp.broadcast_to(own_counts.reshape(owners_total, BINCAP, 1), (owners_total, BINCAP, block_width))
+    outgoing = jnp.concatenate([local, count_cols], axis=2)
+    arrived_sums = jnp.sum(lax.all_to_all(outgoing, "chan", split_axis=0, concat_axis=0, tiled=True), axis=0)
+    sums = arrived_sums[:, : local.shape[2]]
+    counts = arrived_sums[:, local.shape[2]]
     return sums / jnp.sqrt(jnp.maximum(counts, 1.0))[:, None]
 
 

time: 129 us -> 126 us (0.977)
  blocking collectives: 0 us -> 34.8 us
  waiting for transfers between devices: 51.8 us -> 28.6 us
  starting transfers between devices: 37 us -> 23.9 us
    all_to_all x0 -> x1, blocking collectives: none -> 34.8 us  [body(): lax.all_to_all(outgoing, 'chan', split_axis=0, concat_axis=0, tiled=True)]
    all_to_all x2 -> x0, waiting for transfers between devices: 30.1 us -> none  [the longest x1 20.5 us: body(): lax.all_to_all(local, 'chan', split_axis=0, concat_axis=0, tiled=True)]
    all_to_all x2 -> x0, starting transfers between devices: 13.7 us -> none  [the longest x1 7.96 us: body(): lax.all_to_all(own_counts, 'chan', split_axis=0, concat_axis=0, tiled=True)]
    ppermute x1 -> x2, waiting for transfers between devices: 1.69 us -> 9 us  [moved(): return lambda v: lax.ppermute(v, axis, [(i, i ^ step) for i in range(n)])]
    another operation x0 -> x2, other arithmetic: none -> 1.53 us
    ppermute x1 -> x2, starting transfers between devices: 4.36 us -> 4.95 us  [moved(): return lambda v: lax.ppermute(v, axis, [(i, i ^ step) for i in range(n)])]
  transfers between devices with their start and end apart: 5 -> 4, of which waited for: 4 -> 3; matrix products, arithmetic and copies ran while one was open for 12% -> 10% of each run, Pallas kernels for 2% -> 2%
where the time goes in v9:
time: 126 us
  blocking collectives  34.8 us (28%)
  waiting for transfers between devices  28.6 us (23%)
  starting transfers between devices  23.9 us (19%)
  local copies, waits for them, and re-layouts  13.3 us (11%)
  matrix products  10.1 us (8%)
  other arithmetic  6.59 us (5%)
  Pallas kernels  6.16 us (5%)
  between operations  2.09 us (2%)
    all_to_all x1, blocking collectives, body(): lax.all_to_all(outgoing, 'chan', split_axis=0, concat_axis=0, tiled=True)  34.8 us
    all_to_all x1, waiting for transfers between devices, body(): lax.all_to_all(rows, 'win', split_axis=1, concat_axis=1, tiled=True)  19.6 us
    ppermute x1, starting transfers between devices, exchange(): fixed = lax.ppermute(fixed, axis, [(i, i ^ full) for i in range(n)])  15 us
    dot_general x2, matrix products, correlate(): jnp.einsum('cpqw,sqrw->scpr', windows, toeplitz, preferred_element_type=j...  9.51 us
    ppermute x2, waiting for transfers between devices, moved(): return lambda v: lax.ppermute(v, axis, [(i, i ^ step) for i in range(n)])  9 us
    unnamed x13, local copies, waits for them, and re-layouts  6.59 us
    pallas_call x2, Pallas kernels, source_toeplitz(): pl.pallas_call(toeplitz_kernel, grid=(n,), in_specs=[pl.BlockSpec((1, quo...  6.16 us
    ppermute x2, starting transfers between devices, moved(): return lambda v: lax.ppermute(v, axis, [(i, i ^ step) for i in range(n)])  4.95 us
  transfers between devices with their start and end apart: 4, of which 3 were waited for; matrix products, arithmetic and copies ran while one was open for 10% of the time, Pallas kernels for 2%

profile of v9, /device:TPU:1, one launch (start us, length us, event | category | flops | bytes accessed | tf_op | source)
XLA Modules:
  0.0 125.7 jit_solution(9664815406227566871)
XLA Ops:
  0.0 0.8 fusion.44
  0.8 1.1 fusion.18
  1.9 1.1 fusion.31
  3.0 1.3 %fusion.46 = (s32[1]{0:T(128)}, s32[1]{0:T(128)}) fusion(s32[2]{0:T(128)} %param.29), kind=kLoop, calls=%fused_computation.82 | loop fusion | bytes 16 | tf_op jit(solution)/shard_map/slice | solution.py:74
  4.3 0.8 fusion.43
  5.8 15.0 %collective-permute-start.22 = (bf16[3,2048]{1,0:T(4,128)(2,1)S(1)}, bf16[3,2048]{1,0:T(4,128)(2,1)S(1)}, u32[]{:S(2)}, u32[]{:S(2)}) collective-permute-start(bf16[3,2048]{1,0:T(4,128)(2,1)S(1)} %get-tuple-element.59), channel_id=1, source_target_pairs={{0,508},{4,504},{8,500},{12,496},{16,492},{20,488},{24,484},{28,48... | collective-permute-start | bytes 36872 | tf_op jit(solution)/shard_map/ppermute | solution.py:77
  20.7 0.7 bitcast_add_fusion
  21.4 0.2 convert_reduce_fusion
  21.6 0.2 reshape.82
  21.8 0.2 fusion.42
  22.0 0.1 copy_dynamic-update-slice_fusion.1
  22.1 0.1 copy_dynamic-update-slice_fusion
  22.2 0.8 fusion.27
  23.1 0.8 fusion.26
  23.9 0.9 fusion.25
  24.8 0.8 fusion.24
  25.6 0.8 fusion.23
  26.5 0.8 fusion.22
  27.3 0.8 fusion.21
  28.1 0.9 fusion.20
  29.0 0.6 copy.37
  29.6 2.3 %shard_map.46 = bf16[2,16,128,256]{3,2,1,0:T(8,128)(2,1)} custom-call(bf16[2,16,128]{2,1,0:T(8,128)(2,1)} %bitcast.106), custom_call_target="tpu_custom_call" | custom-call | tf_op jit(solution)/shard_map/pallas_call | solution.py:35
  31.9 4.1 %fusion.11 = f32[2,64,8,128]{3,1,2,0:T(8,128)S(1)} fusion(bf16[64,8,16,256]{3,0,2,1:T(8,128)(2,1)} %fusion.20, bf16[2,16,128,256]{3,2,1,0:T(8,128)(2,1)} %shard_map.46), kind=kOutput, calls=%fused_computation.8 | convolution fusion | flops 1073741824 | bytes 6815744 | tf_op jit(solution)/shard_map/cpqw,sqrw->scpr/dot_general | solution.py:55
  36.0 0.1 broadcast_in_dim.10
  36.1 0.1 copy.19
  37.4 7.3 %conditional.2 = (bf16[3,2048]{1,0:T(4,128)(2,1)S(1)}) conditional(s32[]{:T(128)} %bitcast.6, bf16[3,2048]{1,0:T(4,128)(2,1)S(1)} %get-tuple-element.60, bf16[3,2048]{1,0:T(4,128)(2,1)S(1)} %get-tuple-element.60, bf16[3,2048]{1,0:T(4,128)(2,1)S(1)} %get-tuple-element.60, ...), branch_computations={%region_1.2_spmd, %region_2.3_spmd, %region_3.4_spmd, %region_4.5_... | conditional | bytes 73776 | solution.py:66
  37.5 3.0 %collective-permute-start.12 = (bf16[3,2048]{1,0:T(4,128)(2,1)S(1)}, bf16[3,2048]{1,0:T(4,128)(2,1)S(1)}, u32[]{:S(2)}, u32[]{:S(2)}) collective-permute-start(bf16[3,2048]{1,0:T(4,128)(2,1)S(1)} %param.13), channel_id=1, source_target_pairs={{0,52},{4,48},{8,60},{12,56},{16,36},{20,32},{24,44},{28,40},{32,2... | collective-permute-start | bytes 36872 | tf_op jit(solution)/shard_map/cond/branch_13_fun/ppermute | solution.py:62
  40.5 4.2 %collective-permute-done.12 = bf16[3,2048]{1,0:T(4,128)(2,1)S(1)} collective-permute-done((bf16[3,2048]{1,0:T(4,128)(2,1)S(1)}, bf16[3,2048]{1,0:T(4,128)(2,1)S(1)}, u32[]{:S(2)}, u32[]{:S(2)}) %collective-permute-start.12) | collective-permute-done | bytes 12320 | tf_op jit(solution)/shard_map/cond/branch_13_fun/ppermute | solution.py:62
  44.7 6.7 %conditional.3 = (bf16[3,2048]{1,0:T(4,128)(2,1)S(1)}) conditional(s32[]{:T(128)} %bitcast.5, bf16[3,2048]{1,0:T(4,128)(2,1)S(1)} %get-tuple-element.73, bf16[3,2048]{1,0:T(4,128)(2,1)S(1)} %get-tuple-element.73, bf16[3,2048]{1,0:T(4,128)(2,1)S(1)} %get-tuple-element.73, ...), branch_computations={%region_17.18_spmd, %region_18.19_spmd, %region_19.20_spmd, %regio... | conditional | bytes 73776 | solution.py:66
  44.8 1.9 %collective-permute-start.20 = (bf16[3,2048]{1,0:T(4,128)(2,1)S(1)}, bf16[3,2048]{1,0:T(4,128)(2,1)S(1)}, u32[]{:S(2)}, u32[]{:S(2)}) collective-permute-start(bf16[3,2048]{1,0:T(4,128)(2,1)S(1)} %param.22), channel_id=1, source_target_pairs={{0,384},{4,388},{8,392},{12,396},{16,400},{20,404},{24,408},{28,41... | collective-permute-start | bytes 36872 | tf_op jit(solution)/shard_map/cond/branch_6_fun/ppermute | solution.py:62
  46.7 4.8 %collective-permute-done.20 = bf16[3,2048]{1,0:T(4,128)(2,1)S(1)} collective-permute-done((bf16[3,2048]{1,0:T(4,128)(2,1)S(1)}, bf16[3,2048]{1,0:T(4,128)(2,1)S(1)}, u32[]{:S(2)}, u32[]{:S(2)}) %collective-permute-start.20) | collective-permute-done | bytes 12320 | tf_op jit(solution)/shard_map/cond/branch_6_fun/ppermute | solution.py:62
  51.5 0.0 collective-permute-done.22
  51.6 0.6 pad_maximum_fusion.3.src_ref
  52.2 3.9 %shard_map.47 = bf16[4,16,128,256]{3,2,1,0:T(8,128)(2,1)} custom-call(bf16[4,16,128]{2,1,0:T(8,128)(2,1)} %pad_maximum_fusion.3.src_ref), custom_call_target="tpu_custom_call" | custom-call | tf_op jit(solution)/shard_map/pallas_call | solution.py:35
  56.1 5.4 %fusion.6 = f32[4,64,8,128]{3,1,2,0:T(8,128)S(1)} fusion(bf16[64,8,16,256]{3,0,2,1:T(8,128)(2,1)} %fusion.20, bf16[4,16,128,256]{3,2,1,0:T(8,128)(2,1)} %shard_map.47), kind=kOutput, calls=%fused_computation.7 | convolution fusion | flops 2147483648 | bytes 9437184 | tf_op jit(solution)/shard_map/cpqw,sqrw->scpr/dot_general | solution.py:55
  61.5 0.2 maximum_multiply_fusion
  61.7 0.9 copy.17
  62.6 0.7 mul.53
  63.3 1.5 %copy.18 = f32[384,4,256]{2,0,1:T(8,128)} copy(f32[384,4,256]{2,1,0:T(4,128)S(1)} %mul.53) | data formatting | bytes 3145728 | tf_op jit(solution)/shard_map/mul | solution.py:108
  64.8 4.0 %all-to-all-start = ((f32[384,4,256]{2,0,1:T(8,128)}), f32[384,4,256]{2,0,1:T(8,128)S(1)}, u32[]{:S(2)}, u32[]{:S(2)}) async-start(f32[384,4,256]{2,0,1:T(8,128)} %copy.18), calls=%async_computation | async-start | bytes 3145728 | tf_op jit(solution)/shard_map/all_to_all | solution.py:112
  68.9 19.6 %all-to-all-done = f32[384,4,256]{2,0,1:T(8,128)S(1)} async-done(((f32[384,4,256]{2,0,1:T(8,128)}), f32[384,4,256]{2,0,1:T(8,128)S(1)}, u32[]{:S(2)}, u32[]{:S(2)}) %all-to-all-start) | async-done | bytes 1572896 | tf_op jit(solution)/shard_map/all_to_all | solution.py:112
  88.4 0.1 reduce_sum.37
  88.6 0.6 fusion.16
  89.2 0.1 broadcast_in_dim.22
  89.3 0.1 pad_maximum_fusion
  89.4 0.5 copy.20
  89.9 34.8 %all_to_all.10 = f32[128,4,384]{2,1,0:T(4,128)S(1)} all-to-all(f32[128,4,384]{2,1,0:T(4,128)S(1)} %copy.20), channel_id=1, replica_groups=mesh['chan'=128,'win'=4] {'chan'}, dimensions={0} | all-to-all | bytes 1572864 | tf_op jit(solution)/shard_map/all_to_all | solution.py:129
  124.8 0.2 reduce_sum.39
  124.9 0.1 fusion.39
  125.0 0.7 slice_divide_fusion
  (22 shorter events, 0.3 us)
Async XLA Ops:
  5.8 45.8 %collective-permute-start.22 = (bf16[3,2048]{1,0:T(4,128)(2,1)S(1)}, bf16[3,2048]{1,0:T(4,128)(2,1)S(1)}, u32[]{:S(2)}, u32[]{:S(2)}) collective-permute-start(bf16[3,2048]{1,0:T(4,128)(2,1)S(1)} %get-tuple-element.59), channel_id=1, source_target_pairs={{0,508},{4,504},{8,500},{12,496},{16,492},{20,488},{24,484},{28,48... | collective-permute-start | bytes 36872 | tf_op jit(solution)/shard_map/ppermute | solution.py:77
  37.5 7.3 %collective-permute-start.12 = (bf16[3,2048]{1,0:T(4,128)(2,1)S(1)}, bf16[3,2048]{1,0:T(4,128)(2,1)S(1)}, u32[]{:S(2)}, u32[]{:S(2)}) collective-permute-start(bf16[3,2048]{1,0:T(4,128)(2,1)S(1)} %param.13), channel_id=1, source_target_pairs={{0,52},{4,48},{8,60},{12,56},{16,36},{20,32},{24,44},{28,40},{32,2... | collective-permute-start | bytes 36872 | tf_op jit(solution)/shard_map/cond/branch_13_fun/ppermute | solution.py:62
  44.8 6.7 %collective-permute-start.20 = (bf16[3,2048]{1,0:T(4,128)(2,1)S(1)}, bf16[3,2048]{1,0:T(4,128)(2,1)S(1)}, u32[]{:S(2)}, u32[]{:S(2)}) collective-permute-start(bf16[3,2048]{1,0:T(4,128)(2,1)S(1)} %param.22), channel_id=1, source_target_pairs={{0,384},{4,388},{8,392},{12,396},{16,400},{20,404},{24,408},{28,41... | collective-permute-start | bytes 36872 | tf_op jit(solution)/shard_map/cond/branch_6_fun/ppermute | solution.py:62
  64.8 23.7 %all-to-all-start = ((f32[384,4,256]{2,0,1:T(8,128)}), f32[384,4,256]{2,0,1:T(8,128)S(1)}, u32[]{:S(2)}, u32[]{:S(2)}) async-start(f32[384,4,256]{2,0,1:T(8,128)} %copy.18), calls=%async_computation | async-start | bytes 3145728 | tf_op jit(solution)/shard_map/all_to_all | solution.py:112

commit v10 on v9

--- a/solution.py
+++ b/solution.py
@@ -109,7 +109,8 @@
     rows = rows.reshape(-1, 2 * LAG)
     wins_total = lax.axis_size("win")
     rows = rows.reshape(rows.shape[0], wins_total, -1)
-    rows = jnp.sum(lax.all_to_all(rows, "win", split_axis=1, concat_axis=1, tiled=True), axis=1)
+    rows = lax.all_to_all(rows.astype(jnp.bfloat16), "win", split_axis=1, concat_axis=1, tiled=True)
+    rows = jnp.sum(rows.astype(jnp.float32), axis=1)
     owners_total = lax.axis_size("chan")
     nbins = owners_total * BINCAP
     bins_parts = [owner[:rows_set] * BINCAP + slot[:rows_set]]
@@ -126,7 +127,8 @@
     local = local.reshape(owners_total, BINCAP, -1)
     count_cols = jnp.broadcast_to(own_counts.reshape(owners_total, BINCAP, 1), (owners_total, BINCAP, block_width))
     outgoing = jnp.concatenate([local, count_cols], axis=2)
-    arrived_sums = jnp.sum(lax.all_to_all(outgoing, "chan", split_axis=0, concat_axis=0, tiled=True), axis=0)
+    arrived_sums = lax.all_to_all(outgoing.astype(jnp.bfloat16), "chan", split_axis=0, concat_axis=0, tiled=True)
+    arrived_sums = jnp.sum(arrived_sums.astype(jnp.float32), axis=0)
     sums = arrived_sums[:, : local.shape[2]]
     counts = arrived_sums[:, local.shape[2]]
     return sums / jnp.sqrt(jnp.maximum(counts, 1.0))[:, None]

time: 126 us -> 100 us (0.79)
  waiting for transfers between devices: 28.6 us -> 16.1 us
  blocking collectives: 34.8 us -> 25.4 us
  local copies, waits for them, and re-layouts: 13.3 us -> 6.97 us
  starting transfers between devices: 23.9 us -> 25.8 us
    all_to_all x1, blocking collectives: 34.8 us -> 25.4 us  [body(): lax.all_to_all(outgoing.astype(jnp.bfloat16), 'chan', split_axis=0, conca...]
    all_to_all x1, waiting for transfers between devices: 19.6 us -> 10.3 us  [body(): lax.all_to_all(rows.astype(jnp.bfloat16), 'win', split_axis=1, concat_axi...]
    unnamed x13 -> x15, local copies, waits for them, and re-layouts: 6.59 us -> 2.34 us
    ppermute x2, waiting for transfers between devices: 9 us -> 5.78 us  [moved(): return lambda v: lax.ppermute(v, axis, [(i, i ^ step) for i in range(n)])]
    mul x3 -> x0, local copies, waits for them, and re-layouts: 3.1 us -> none  [body(): rows = jnp.concatenate([own, far], axis=0) * scale]
    convert_element_type x0 -> x3, local copies, waits for them, and re-layouts: none -> 2.01 us  [body(): rows.astype(jnp.bfloat16)]
    ppermute x2, starting transfers between devices: 4.95 us -> 6.83 us  [moved(): return lambda v: lax.ppermute(v, axis, [(i, i ^ step) for i in range(n)])]
  transfers between devices with their start and end apart: 4 -> 4, of which waited for: 3 -> 3; matrix products, arithmetic and copies ran while one was open for 10% -> 7% of each run, Pallas kernels for 2% -> 2%
where the time goes in v10:
time: 100 us; the launch traced here: 99.5 us
  starting transfers between devices  25.8 us (26%)
  blocking collectives  25.4 us (25%)
  waiting for transfers between devices  16.1 us (16%)
  matrix products  10.1 us (10%)
  local copies, waits for them, and re-layouts  6.97 us (7%)
  other arithmetic  6.69 us (7%)
  Pallas kernels  6.23 us (6%)
  between operations  2.15 us (2%)
    all_to_all x1, blocking collectives, body(): lax.all_to_all(outgoing.astype(jnp.bfloat16), 'chan', split_axis=0, conca...  25.4 us
    ppermute x1, starting transfers between devices, exchange(): fixed = lax.ppermute(fixed, axis, [(i, i ^ full) for i in range(n)])  15 us
    all_to_all x1, waiting for transfers between devices, body(): lax.all_to_all(rows.astype(jnp.bfloat16), 'win', split_axis=1, concat_axi...  10.3 us
    dot_general x2, matrix products, correlate(): jnp.einsum('cpqw,sqrw->scpr', windows, toeplitz, preferred_element_type=j...  9.51 us
    ppermute x2, starting transfers between devices, moved(): return lambda v: lax.ppermute(v, axis, [(i, i ^ step) for i in range(n)])  6.83 us
    pallas_call x2, Pallas kernels, source_toeplitz(): pl.pallas_call(toeplitz_kernel, grid=(n,), in_specs=[pl.BlockSpec((1, quo...  6.23 us
    ppermute x2, waiting for transfers between devices, moved(): return lambda v: lax.ppermute(v, axis, [(i, i ^ step) for i in range(n)])  5.78 us
    all_to_all x1, starting transfers between devices, body(): lax.all_to_all(rows.astype(jnp.bfloat16), 'win', split_axis=1, concat_axi...  4.01 us
  transfers between devices with their start and end apart: 4, of which 3 were waited for; matrix products, arithmetic and copies ran while one was open for 7% of the time, Pallas kernels for 2%

profile of v10, /device:TPU:1, one launch (start us, length us, event | category | flops | bytes accessed | tf_op | source)
XLA Modules:
  0.0 99.5 jit_solution(6321343769071197598)
XLA Ops:
  0.0 0.8 fusion.44
  0.8 1.1 %fusion.18 = f32[64]{0:T(128)S(1)} fusion(bf16[1,64,2048]{2,1,0:T(8,128)(2,1)} %param.28), kind=kLoop, calls=%fused_computation.18 | loop fusion | flops 393152 | bytes 262400 | tf_op jit(solution)/shard_map/reduce_sum | solution.py:19
  1.9 1.1 %fusion.31 = bf16[64,2048]{1,0:T(8,128)(2,1)S(1)} fusion(bf16[1,64,2048]{2,1,0:T(8,128)(2,1)} %param.28, f32[64]{0:T(128)S(1)} %add_rsqrt_fusion), kind=kLoop, calls=%fused_computation.42 | loop fusion | flops 393216 | bytes 524544 | tf_op jit(solution)/shard_map/squeeze | solution.py:90
  3.0 1.3 %fusion.46 = (s32[1]{0:T(128)}, s32[1]{0:T(128)}) fusion(s32[2]{0:T(128)} %param.29), kind=kLoop, calls=%fused_computation.85 | loop fusion | bytes 16 | tf_op jit(solution)/shard_map/slice | solution.py:74
  4.3 0.8 fusion.43
  5.8 15.0 %collective-permute-start.22 = (bf16[3,2048]{1,0:T(4,128)(2,1)S(1)}, bf16[3,2048]{1,0:T(4,128)(2,1)S(1)}, u32[]{:S(2)}, u32[]{:S(2)}) collective-permute-start(bf16[3,2048]{1,0:T(4,128)(2,1)S(1)} %get-tuple-element.59), channel_id=1, source_target_pairs={{0,508},{4,504},{8,500},{12,496},{16,492},{20,488},{24,484},{28,48... | collective-permute-start | bytes 36872 | tf_op jit(solution)/shard_map/ppermute | solution.py:77
  20.7 0.7 bitcast_add_fusion
  21.4 0.2 convert_reduce_fusion.2
  21.6 0.2 reshape.83
  21.8 0.2 fusion.42
  22.0 0.1 copy_dynamic-update-slice_fusion.1
  22.1 0.1 copy_dynamic-update-slice_fusion
  22.6 0.0 copy-start
  22.6 0.6 copy.37
  23.3 1.3 %copy-done = bf16[64,8,16,256]{3,0,2,1:T(8,128)(2,1)} copy-done((bf16[64,8,16,256]{3,0,2,1:T(8,128)(2,1)}, bf16[64,8,16,256]{3,0,2,1:T(8,128)(2,1)S(1)}, u32[]{:S(2)}) %copy-start) | copy-done | bytes 4194328
  24.6 2.3 %shard_map.46 = bf16[2,16,128,256]{3,2,1,0:T(8,128)(2,1)} custom-call(bf16[2,16,128]{2,1,0:T(8,128)(2,1)} %bitcast.106), custom_call_target="tpu_custom_call" | custom-call | tf_op jit(solution)/shard_map/pallas_call | solution.py:35
  26.9 4.1 %fusion.12 = f32[2,64,8,128]{3,1,2,0:T(8,128)S(1)} fusion(bf16[64,8,16,256]{3,0,2,1:T(8,128)(2,1)} %copy-done, bf16[2,16,128,256]{3,2,1,0:T(8,128)(2,1)} %shard_map.46), kind=kOutput, calls=%fused_computation.10 | convolution fusion | flops 1073741824 | bytes 6815744 | tf_op jit(solution)/shard_map/cpqw,sqrw->scpr/dot_general | solution.py:55
  31.0 0.1 reshape.90
  31.1 0.1 copy.19
  32.5 6.3 %conditional.2 = (bf16[3,2048]{1,0:T(4,128)(2,1)S(1)}) conditional(s32[]{:T(128)} %bitcast.6, bf16[3,2048]{1,0:T(4,128)(2,1)S(1)} %get-tuple-element.60, bf16[3,2048]{1,0:T(4,128)(2,1)S(1)} %get-tuple-element.60, bf16[3,2048]{1,0:T(4,128)(2,1)S(1)} %get-tuple-element.60, ...), branch_computations={%region_1.2_spmd, %region_2.3_spmd, %region_3.4_spmd, %region_4.5_... | conditional | bytes 73776 | solution.py:66
  32.5 4.7 %collective-permute-start.3 = (bf16[3,2048]{1,0:T(4,128)(2,1)S(1)}, bf16[3,2048]{1,0:T(4,128)(2,1)S(1)}, u32[]{:S(2)}, u32[]{:S(2)}) collective-permute-start(bf16[3,2048]{1,0:T(4,128)(2,1)S(1)} %param.4), channel_id=1, source_target_pairs={{0,16},{4,20},{8,24},{12,28},{16,0},{20,4},{24,8},{28,12},{32,48},... | collective-permute-start | bytes 36872 | tf_op jit(solution)/shard_map/cond/branch_4_fun/ppermute | solution.py:62
  37.2 1.6 %collective-permute-done.3 = bf16[3,2048]{1,0:T(4,128)(2,1)S(1)} collective-permute-done((bf16[3,2048]{1,0:T(4,128)(2,1)S(1)}, bf16[3,2048]{1,0:T(4,128)(2,1)S(1)}, u32[]{:S(2)}, u32[]{:S(2)}) %collective-permute-start.3) | collective-permute-done | bytes 12320 | tf_op jit(solution)/shard_map/cond/branch_4_fun/ppermute | solution.py:62
  38.8 6.4 %conditional.3 = (bf16[3,2048]{1,0:T(4,128)(2,1)S(1)}) conditional(s32[]{:T(128)} %bitcast.5, bf16[3,2048]{1,0:T(4,128)(2,1)S(1)} %get-tuple-element.73, bf16[3,2048]{1,0:T(4,128)(2,1)S(1)} %get-tuple-element.73, bf16[3,2048]{1,0:T(4,128)(2,1)S(1)} %get-tuple-element.73, ...), branch_computations={%region_17.18_spmd, %region_18.19_spmd, %region_19.20_spmd, %regio... | conditional | bytes 73776 | solution.py:66
  38.8 2.2 %collective-permute-start.17 = (bf16[3,2048]{1,0:T(4,128)(2,1)S(1)}, bf16[3,2048]{1,0:T(4,128)(2,1)S(1)}, u32[]{:S(2)}, u32[]{:S(2)}) collective-permute-start(bf16[3,2048]{1,0:T(4,128)(2,1)S(1)} %param.19), channel_id=1, source_target_pairs={{0,192},{4,196},{8,200},{12,204},{16,208},{20,212},{24,216},{28,22... | collective-permute-start | bytes 36872 | tf_op jit(solution)/shard_map/cond/branch_3_fun/ppermute | solution.py:62
  41.0 4.2 %collective-permute-done.17 = bf16[3,2048]{1,0:T(4,128)(2,1)S(1)} collective-permute-done((bf16[3,2048]{1,0:T(4,128)(2,1)S(1)}, bf16[3,2048]{1,0:T(4,128)(2,1)S(1)}, u32[]{:S(2)}, u32[]{:S(2)}) %collective-permute-start.17) | collective-permute-done | bytes 12320 | tf_op jit(solution)/shard_map/cond/branch_3_fun/ppermute | solution.py:62
  45.2 0.0 collective-permute-done.22
  45.3 0.6 pad_maximum_fusion.3.src_ref
  45.9 3.9 %shard_map.47 = bf16[4,16,128,256]{3,2,1,0:T(8,128)(2,1)} custom-call(bf16[4,16,128]{2,1,0:T(8,128)(2,1)} %pad_maximum_fusion.3.src_ref), custom_call_target="tpu_custom_call" | custom-call | tf_op jit(solution)/shard_map/pallas_call | solution.py:35
  49.9 5.4 %fusion.7 = f32[4,64,8,128]{3,1,2,0:T(8,128)S(1)} fusion(bf16[64,8,16,256]{3,0,2,1:T(8,128)(2,1)} %copy-done, bf16[4,16,128,256]{3,2,1,0:T(8,128)(2,1)} %shard_map.47), kind=kOutput, calls=%fused_computation.9 | convolution fusion | flops 2147483648 | bytes 9437184 | tf_op jit(solution)/shard_map/cpqw,sqrw->scpr/dot_general | solution.py:55
  55.3 0.2 fusion.6
  55.5 0.5 copy.17
  56.0 0.5 convert_element_type.43
  56.5 1.0 copy.18
  57.5 4.0 %all-to-all-start = ((bf16[384,4,256]{2,0,1:T(8,128)(2,1)}), bf16[384,4,256]{2,0,1:T(8,128)(2,1)S(1)}, u32[]{:S(2)}, u32[]{:S(2)}) async-start(bf16[384,4,256]{2,0,1:T(8,128)(2,1)} %copy.18), calls=%async_computation | async-start | bytes 1572864 | tf_op jit(solution)/shard_map/all_to_all | solution.py:112
  61.6 10.3 %all-to-all-done = bf16[384,4,256]{2,0,1:T(8,128)(2,1)S(1)} async-done(((bf16[384,4,256]{2,0,1:T(8,128)(2,1)}), bf16[384,4,256]{2,0,1:T(8,128)(2,1)S(1)}, u32[]{:S(2)}, u32[]{:S(2)}) %all-to-all-start) | async-done | bytes 786464 | tf_op jit(solution)/shard_map/all_to_all | solution.py:112
  71.9 0.1 convert_reduce_fusion
  72.0 0.6 convolution_convert_fusion
  72.6 0.1 broadcast_in_dim.22
  72.8 0.3 copy.20
  73.1 25.4 %all_to_all.10 = bf16[128,4,384]{2,1,0:T(4,128)(2,1)S(1)} all-to-all(bf16[128,4,384]{2,1,0:T(4,128)(2,1)S(1)} %copy.20), channel_id=1, replica_groups=mesh['chan'=128,'win'=4] {'chan'}, dimensions={0} | all-to-all | bytes 786432 | tf_op jit(solution)/shard_map/all_to_all | solution.py:130
  98.5 0.2 convert_reduce_fusion.1
  98.7 0.1 fusion.39
  98.8 0.7 slice_divide_fusion
  (31 shorter events, 0.7 us)
Async XLA Ops:
  5.8 39.5 %collective-permute-start.22 = (bf16[3,2048]{1,0:T(4,128)(2,1)S(1)}, bf16[3,2048]{1,0:T(4,128)(2,1)S(1)}, u32[]{:S(2)}, u32[]{:S(2)}) collective-permute-start(bf16[3,2048]{1,0:T(4,128)(2,1)S(1)} %get-tuple-element.59), channel_id=1, source_target_pairs={{0,508},{4,504},{8,500},{12,496},{16,492},{20,488},{24,484},{28,48... | collective-permute-start | bytes 36872 | tf_op jit(solution)/shard_map/ppermute | solution.py:77
  22.6 2.0 %copy-start = (bf16[64,8,16,256]{3,0,2,1:T(8,128)(2,1)}, bf16[64,8,16,256]{3,0,2,1:T(8,128)(2,1)S(1)}, u32[]{:S(2)}) copy-start(bf16[64,8,16,256]{3,0,2,1:T(8,128)(2,1)S(1)} %fusion.20) | copy-start | bytes 12582916
  32.5 6.2 %collective-permute-start.3 = (bf16[3,2048]{1,0:T(4,128)(2,1)S(1)}, bf16[3,2048]{1,0:T(4,128)(2,1)S(1)}, u32[]{:S(2)}, u32[]{:S(2)}) collective-permute-start(bf16[3,2048]{1,0:T(4,128)(2,1)S(1)} %param.4), channel_id=1, source_target_pairs={{0,16},{4,20},{8,24},{12,28},{16,0},{20,4},{24,8},{28,12},{32,48},... | collective-permute-start | bytes 36872 | tf_op jit(solution)/shard_map/cond/branch_4_fun/ppermute | solution.py:62
  38.8 6.4 %collective-permute-start.17 = (bf16[3,2048]{1,0:T(4,128)(2,1)S(1)}, bf16[3,2048]{1,0:T(4,128)(2,1)S(1)}, u32[]{:S(2)}, u32[]{:S(2)}) collective-permute-start(bf16[3,2048]{1,0:T(4,128)(2,1)S(1)} %param.19), channel_id=1, source_target_pairs={{0,192},{4,196},{8,200},{12,204},{16,208},{20,212},{24,216},{28,22... | collective-permute-start | bytes 36872 | tf_op jit(solution)/shard_map/cond/branch_3_fun/ppermute | solution.py:62
  57.5 14.4 %all-to-all-start = ((bf16[384,4,256]{2,0,1:T(8,128)(2,1)}), bf16[384,4,256]{2,0,1:T(8,128)(2,1)S(1)}, u32[]{:S(2)}, u32[]{:S(2)}) async-start(bf16[384,4,256]{2,0,1:T(8,128)(2,1)} %copy.18), calls=%async_computation | async-start | bytes 1572864 | tf_op jit(solution)/shard_map/all_to_all | solution.py:112

commit v11 on v10

--- a/solution.py
+++ b/solution.py
@@ -102,15 +102,17 @@
     arrived = exchange(payload, round_masks, "chan")
     windows = receiver_windows(normed)
     scale = 1.0 / jnp.sqrt(jnp.float32(samples))
-    own = correlate(windows, source_toeplitz(sources))
+    wins_total = lax.axis_size("win")
+
+    def window_sum(part):
+        part = (part * scale).reshape(-1, wins_total, 2 * LAG // wins_total)
+        part = lax.all_to_all(part.astype(jnp.bfloat16), "win", split_axis=1, concat_axis=1, tiled=True)
+        return jnp.sum(part.astype(jnp.float32), axis=1)
+
+    own = window_sum(correlate(windows, source_toeplitz(sources)))
     partners = jnp.concatenate([arrived[r, :SRC] for r in range(ROUNDS)], axis=0)
-    far = correlate(windows, source_toeplitz(partners))
-    rows = jnp.concatenate([own, far], axis=0) * scale
-    rows = rows.reshape(-1, 2 * LAG)
-    wins_total = lax.axis_size("win")
-    rows = rows.reshape(rows.shape[0], wins_total, -1)
-    rows = lax.all_to_all(rows.astype(jnp.bfloat16), "win", split_axis=1, concat_axis=1, tiled=True)
-    rows = jnp.sum(rows.astype(jnp.float32), axis=1)
+    far = window_sum(correlate(windows, source_toeplitz(partners)))
+    rows = jnp.concatenate([own, far], axis=0)
     owners_total = lax.axis_size("chan")
     nbins = owners_total * BINCAP
     bins_parts = [owner[:rows_set] * BINCAP + slot[:rows_set]]

time: 100 us -> 106 us (1.060); the launches traced: 99.5 us -> 107 us
  blocking collectives: 25.4 us -> 28.9 us
  waiting for transfers between devices: 16.1 us -> 18.3 us
  starting transfers between devices: 25.8 us -> 27.1 us
    ppermute x2, waiting for transfers between devices: 5.78 us -> 10.8 us  [moved(): return lambda v: lax.ppermute(v, axis, [(i, i ^ step) for i in range(n)])]
    all_to_all x1 -> x2, starting transfers between devices: 4.01 us -> 8.36 us  [window_sum(): lax.all_to_all(part.astype(jnp.bfloat16), 'win', split_axis=1, concat_axi...]
    all_to_all x1, blocking collectives: 25.4 us -> 28.9 us  [body(): lax.all_to_all(outgoing.astype(jnp.bfloat16), 'chan', split_axis=0, conca...]
    ppermute x2, starting transfers between devices: 6.83 us -> 3.84 us  [moved(): return lambda v: lax.ppermute(v, axis, [(i, i ^ step) for i in range(n)])]
    all_to_all x1 -> x2, waiting for transfers between devices: 10.3 us -> 7.51 us  [window_sum(): lax.all_to_all(part.astype(jnp.bfloat16), 'win', split_axis=1, concat_axi...]
    convert_element_type x3 -> x6, local copies, waits for them, and re-layouts: 2.01 us -> 2.64 us  [window_sum(): part.astype(jnp.bfloat16)]
  transfers between devices with their start and end apart: 4 -> 5, of which waited for: 3 -> 3; matrix products, arithmetic and copies ran while one was open for 7% -> 15% of each run, Pallas kernels for 2% -> 6%
where the time goes in v11:
time: 106 us; the launch traced here: 107 us
  blocking collectives  28.9 us (27%)
  starting transfers between devices  27.1 us (26%)
  waiting for transfers between devices  18.3 us (17%)
  matrix products  10.5 us (10%)
  local copies, waits for them, and re-layouts  7.37 us (7%)
  other arithmetic  6.62 us (6%)
  Pallas kernels  6.22 us (6%)
  between operations  2.24 us (2%)
    all_to_all x1, blocking collectives, body(): lax.all_to_all(outgoing.astype(jnp.bfloat16), 'chan', split_axis=0, conca...  28.9 us
    ppermute x1, starting transfers between devices, exchange(): fixed = lax.ppermute(fixed, axis, [(i, i ^ full) for i in range(n)])  15 us
    ppermute x2, waiting for transfers between devices, moved(): return lambda v: lax.ppermute(v, axis, [(i, i ^ step) for i in range(n)])  10.8 us
    dot_general x2, matrix products, correlate(): jnp.einsum('cpqw,sqrw->scpr', windows, toeplitz, preferred_element_type=j...  9.92 us
    all_to_all x2, starting transfers between devices, window_sum(): lax.all_to_all(part.astype(jnp.bfloat16), 'win', split_axis=1, concat_axi...  8.36 us
    all_to_all x2, waiting for transfers between devices, window_sum(): lax.all_to_all(part.astype(jnp.bfloat16), 'win', split_axis=1, concat_axi...  7.51 us
    pallas_call x2, Pallas kernels, source_toeplitz(): pl.pallas_call(toeplitz_kernel, grid=(n,), in_specs=[pl.BlockSpec((1, quo...  6.22 us
    ppermute x2, starting transfers between devices, moved(): return lambda v: lax.ppermute(v, axis, [(i, i ^ step) for i in range(n)])  3.84 us
  transfers between devices with their start and end apart: 5, of which 3 were waited for; matrix products, arithmetic and copies ran while one was open for 15% of the time, Pallas kernels for 6%

profile of v11, /device:TPU:1, one launch (start us, length us, event | category | flops | bytes accessed | tf_op | source)
XLA Modules:
  0.0 107.4 jit_solution(13600563899481011543)
XLA Ops:
  0.0 0.8 fusion.74
  0.8 1.1 %fusion.46 = f32[64]{0:T(128)S(1)} fusion(bf16[1,64,2048]{2,1,0:T(8,128)(2,1)} %param.28), kind=kLoop, calls=%fused_computation.22 | loop fusion | flops 393152 | bytes 262400 | tf_op jit(solution)/shard_map/reduce_sum | solution.py:19
  1.9 1.1 fusion.60
  3.0 1.3 %fusion.76 = (s32[1]{0:T(128)}, s32[1]{0:T(128)}) fusion(s32[2]{0:T(128)} %param.29), kind=kLoop, calls=%fused_computation.91 | loop fusion | bytes 16 | tf_op jit(solution)/shard_map/slice | solution.py:74
  4.3 0.8 fusion.73
  5.8 15.0 %collective-permute-start.22 = (bf16[3,2048]{1,0:T(4,128)(2,1)S(1)}, bf16[3,2048]{1,0:T(4,128)(2,1)S(1)}, u32[]{:S(2)}, u32[]{:S(2)}) collective-permute-start(bf16[3,2048]{1,0:T(4,128)(2,1)S(1)} %get-tuple-element.59), channel_id=1, source_target_pairs={{0,508},{4,504},{8,500},{12,496},{16,492},{20,488},{24,484},{28,48... | collective-permute-start | bytes 36872 | tf_op jit(solution)/shard_map/ppermute | solution.py:77
  20.8 0.2 reshape.71
  21.0 0.2 fusion.72
  21.2 0.1 copy_dynamic-update-slice_fusion.1
  21.3 0.1 copy_dynamic-update-slice_fusion
  21.8 0.0 copy-start
  21.9 0.6 copy.37
  22.5 1.3 %copy-done = bf16[64,8,16,256]{3,0,2,1:T(8,128)(2,1)} copy-done((bf16[64,8,16,256]{3,0,2,1:T(8,128)(2,1)}, bf16[64,8,16,256]{3,0,2,1:T(8,128)(2,1)S(1)}, u32[]{:S(2)}) %copy-start) | copy-done | bytes 4194328
  23.8 2.3 %shard_map.46 = bf16[2,16,128,256]{3,2,1,0:T(8,128)(2,1)} custom-call(bf16[2,16,128]{2,1,0:T(8,128)(2,1)} %bitcast.141), custom_call_target="tpu_custom_call" | custom-call | tf_op jit(solution)/shard_map/pallas_call | solution.py:35
  26.1 4.1 %fusion.41 = bf16[2,64,8,128]{3,1,2,0:T(8,128)(2,1)S(1)} fusion(bf16[64,8,16,256]{3,0,2,1:T(8,128)(2,1)} %copy-done, bf16[2,16,128,256]{3,2,1,0:T(8,128)(2,1)} %shard_map.46), kind=kOutput, calls=%fused_computation.14 | convolution fusion | flops 1074003968 | bytes 6553600 | tf_op jit(solution)/shard_map/cpqw,sqrw->scpr/dot_general | solution.py:55
  30.2 0.2 copy.17
  30.4 0.2 convert_element_type.59
  30.6 0.7 copy.18
  31.3 4.0 %all-to-all-start = ((bf16[128,4,256]{2,0,1:T(8,128)(2,1)}), bf16[128,4,256]{2,0,1:T(8,128)(2,1)S(1)}, u32[]{:S(2)}, u32[]{:S(2)}) async-start(bf16[128,4,256]{2,0,1:T(8,128)(2,1)} %copy.18), calls=%async_computation | async-start | bytes 524288 | tf_op jit(solution)/shard_map/all_to_all | solution.py:109
  35.3 0.7 bitcast_add_fusion
  36.0 0.2 convert_reduce_fusion.2
  36.2 0.1 reshape.79
  37.6 6.3 %conditional.2 = (bf16[3,2048]{1,0:T(4,128)(2,1)S(1)}) conditional(s32[]{:T(128)} %bitcast.6, bf16[3,2048]{1,0:T(4,128)(2,1)S(1)} %get-tuple-element.60, bf16[3,2048]{1,0:T(4,128)(2,1)S(1)} %get-tuple-element.60, bf16[3,2048]{1,0:T(4,128)(2,1)S(1)} %get-tuple-element.60, ...), branch_computations={%region_1.2_spmd, %region_2.3_spmd, %region_3.4_spmd, %region_4.5_... | conditional | bytes 73776 | solution.py:66
  37.7 1.9 %collective-permute-start.14 = (bf16[3,2048]{1,0:T(4,128)(2,1)S(1)}, bf16[3,2048]{1,0:T(4,128)(2,1)S(1)}, u32[]{:S(2)}, u32[]{:S(2)}) collective-permute-start(bf16[3,2048]{1,0:T(4,128)(2,1)S(1)} %param.15), channel_id=1, source_target_pairs={{0,60},{4,56},{8,52},{12,48},{16,44},{20,40},{24,36},{28,32},{32,2... | collective-permute-start | bytes 36872 | tf_op jit(solution)/shard_map/cond/branch_15_fun/ppermute | solution.py:62
  39.6 4.3 %collective-permute-done.14 = bf16[3,2048]{1,0:T(4,128)(2,1)S(1)} collective-permute-done((bf16[3,2048]{1,0:T(4,128)(2,1)S(1)}, bf16[3,2048]{1,0:T(4,128)(2,1)S(1)}, u32[]{:S(2)}, u32[]{:S(2)}) %collective-permute-start.14) | collective-permute-done | bytes 12320 | tf_op jit(solution)/shard_map/cond/branch_15_fun/ppermute | solution.py:62
  43.9 8.4 %conditional.3 = (bf16[3,2048]{1,0:T(4,128)(2,1)S(1)}) conditional(s32[]{:T(128)} %bitcast.5, bf16[3,2048]{1,0:T(4,128)(2,1)S(1)} %get-tuple-element.73, bf16[3,2048]{1,0:T(4,128)(2,1)S(1)} %get-tuple-element.73, bf16[3,2048]{1,0:T(4,128)(2,1)S(1)} %get-tuple-element.73, ...), branch_computations={%region_17.18_spmd, %region_18.19_spmd, %region_19.20_spmd, %regio... | conditional | bytes 73776 | solution.py:66
  44.0 1.9 %collective-permute-start.18 = (bf16[3,2048]{1,0:T(4,128)(2,1)S(1)}, bf16[3,2048]{1,0:T(4,128)(2,1)S(1)}, u32[]{:S(2)}, u32[]{:S(2)}) collective-permute-start(bf16[3,2048]{1,0:T(4,128)(2,1)S(1)} %param.20), channel_id=1, source_target_pairs={{0,256},{4,260},{8,264},{12,268},{16,272},{20,276},{24,280},{28,28... | collective-permute-start | bytes 36872 | tf_op jit(solution)/shard_map/cond/branch_4_fun/ppermute | solution.py:62
  45.9 6.5 %collective-permute-done.18 = bf16[3,2048]{1,0:T(4,128)(2,1)S(1)} collective-permute-done((bf16[3,2048]{1,0:T(4,128)(2,1)S(1)}, bf16[3,2048]{1,0:T(4,128)(2,1)S(1)}, u32[]{:S(2)}, u32[]{:S(2)}) %collective-permute-start.18) | collective-permute-done | bytes 12320 | tf_op jit(solution)/shard_map/cond/branch_4_fun/ppermute | solution.py:62
  52.4 0.0 collective-permute-done.22
  52.5 0.6 pad_maximum_fusion.3.src_ref
  53.1 3.9 %shard_map.47 = bf16[4,16,128,256]{3,2,1,0:T(8,128)(2,1)} custom-call(bf16[4,16,128]{2,1,0:T(8,128)(2,1)} %pad_maximum_fusion.3.src_ref), custom_call_target="tpu_custom_call" | custom-call | tf_op jit(solution)/shard_map/pallas_call | solution.py:35
  57.0 5.8 %fusion.21 = bf16[4,64,8,128]{3,1,2,0:T(8,128)(2,1)S(1)} fusion(bf16[64,8,16,256]{3,0,2,1:T(8,128)(2,1)} %copy-done, bf16[4,16,128,256]{3,2,1,0:T(8,128)(2,1)} %shard_map.47), kind=kOutput, calls=%fused_computation.9 | convolution fusion | flops 2148007936 | bytes 8912896 | tf_op jit(solution)/shard_map/cpqw,sqrw->scpr/dot_general | solution.py:55
  62.9 0.3 copy.19
  63.2 0.3 convert_element_type.63
  63.6 0.9 copy.20
  64.5 0.0 all-to-all-done
  64.5 4.3 %all-to-all-start.1 = ((bf16[256,4,256]{2,0,1:T(8,128)(2,1)}), bf16[256,4,256]{2,0,1:T(8,128)(2,1)S(1)}, u32[]{:S(2)}, u32[]{:S(2)}) async-start(bf16[256,4,256]{2,0,1:T(8,128)(2,1)} %copy.20), calls=%async_computation.1 | async-start | bytes 1048576 | tf_op jit(solution)/shard_map/all_to_all | solution.py:109
  68.9 7.5 %all-to-all-done.1 = bf16[256,4,256]{2,0,1:T(8,128)(2,1)S(1)} async-done(((bf16[256,4,256]{2,0,1:T(8,128)(2,1)}), bf16[256,4,256]{2,0,1:T(8,128)(2,1)S(1)}, u32[]{:S(2)}, u32[]{:S(2)}) %all-to-all-start.1) | async-done | bytes 524320 | tf_op jit(solution)/shard_map/all_to_all | solution.py:109
  76.4 0.1 convert_reduce_fusion
  76.4 0.6 convolution_convert_fusion
  77.1 0.1 reshape.72
  77.1 0.2 broadcast_in_dim.22
  77.3 0.2 pad_maximum_fusion
  77.5 28.9 %all_to_all.15 = bf16[128,4,384]{2,1,0:T(4,128)(2,1)S(1)} all-to-all(bf16[128,4,384]{2,1,0:T(4,128)(2,1)S(1)} %pad_maximum_fusion), channel_id=1, replica_groups=mesh['chan'=128,'win'=4] {'chan'}, dimensions={0} | all-to-all | bytes 786432 | tf_op jit(solution)/shard_map/all_to_all | solution.py:132
  106.4 0.2 convert_reduce_fusion.1
  106.6 0.1 fusion.68
  106.7 0.7 slice_divide_fusion
  (30 shorter events, 0.6 us)
Async XLA Ops:
  5.8 46.6 %collective-permute-start.22 = (bf16[3,2048]{1,0:T(4,128)(2,1)S(1)}, bf16[3,2048]{1,0:T(4,128)(2,1)S(1)}, u32[]{:S(2)}, u32[]{:S(2)}) collective-permute-start(bf16[3,2048]{1,0:T(4,128)(2,1)S(1)} %get-tuple-element.59), channel_id=1, source_target_pairs={{0,508},{4,504},{8,500},{12,496},{16,492},{20,488},{24,484},{28,48... | collective-permute-start | bytes 36872 | tf_op jit(solution)/shard_map/ppermute | solution.py:77
  21.8 2.0 %copy-start = (bf16[64,8,16,256]{3,0,2,1:T(8,128)(2,1)}, bf16[64,8,16,256]{3,0,2,1:T(8,128)(2,1)S(1)}, u32[]{:S(2)}) copy-start(bf16[64,8,16,256]{3,0,2,1:T(8,128)(2,1)S(1)} %fusion.48) | copy-start | bytes 12582916
  31.3 33.1 %all-to-all-start = ((bf16[128,4,256]{2,0,1:T(8,128)(2,1)}), bf16[128,4,256]{2,0,1:T(8,128)(2,1)S(1)}, u32[]{:S(2)}, u32[]{:S(2)}) async-start(bf16[128,4,256]{2,0,1:T(8,128)(2,1)} %copy.18), calls=%async_computation | async-start | bytes 524288 | tf_op jit(solution)/shard_map/all_to_all | solution.py:109
  37.7 6.3 %collective-permute-start.14 = (bf16[3,2048]{1,0:T(4,128)(2,1)S(1)}, bf16[3,2048]{1,0:T(4,128)(2,1)S(1)}, u32[]{:S(2)}, u32[]{:S(2)}) collective-permute-start(bf16[3,2048]{1,0:T(4,128)(2,1)S(1)} %param.15), channel_id=1, source_target_pairs={{0,60},{4,56},{8,52},{12,48},{16,44},{20,40},{24,36},{28,32},{32,2... | collective-permute-start | bytes 36872 | tf_op jit(solution)/shard_map/cond/branch_15_fun/ppermute | solution.py:62
  44.0 8.4 %collective-permute-start.18 = (bf16[3,2048]{1,0:T(4,128)(2,1)S(1)}, bf16[3,2048]{1,0:T(4,128)(2,1)S(1)}, u32[]{:S(2)}, u32[]{:S(2)}) collective-permute-start(bf16[3,2048]{1,0:T(4,128)(2,1)S(1)} %param.20), channel_id=1, source_target_pairs={{0,256},{4,260},{8,264},{12,268},{16,272},{20,276},{24,280},{28,28... | collective-permute-start | bytes 36872 | tf_op jit(solution)/shard_map/cond/branch_4_fun/ppermute | solution.py:62
  64.5 11.9 %all-to-all-start.1 = ((bf16[256,4,256]{2,0,1:T(8,128)(2,1)}), bf16[256,4,256]{2,0,1:T(8,128)(2,1)S(1)}, u32[]{:S(2)}, u32[]{:S(2)}) async-start(bf16[256,4,256]{2,0,1:T(8,128)(2,1)} %copy.20), calls=%async_computation.1 | async-start | bytes 1048576 | tf_op jit(solution)/shard_map/all_to_all | solution.py:109
